TPU v7x, 256 devices: a whole 4x4x8 slice. The times are simulated.
256 devices in a mesh: row: 32 (over y, z_hi, x), col: 8 (over z_lo, core).
Axes of the slice: x: 4, y: 4, z: 8 (z_hi: 2, z_lo: 4; z = z_hi * 4 + z_lo), core: 2. Of those that a mesh axis runs over, the one named last changes fastest.
Arguments:
- trailing: float32 [2, 32768, 4096], P(None, 'row', 'col'), may hold values from -6 to 6
- panel: float32 [2, 32768, 256], P(None, ('row', 'col')), may hold values from -4 to 4
- diag_inverse: float32 [2, 256, 256], replicated, as said below
Outputs:
- scaled: float32 [2, 32768, 256], P(None, ('row', 'col'))
- updated: float32 [2, 32768, 4096], P(None, 'row', 'col')
Inputs may be any that keep to these rules, and one draw needn't show every extreme that they name: diag_inverse is complex-symmetric: each part equals its own transpose.
All inputs are finite; a program needn't handle non-finite values.
Results may differ from a plain program's by a relative error of at most 0.00007.
Values sent between devices are 32-bit elements; how exact they have to be, the bound alone decides.
No kernel may reach another device: no remote copies, remote signals or barrier semaphores. Data moves between devices by JAX's collectives and lax.ppermute only.
A program may use at most 64 MiB of HBM per device.

v0:
```python
import jax
import jax.numpy as jnp
from jax import lax
from jax.sharding import PartitionSpec as P


def from_root(value, axis, source):
    kept = jnp.where(lax.axis_index(axis) == source, value, 0).astype(value.dtype)
    return lax.psum(kept, axis)


def complex_product(left, right):
    hp = lax.Precision.HIGHEST
    real_part = jnp.dot(left[0], right[0], precision=hp) - jnp.dot(left[1], right[1], precision=hp)
    imag_part = jnp.dot(left[0], right[1], precision=hp) + jnp.dot(left[1], right[0], precision=hp)
    return jnp.stack([real_part, imag_part])


def product_transposed(left, right):
    hp = lax.Precision.HIGHEST
    dims = (((1,), (1,)), ((), ()))
    real_part = lax.dot_general(left[0], right[0], dims, precision=hp) - lax.dot_general(
        left[1], right[1], dims, precision=hp
    )
    imag_part = lax.dot_general(left[0], right[1], dims, precision=hp) + lax.dot_general(
        left[1], right[0], dims, precision=hp
    )
    return jnp.stack([real_part, imag_part])


def local(trailing, panel, diag_inverse):
    scaled = complex_product(panel, diag_inverse)
    block_height = trailing.shape[1]
    width = trailing.shape[2]
    column = lax.axis_index("col")
    owner = column * width // block_height
    offset = column * width % block_height
    block = lax.all_gather(panel, "col", axis=1, tiled=True)
    own_window = lax.dynamic_slice_in_dim(block, offset, width, 1)
    window = from_root(own_window, "row", owner)
    tiles = complex_product(window, diag_inverse)
    updated = trailing - product_transposed(block, tiles)
    return (scaled, updated)


def solution(mesh):
    return jax.shard_map(
        local,
        mesh=mesh,
        in_specs=(P(None, "row", "col"), P(None, ("row", "col"), None), P()),
        out_specs=(P(None, ("row", "col"), None), P(None, "row", "col")),
        check_vma=False,
    )
```

profile of v0, /device:TPU:2, one launch (start us, length us, event | category | flops | bytes accessed | tf_op | source)
XLA Modules:
  0.0 511.7 jit_solution(11597531821732049873)
XLA Ops:
  7.2 0.0 all-gather.2.cloned.1.call-start
  7.2 0.7 all-gather.2.cloned.1.call-update
  7.9 0.0 all-reduce.2.cloned.1.call-start
  8.0 43.6 %all-gather.2.cloned.1.call-done = f32[2,1024,256]{2,1,0:T(8,128)} async-done(((f32[2,128,256]{2,1,0:T(8,128)}), f32[2,1024,256]{2,1,0:T(8,128)}) %all-gather.2.cloned.1.call-update) | async-done | bytes 2097168 | tf_op jit(solution)/shard_map/all_gather | solution.py:38
  51.5 2.3 dynamic-slice_select_fusion
  53.8 0.0 all-reduce.2.cloned.1.call-update
  53.8 0.0 copy-start.2
  53.9 0.0 copy-start.4
  53.9 5.4 %copy.5 = f32[2,1024,512]{1,2,0:T(8,128)} copy(f32[2,1024,512]{2,1,0:T(8,128)} %param.3) | data formatting | bytes 8388608 | tf_op args[0]
  59.3 0.0 copy-done.2
  59.3 0.0 copy-done.4
  59.3 0.3 fusion.8
  59.6 0.3 fusion
  59.9 0.3 fusion.14
  60.2 0.3 fusion.1
  60.5 0.7 pad_maximum_fusion
  61.2 0.0 copy-start.1
  61.2 422.0 %all-reduce.2.cloned.1.call-done = f32[2,512,256]{2,1,0:T(8,128)} async-done(((f32[2,512,256]{2,1,0:T(8,128)}), f32[2,512,256]{2,1,0:T(8,128)}) %all-reduce.2.cloned.1.call-update) | async-done | bytes 1048592 | tf_op jit(solution)/shard_map/psum | solution.py:9
  483.1 1.6 fusion.4
  484.8 1.6 fusion.5
  486.4 1.6 convolution_add_fusion
  488.0 0.0 copy-done.1
  488.0 0.0 copy-start.3
  488.0 1.9 fusion.2
  489.9 0.0 copy-done.3
  489.9 0.6 convolution_subtract_fusion
  490.5 1.9 fusion.3
  492.4 2.0 add_bitcast_fusion
  494.4 0.0 copy-start
  494.4 2.0 subtract_bitcast_fusion
  496.4 0.2 copy-done
  496.6 2.9 maximum_subtract_fusion
  499.5 5.4 %copy.6 = f32[2,1024,512]{2,1,0:T(8,128)} copy(f32[2,1024,512]{1,2,0:T(8,128)} %maximum_subtract_fusion) | data formatting | bytes 8388608
Async XLA Ops:
  7.2 44.4 %all-gather.2.cloned.1.call-start = ((), (), s32[]{:S(2)}) async-start(), calls=%async_computation | async-start | bytes 2359296 | tf_op jit(solution)/shard_map/all_gather | solution.py:38
  7.9 475.2 %all-reduce.2.cloned.1.call-start = ((), (), s32[]{:S(2)}) async-start(), calls=%async_computation.1 | async-start | bytes 2097152 | tf_op jit(solution)/shard_map/psum | solution.py:9
  53.8 5.5 %copy-start.2 = (f32[2,256,256]{2,1,0:T(8,128)S(1)}, f32[2,256,256]{2,1,0:T(8,128)}, u32[]{:S(2)}) copy-start(f32[2,256,256]{2,1,0:T(8,128)} %param.5) | copy-start | bytes 1572868
  53.9 5.4 %copy-start.4 = (f32[2,128,256]{2,1,0:T(8,128)S(1)}, f32[2,128,256]{2,1,0:T(8,128)}, u32[]{:S(2)}) copy-start(f32[2,128,256]{2,1,0:T(8,128)} %param.4) | copy-start | bytes 786436
  61.2 426.8 %copy-start.1 = (f32[2,1024,256]{2,1,0:T(8,128)S(1)}, f32[2,1024,256]{2,1,0:T(8,128)}, u32[]{:S(2)}) copy-start(f32[2,1024,256]{2,1,0:T(8,128)} %all-gather.2.cloned.1.call-done) | copy-start | bytes 6291460
  488.0 1.9 copy-start.3
  494.4 2.2 copy-start
Sparse Core Ops, SparseCore 0:
  9.8 41.7 all-gather.1
  54.2 428.9 all-reduce.1
where the time goes:
time: 512 us
  waiting for transfers between devices  466 us (91%)
  matrix products  14.3 us (3%)
  between operations  14.2 us (3%)
  local copies, waits for them, and re-layouts  11 us (2%)
  other arithmetic  5.86 us (1%)
    psum x1, waiting for transfers between devices, from_root(): return lax.psum(kept, axis)  422 us
    all_gather x1, waiting for transfers between devices, local(): block = lax.all_gather(panel, 'col', axis=1, tiled=True)  43.6 us
    unnamed x12, local copies, waits for them, and re-layouts  11 us
  transfers between devices with their start and end apart: 2, of which 2 were waited for; matrix products, arithmetic and copies ran while one was open for 1% of the time, Pallas kernels for 0%

commit v1 on v0

v1 whole, which is shorter than its diff:
```python
import jax
import jax.numpy as jnp
from jax import lax
from jax.sharding import Mesh
from jax.sharding import PartitionSpec as P

AXES = ("y", "zh", "x", "zl", "core")
ROW = ("y", "zh", "x")
COL = ("zl", "core")


def complex_product(left, right):
    hp = lax.Precision.HIGHEST
    real_part = jnp.dot(left[0], right[0], precision=hp) - jnp.dot(left[1], right[1], precision=hp)
    imag_part = jnp.dot(left[0], right[1], precision=hp) + jnp.dot(left[1], right[0], precision=hp)
    return jnp.stack([real_part, imag_part])


def product_transposed(left, right):
    hp = lax.Precision.HIGHEST
    dims = (((1,), (1,)), ((), ()))
    real_part = lax.dot_general(left[0], right[0], dims, precision=hp) - lax.dot_general(
        left[1], right[1], dims, precision=hp
    )
    imag_part = lax.dot_general(left[0], right[1], dims, precision=hp) + lax.dot_general(
        left[1], right[0], dims, precision=hp
    )
    return jnp.stack([real_part, imag_part])


def make_local(sizes):
    ny, nh, nx, nl, nc = sizes

    def lin(y, h, x, l, c):
        return (((y * nh + h) * nx + x) * nl + l) * nc + c

    pieces = nl * nc
    transpose = []
    for g in range(nx):
        for l in range(nl):
            for c in range(nc):
                p = nc * l + c
                transpose.append((lin(0, 0, g, l, c), lin(0, 0, p % nx, g, p // nx)))

    def shift(y0, y1, h0, h1):
        return [
            (lin(y0, h0, x, l, c), lin(y1, h1, x, l, c))
            for x in range(nx)
            for l in range(nl)
            for c in range(nc)
        ]

    def local(trailing, panel, diag_inverse):
        scaled = complex_product(panel, diag_inverse)
        block = lax.all_gather(panel, COL, axis=1, tiled=True)

        yi = lax.axis_index("y")
        hi = lax.axis_index("zh")
        piece = lax.ppermute(panel, AXES, transpose)
        r1 = lax.ppermute(piece, AXES, shift(0, 1, 0, 0))
        r3 = lax.ppermute(piece, AXES, shift(0, ny - 1, 0, 0))
        r2 = lax.ppermute(r1, AXES, shift(1, 2, 0, 0))
        along_y = jnp.where(yi == 1, r1, jnp.where(yi == 2, r2, jnp.where(yi == ny - 1, r3, piece)))
        rz = lax.ppermute(along_y, AXES, [pr for y in range(ny) for pr in shift(y, y, 0, 1)])
        held = jnp.where(hi == 0, along_y, rz)
        window = lax.all_gather(held, "x", axis=1, tiled=True)

        tiles = complex_product(window, diag_inverse)
        updated = trailing - product_transposed(block, tiles)
        return (scaled, updated)

    return local


def solution(mesh):
    ny, nh, nx = 4, 2, 4
    nl, nc = 4, 2
    devices = mesh.devices.reshape(ny, nh, nx, nl, nc)
    fine = Mesh(devices, AXES)
    return jax.shard_map(
        make_local((ny, nh, nx, nl, nc)),
        mesh=fine,
        in_specs=(P(None, ROW, COL), P(None, ROW + COL, None), P()),
        out_specs=(P(None, ROW + COL, None), P(None, ROW, COL)),
        check_vma=False,
    )
```

time: 512 us -> 151 us (0.29)
  the two profiles are of different devices: /device:TPU:2 before, /device:TPU:7 now
where the time goes in v1:
time: 151 us; the launch traced here: 149 us
  waiting for transfers between devices  92.2 us (61%)
  matrix products  14.7 us (10%)
  between operations  14.2 us (9%)
  starting transfers between devices  12.3 us (8%)
  local copies, waits for them, and re-layouts  11 us (7%)
  other arithmetic  4.41 us (3%)
    all_gather x1, waiting for transfers between devices, local(): window = lax.all_gather(held, 'x', axis=1, tiled=True)  41.9 us
    all_gather x1, waiting for transfers between devices, local(): block = lax.all_gather(panel, COL, axis=1, tiled=True)  37.6 us
    unnamed x12, local copies, waits for them, and re-layouts  11 us
    ppermute x1, starting transfers between devices, local(): piece = lax.ppermute(panel, AXES, transpose)  7.66 us
    ppermute x1, waiting for transfers between devices, local(): piece = lax.ppermute(panel, AXES, transpose)  6.12 us
    ppermute x1, waiting for transfers between devices, local(): lax.ppermute(along_y, AXES, [pr for y in range(ny) for pr in shift(y, y,...  3.28 us
    dot_general x1, matrix products, product_transposed(): lax.dot_general(left[0], right[0], dims, precision=hp)  3.24 us
  transfers between devices with their start and end apart: 7, of which 6 were waited for; matrix products, arithmetic and copies ran while one was open for 8% of the time, Pallas kernels for 0%

profile of v1, /device:TPU:7, one launch (start us, length us, event | category | flops | bytes accessed | tf_op | source)
XLA Modules:
  0.0 148.9 jit_solution(12657731391345822271)
XLA Ops:
  7.2 0.0 all-gather.3.cloned.1.call-start
  7.2 7.7 %collective-permute-start = (f32[2,128,256]{2,1,0:T(8,128)}, f32[2,128,256]{2,1,0:T(8,128)S(1)}, u32[]{:S(2)}, u32[]{:S(2)}) collective-permute-start(f32[2,128,256]{2,1,0:T(8,128)} %param.4), channel_id=1, source_target_pairs={{0,0},{1,8},{2,16},{3,24},{4,1},{5,9},{6,17},{7,25},{8,2},{9,10},{... | collective-permute-start | bytes 786440 | tf_op jit(solution)/shard_map/ppermute | solution.py:59
  14.9 6.1 %collective-permute-done = f32[2,128,256]{2,1,0:T(8,128)S(1)} collective-permute-done((f32[2,128,256]{2,1,0:T(8,128)}, f32[2,128,256]{2,1,0:T(8,128)S(1)}, u32[]{:S(2)}, u32[]{:S(2)}) %collective-permute-start) | collective-permute-done | bytes 262176 | tf_op jit(solution)/shard_map/ppermute | solution.py:59
  21.0 1.3 collective-permute-start.1
  22.3 1.3 collective-permute-start.3
  23.6 2.0 %collective-permute-done.1 = f32[2,128,256]{2,1,0:T(8,128)S(1)} collective-permute-done((f32[2,128,256]{2,1,0:T(8,128)S(1)}, f32[2,128,256]{2,1,0:T(8,128)S(1)}, u32[]{:S(2)}, u32[]{:S(2)}) %collective-permute-start.1) | collective-permute-done | bytes 262176 | tf_op jit(solution)/shard_map/ppermute | solution.py:60
  25.6 0.7 collective-permute-start.2
  26.3 0.6 collective-permute-done.3
  26.9 0.0 collective-permute-done.2
  26.9 0.1 select_select_fusion
  27.0 1.3 collective-permute-start.4
  28.3 3.3 %collective-permute-done.4 = f32[2,128,256]{2,1,0:T(8,128)S(1)} collective-permute-done((f32[2,128,256]{2,1,0:T(8,128)S(1)}, f32[2,128,256]{2,1,0:T(8,128)S(1)}, u32[]{:S(2)}, u32[]{:S(2)}) %collective-permute-start.4) | collective-permute-done | bytes 262176 | tf_op jit(solution)/shard_map/ppermute | solution.py:64
  31.6 0.7 broadcast_select_fusion
  32.3 0.0 all-gather.3.cloned.1.call-update
  32.3 0.0 all-gather.5.cloned.1.call-start
  32.4 0.7 all-gather.5.cloned.1.call-update
  33.1 0.0 copy-start.1
  33.1 0.0 copy-start.4
  33.1 5.4 %copy.5 = f32[2,1024,512]{1,2,0:T(8,128)} copy(f32[2,1024,512]{2,1,0:T(8,128)} %param.3) | data formatting | bytes 8388608 | tf_op args[0]
  38.5 0.0 copy-done.1
  38.5 0.0 copy-done.4
  38.5 0.3 fusion.8
  38.8 0.3 fusion
  39.1 0.3 fusion.14
  39.4 0.3 fusion.1
  39.7 0.7 pad_maximum_fusion
  40.4 41.9 %all-gather.3.cloned.1.call-done = f32[2,512,256]{2,1,0:T(8,128)} async-done(((f32[2,128,256]{2,1,0:T(8,128)}), f32[2,512,256]{2,1,0:T(8,128)}) %all-gather.3.cloned.1.call-update) | async-done | bytes 1048592 | tf_op jit(solution)/shard_map/all_gather | solution.py:66
  82.3 0.0 copy-start.3
  82.3 1.7 %fusion.5 = f32[512,256]{1,0:T(8,128)S(1)} fusion(f32[2,512,256]{2,1,0:T(8,128)} %all-gather.3.cloned.1.call-done, f32[2,256,256]{2,1,0:T(8,128)S(1)} %copy-done.1), kind=kOutput, calls=%fused_computation.16 | convolution fusion | flops 402653184 | bytes 1310720 | tf_op jit(solution)/shard_map/dot_general | solution.py:14
  84.0 1.6 %fusion.4 = f32[512,256]{1,0:T(8,128)S(1)} fusion(f32[2,512,256]{2,1,0:T(8,128)} %all-gather.3.cloned.1.call-done, f32[2,256,256]{2,1,0:T(8,128)S(1)} %copy-done.1), kind=kOutput, calls=%fused_computation.15 | convolution fusion | flops 402653184 | bytes 1310720 | tf_op jit(solution)/shard_map/dot_general | solution.py:15
  85.7 0.0 copy-done.3
  85.7 0.6 convolution_subtract_fusion
  86.3 0.6 convolution_add_fusion
  86.8 37.6 %all-gather.5.cloned.1.call-done = f32[2,1024,256]{2,1,0:T(8,128)} async-done(((f32[2,128,256]{2,1,0:T(8,128)}), f32[2,1024,256]{2,1,0:T(8,128)}) %all-gather.5.cloned.1.call-update) | async-done | bytes 2097168 | tf_op jit(solution)/shard_map/all_gather | solution.py:55
  124.4 0.0 copy-start.2
  124.4 3.2 %fusion.3 = f32[512,1024]{1,0:T(8,128)S(1)} fusion(f32[512,256]{1,0:T(8,128)S(1)} %convolution_subtract_fusion, f32[2,1024,256]{2,1,0:T(8,128)} %all-gather.5.cloned.1.call-done), kind=kOutput, calls=%fused_computation.12 | convolution fusion | flops 1610612736 | bytes 3670016 | tf_op jit(solution)/shard_map/dot_general | solution.py:22
  127.7 0.0 copy-done.2
  127.7 1.9 %fusion.2 = f32[512,1024]{1,0:T(8,128)S(1)} fusion(f32[512,256]{1,0:T(8,128)S(1)} %convolution_add_fusion, f32[2,1024,256]{2,1,0:T(8,128)S(1)} %copy-done.2), kind=kOutput, calls=%fused_computation.11 | convolution fusion | flops 1610612736 | bytes 3670016 | tf_op jit(solution)/shard_map/dot_general | solution.py:25
  129.6 2.0 %subtract_bitcast_fusion = f32[1,1024,512]{1,2,0:T(8,128)S(1)} fusion(f32[512,1024]{1,0:T(8,128)S(1)} %fusion.3, f32[512,256]{1,0:T(8,128)S(1)} %convolution_add_fusion, f32[2,1024,256]{2,1,0:T(8,128)S(1)} %copy-done.2), kind=kOutput, calls=%fused_computation.2 | convolution fusion | flops 1611137024 | bytes 5767168 | tf_op jit(solution)/shard_map/dot_general | solution.py:22
  131.6 0.0 copy-start
  131.6 2.0 %add_bitcast_fusion = f32[1,1024,512]{1,2,0:T(8,128)S(1)} fusion(f32[512,1024]{1,0:T(8,128)S(1)} %fusion.2, f32[512,256]{1,0:T(8,128)S(1)} %convolution_subtract_fusion, f32[2,1024,256]{2,1,0:T(8,128)S(1)} %copy-done.2), kind=kOutput, calls=%fused_computation.1 | convolution fusion | flops 1611137024 | bytes 5767168 | tf_op jit(solution)/shard_map/dot_general | solution.py:25
  133.6 0.2 copy-done
  133.8 2.9 %maximum_subtract_fusion = f32[2,1024,512]{1,2,0:T(8,128)} fusion(f32[2,1024,512]{1,2,0:T(8,128)S(1)} %copy-done, f32[1,1024,512]{1,2,0:T(8,128)S(1)} %add_bitcast_fusion, f32[1,1024,512]{1,2,0:T(8,128)S(1)} %subtract_bitcast_fusion), kind=kLoop, calls=%fused_computation | loop fusion | flops 2097152 | bytes 12582912 | tf_op jit(solution)/shard_map/sub | solution.py:69
  136.7 5.4 %copy.6 = f32[2,1024,512]{2,1,0:T(8,128)} copy(f32[2,1024,512]{1,2,0:T(8,128)} %maximum_subtract_fusion) | data formatting | bytes 8388608
Async XLA Ops:
  7.2 75.1 %all-gather.3.cloned.1.call-start = ((), (), s32[]{:S(2)}) async-start(), calls=%async_computation | async-start | bytes 1310720 | tf_op jit(solution)/shard_map/all_gather | solution.py:66
  7.2 13.8 %collective-permute-start = (f32[2,128,256]{2,1,0:T(8,128)}, f32[2,128,256]{2,1,0:T(8,128)S(1)}, u32[]{:S(2)}, u32[]{:S(2)}) collective-permute-start(f32[2,128,256]{2,1,0:T(8,128)} %param.4), channel_id=1, source_target_pairs={{0,0},{1,8},{2,16},{3,24},{4,1},{5,9},{6,17},{7,25},{8,2},{9,10},{... | collective-permute-start | bytes 786440 | tf_op jit(solution)/shard_map/ppermute | solution.py:59
  21.0 4.6 %collective-permute-start.1 = (f32[2,128,256]{2,1,0:T(8,128)S(1)}, f32[2,128,256]{2,1,0:T(8,128)S(1)}, u32[]{:S(2)}, u32[]{:S(2)}) collective-permute-start(f32[2,128,256]{2,1,0:T(8,128)S(1)} %collective-permute-done), channel_id=1, source_target_pairs={{0,64},{1,65},{2,66},{3,67},{4,68},{5,69},{6,70},{7,71},{8,72},{9,... | collective-permute-start | bytes 786440 | tf_op jit(solution)/shard_map/ppermute | solution.py:60
  22.3 4.6 %collective-permute-start.3 = (f32[2,128,256]{2,1,0:T(8,128)S(1)}, f32[2,128,256]{2,1,0:T(8,128)S(1)}, u32[]{:S(2)}, u32[]{:S(2)}) collective-permute-start(f32[2,128,256]{2,1,0:T(8,128)S(1)} %collective-permute-done), channel_id=1, source_target_pairs={{0,192},{1,193},{2,194},{3,195},{4,196},{5,197},{6,198},{7,199},{8... | collective-permute-start | bytes 786440 | tf_op jit(solution)/shard_map/ppermute | solution.py:61
  25.6 1.3 collective-permute-start.2
  27.0 4.6 %collective-permute-start.4 = (f32[2,128,256]{2,1,0:T(8,128)S(1)}, f32[2,128,256]{2,1,0:T(8,128)S(1)}, u32[]{:S(2)}, u32[]{:S(2)}) collective-permute-start(f32[2,128,256]{2,1,0:T(8,128)S(1)} %select_select_fusion), channel_id=1, source_target_pairs={{0,32},{1,33},{2,34},{3,35},{4,36},{5,37},{6,38},{7,39},{8,40},{9,... | collective-permute-start | bytes 786440 | tf_op jit(solution)/shard_map/ppermute | solution.py:64
  32.3 92.1 %all-gather.5.cloned.1.call-start = ((), (), s32[]{:S(2)}) async-start(), calls=%async_computation.1 | async-start | bytes 2359296 | tf_op jit(solution)/shard_map/all_gather | solution.py:55
  33.1 5.5 %copy-start.1 = (f32[2,256,256]{2,1,0:T(8,128)S(1)}, f32[2,256,256]{2,1,0:T(8,128)}, u32[]{:S(2)}) copy-start(f32[2,256,256]{2,1,0:T(8,128)} %param.5) | copy-start | bytes 1572868
  33.1 5.4 %copy-start.4 = (f32[2,128,256]{2,1,0:T(8,128)S(1)}, f32[2,128,256]{2,1,0:T(8,128)}, u32[]{:S(2)}) copy-start(f32[2,128,256]{2,1,0:T(8,128)} %param.4) | copy-start | bytes 786436
  82.3 3.3 %copy-start.3 = (f32[2,512,256]{2,1,0:T(8,128)S(1)}, f32[2,512,256]{2,1,0:T(8,128)}, u32[]{:S(2)}) copy-start(f32[2,512,256]{2,1,0:T(8,128)} %all-gather.3.cloned.1.call-done) | copy-start | bytes 3145732
  124.4 3.2 %copy-start.2 = (f32[2,1024,256]{2,1,0:T(8,128)S(1)}, f32[2,1024,256]{2,1,0:T(8,128)}, u32[]{:S(2)}) copy-start(f32[2,1024,256]{2,1,0:T(8,128)} %all-gather.5.cloned.1.call-done) | copy-start | bytes 6291460
  131.6 2.2 %copy-start = (f32[2,1024,512]{1,2,0:T(8,128)S(1)}, f32[2,1024,512]{1,2,0:T(8,128)}, u32[]{:S(2)}) copy-start(f32[2,1024,512]{1,2,0:T(8,128)} %copy.5) | copy-start | bytes 12582916
Sparse Core Ops, SparseCore 0:
  32.4 49.8 all-gather.2
  84.1 40.2 all-gather.4

commit v2 on v1

--- a/solution.py
+++ b/solution.py
@@ -34,36 +34,68 @@
     def lin(y, h, x, l, c):
         return (((y * nh + h) * nx + x) * nl + l) * nc + c
 
-    pieces = nl * nc
-    transpose = []
-    for g in range(nx):
-        for l in range(nl):
-            for c in range(nc):
-                p = nc * l + c
-                transpose.append((lin(0, 0, g, l, c), lin(0, 0, p % nx, g, p // nx)))
+    def plane(h, y):
+        return y * nh + h
 
-    def shift(y0, y1, h0, h1):
-        return [
-            (lin(y0, h0, x, l, c), lin(y1, h1, x, l, c))
-            for x in range(nx)
-            for l in range(nl)
-            for c in range(nc)
-        ]
+    def spread(y1, h1):
+        pairs = []
+        for g in range(nx):
+            for l in range(nl):
+                for c in range(nc):
+                    p = nc * l + c
+                    pairs.append((lin(0, 0, g, l, c), lin(y1, h1, p % nx, g, p // nx)))
+        return pairs
+
+    first = [(0, 0), (1, 0), (ny - 1, 0), (0, 1)]
+    relay_one = [((1, 0), (2, 0)), ((0, 1), (1, 1)), ((ny - 1, 0), (2, 1))]
+    relay_two = [((0, 1), (ny - 1, 1))]
+
+    def shifts(n, k):
+        return [(i, (i + k) % n) for i in range(n)]
+
+    def reorder(pieces, idx, n):
+        out = []
+        for j in range(n):
+            val = pieces[0]
+            for k in range(1, n):
+                val = jnp.where((idx - j) % n == k, pieces[k], val)
+            out.append(val)
+        return jnp.concatenate(out, axis=1)
+
+    def gather(piece, axis, idx, n):
+        got = [piece] + [lax.ppermute(piece, axis, shifts(n, k)) for k in range(1, n)]
+        return reorder(got, idx, n)
 
     def local(trailing, panel, diag_inverse):
         scaled = complex_product(panel, diag_inverse)
-        block = lax.all_gather(panel, COL, axis=1, tiled=True)
 
         yi = lax.axis_index("y")
         hi = lax.axis_index("zh")
-        piece = lax.ppermute(panel, AXES, transpose)
-        r1 = lax.ppermute(piece, AXES, shift(0, 1, 0, 0))
-        r3 = lax.ppermute(piece, AXES, shift(0, ny - 1, 0, 0))
-        r2 = lax.ppermute(r1, AXES, shift(1, 2, 0, 0))
-        along_y = jnp.where(yi == 1, r1, jnp.where(yi == 2, r2, jnp.where(yi == ny - 1, r3, piece)))
-        rz = lax.ppermute(along_y, AXES, [pr for y in range(ny) for pr in shift(y, y, 0, 1)])
-        held = jnp.where(hi == 0, along_y, rz)
-        window = lax.all_gather(held, "x", axis=1, tiled=True)
+        xi = lax.axis_index("x")
+        li = lax.axis_index("zl")
+        ci = lax.axis_index("core")
+
+        got_a = [lax.ppermute(panel, AXES, spread(y1, h1)) for y1, h1 in first]
+        held_a = got_a[0]
+        for (y1, h1), got in zip(first[1:], got_a[1:]):
+            held_a = jnp.where((yi == y1) & (hi == h1), got, held_a)
+        b1 = lax.ppermute(held_a, ("y", "zh"), [(plane(h0, y0), plane(h1, y1)) for (y0, h0), (y1, h1) in relay_one])
+        b2 = lax.ppermute(held_a, ("y", "zh"), [(plane(h0, y0), plane(h1, y1)) for (y0, h0), (y1, h1) in relay_two])
+        held = held_a
+        for (_, _), (y1, h1) in relay_one:
+            held = jnp.where((yi == y1) & (hi == h1), b1, held)
+        for (_, _), (y1, h1) in relay_two:
+            held = jnp.where((yi == y1) & (hi == h1), b2, held)
+        window = gather(held, "x", xi, nx)
+
+        mine = gather(panel, "zl", li, nl)
+        other = lax.ppermute(mine, "core", shifts(nc, 1))
+        lo = jnp.where(ci == 0, mine, other)
+        hi_ = jnp.where(ci == 0, other, mine)
+        two, rows, width = mine.shape[0], panel.shape[1], mine.shape[2]
+        block = jnp.stack(
+            [lo.reshape(two, nl, rows, width), hi_.reshape(two, nl, rows, width)], axis=2
+        ).reshape(two, nl * nc * rows, width)
 
         tiles = complex_product(window, diag_inverse)
         updated = trailing - product_transposed(block, tiles)

time: 151 us -> 107 us (0.71)
  the two profiles are of different devices: /device:TPU:7 before, /device:TPU:1 now
where the time goes in v2:
time: 107 us; the launch traced here: 106 us
  starting transfers between devices  47.4 us (44%)
  waiting for transfers between devices  40.1 us (37%)
  matrix products  13.2 us (12%)
  other arithmetic  4.56 us (4%)
    ppermute x6, starting transfers between devices, gather(): lax.ppermute(piece, axis, shifts(n, k))  27.7 us
    ppermute x6, waiting for transfers between devices, gather(): lax.ppermute(piece, axis, shifts(n, k))  24.8 us
    ppermute x4, starting transfers between devices, local(): got_a = [lax.ppermute(panel, AXES, spread(y1, h1)) for y1, h1 in first]  15.9 us
    ppermute x4, waiting for transfers between devices, local(): got_a = [lax.ppermute(panel, AXES, spread(y1, h1)) for y1, h1 in first]  15.3 us
    sub x1, other arithmetic, local(): updated = trailing - product_transposed(block, tiles)  3.03 us
    ppermute x1, starting transfers between devices, local(): other = lax.ppermute(mine, 'core', shifts(nc, 1))  2.48 us
  transfers between devices with their start and end apart: 13, of which 3 were waited for; matrix products, arithmetic and copies ran while one was open for 6% of the time, Pallas kernels for 0%

profile of v2, /device:TPU:1, one launch (start us, length us, event | category | flops | bytes accessed | tf_op | source)
XLA Modules:
  0.0 106.3 jit_solution(10524006170255404480)
XLA Ops:
  0.6 0.0 copy-start.2
  0.6 0.0 copy-start
  0.7 11.3 %collective-permute-start.4 = (f32[2,128,256]{2,1,0:T(8,128)}, f32[2,128,256]{2,1,0:T(8,128)S(1)}, u32[]{:S(2)}, u32[]{:S(2)}) collective-permute-start(f32[2,128,256]{2,1,0:T(8,128)} %param.4), channel_id=1, source_target_pairs={{0,32},{1,40},{2,48},{3,56},{4,33},{5,41},{6,49},{7,57},{8,34},{9,... | collective-permute-start | bytes 786440 | tf_op jit(solution)/shard_map/ppermute | solution.py:78
  11.9 1.3 %collective-permute-start.5 = (f32[2,128,256]{2,1,0:T(8,128)}, f32[2,128,256]{2,1,0:T(8,128)S(1)}, u32[]{:S(2)}, u32[]{:S(2)}) collective-permute-start(f32[2,128,256]{2,1,0:T(8,128)} %param.4), channel_id=1, source_target_pairs={{0,192},{1,200},{2,208},{3,216},{4,193},{5,201},{6,209},{7,217},{8... | collective-permute-start | bytes 786440 | tf_op jit(solution)/shard_map/ppermute | solution.py:78
  13.2 1.3 %collective-permute-start.6 = (f32[2,128,256]{2,1,0:T(8,128)}, f32[2,128,256]{2,1,0:T(8,128)S(1)}, u32[]{:S(2)}, u32[]{:S(2)}) collective-permute-start(f32[2,128,256]{2,1,0:T(8,128)} %param.4), channel_id=1, source_target_pairs={{0,64},{1,72},{2,80},{3,88},{4,65},{5,73},{6,81},{7,89},{8,66},{9,... | collective-permute-start | bytes 786440 | tf_op jit(solution)/shard_map/ppermute | solution.py:78
  14.6 2.0 %collective-permute-start.7 = (f32[2,128,256]{2,1,0:T(8,128)}, f32[2,128,256]{2,1,0:T(8,128)S(1)}, u32[]{:S(2)}, u32[]{:S(2)}) collective-permute-start(f32[2,128,256]{2,1,0:T(8,128)} %param.4), channel_id=1, source_target_pairs={{0,0},{1,8},{2,16},{3,24},{4,1},{5,9},{6,17},{7,25},{8,2},{9,10},{... | collective-permute-start | bytes 786440 | tf_op jit(solution)/shard_map/ppermute | solution.py:78
  16.6 4.6 %collective-permute-start = (f32[2,128,256]{2,1,0:T(8,128)}, f32[2,128,256]{2,1,0:T(8,128)S(1)}, u32[]{:S(2)}, u32[]{:S(2)}) collective-permute-start(f32[2,128,256]{2,1,0:T(8,128)} %param.4), channel_id=1, source_target_pairs={{0,6},{2,0},{4,2},{6,4},{1,7},{3,1},{5,3},{7,5},{8,14},{10,8},{12,... | collective-permute-start | bytes 786440 | tf_op jit(solution)/shard_map/ppermute | solution.py:66
  21.2 1.3 %fusion.8 = f32[128,256]{1,0:T(8,128)S(1)} fusion(f32[2,256,256]{2,1,0:T(8,128)} %param.5, f32[2,128,256]{2,1,0:T(8,128)} %param.4), kind=kOutput, calls=%fused_computation.26 | convolution fusion | flops 100663296 | bytes 524288 | tf_op jit(solution)/shard_map/dot_general | solution.py:15
  22.5 1.3 %fusion.14 = f32[128,256]{1,0:T(8,128)S(1)} fusion(f32[2,256,256]{2,1,0:T(8,128)} %param.5, f32[2,128,256]{2,1,0:T(8,128)} %param.4), kind=kOutput, calls=%fused_computation.32 | convolution fusion | flops 100663296 | bytes 524288 | tf_op jit(solution)/shard_map/dot_general | solution.py:14
  23.8 0.0 collective-permute-done.4
  23.8 16.4 %collective-permute-start.1 = (f32[2,128,256]{2,1,0:T(8,128)}, f32[2,128,256]{2,1,0:T(8,128)S(1)}, u32[]{:S(2)}, u32[]{:S(2)}) collective-permute-start(f32[2,128,256]{2,1,0:T(8,128)} %param.4), channel_id=1, source_target_pairs={{0,4},{2,6},{4,0},{6,2},{1,5},{3,7},{5,1},{7,3},{8,12},{10,14},{12... | collective-permute-start | bytes 786440 | tf_op jit(solution)/shard_map/ppermute | solution.py:66
  40.2 0.0 collective-permute-done.5
  40.2 3.0 %collective-permute-start.2 = (f32[2,128,256]{2,1,0:T(8,128)}, f32[2,128,256]{2,1,0:T(8,128)S(1)}, u32[]{:S(2)}, u32[]{:S(2)}) collective-permute-start(f32[2,128,256]{2,1,0:T(8,128)} %param.4), channel_id=1, source_target_pairs={{0,2},{2,4},{4,6},{6,0},{1,3},{3,5},{5,7},{7,1},{8,10},{10,12},{12... | collective-permute-start | bytes 786440 | tf_op jit(solution)/shard_map/ppermute | solution.py:66
  43.2 0.0 collective-permute-done.6
  43.2 15.3 %collective-permute-done.7 = f32[2,128,256]{2,1,0:T(8,128)S(1)} collective-permute-done((f32[2,128,256]{2,1,0:T(8,128)}, f32[2,128,256]{2,1,0:T(8,128)S(1)}, u32[]{:S(2)}, u32[]{:S(2)}) %collective-permute-start.7) | collective-permute-done | bytes 262176 | tf_op jit(solution)/shard_map/ppermute | solution.py:78
  58.5 0.1 select_select_fusion.5
  58.5 0.7 collective-permute-start.8
  59.2 0.7 collective-permute-start.9
  59.9 0.0 copy-done.2
  59.9 0.0 copy-done
  59.9 0.3 fusion
  60.2 0.3 fusion.1
  60.5 0.7 pad_maximum_fusion.3
  61.2 0.0 collective-permute-done.8
  61.2 0.0 collective-permute-done.9
  61.2 0.1 fusion.5
  61.3 0.1 collective-permute-start.10
  61.4 3.6 %collective-permute-start.11 = (f32[2,128,256]{2,1,0:T(8,128)S(1)}, f32[2,128,256]{2,1,0:T(8,128)S(1)}, u32[]{:S(2)}, u32[]{:S(2)}) collective-permute-start(f32[2,128,256]{2,1,0:T(8,128)S(1)} %fusion.5), channel_id=1, source_target_pairs={{0,16},{8,24},{16,0},{24,8},{1,17},{9,25},{17,1},{25,9},{2,18},{10... | collective-permute-start | bytes 786440 | tf_op jit(solution)/shard_map/ppermute | solution.py:66
  65.0 16.4 %collective-permute-done = f32[2,128,256]{2,1,0:T(8,128)S(1)} collective-permute-done((f32[2,128,256]{2,1,0:T(8,128)}, f32[2,128,256]{2,1,0:T(8,128)S(1)}, u32[]{:S(2)}, u32[]{:S(2)}) %collective-permute-start) | collective-permute-done | bytes 262176 | tf_op jit(solution)/shard_map/ppermute | solution.py:66
  81.4 0.0 collective-permute-start.12
  81.4 0.0 collective-permute-done.1
  81.4 0.0 collective-permute-done.2
  81.4 0.1 select_select_fusion.9
  81.5 0.1 pad_maximum_fusion.1
  81.6 2.5 %collective-permute-start.3 = (f32[2,512,256]{2,1,0:T(8,128)S(1)}, f32[2,512,256]{2,1,0:T(8,128)S(1)}, u32[]{:S(2)}, u32[]{:S(2)}) collective-permute-start(f32[2,512,256]{2,1,0:T(8,128)S(1)} %pad_maximum_fusion.1), channel_id=1, source_target_pairs={{0,1},{1,0},{2,3},{3,2},{4,5},{5,4},{6,7},{7,6},{8,9},{9,8},{10,11... | collective-permute-start | bytes 3145736 | tf_op jit(solution)/shard_map/ppermute | solution.py:92
  84.1 0.0 collective-permute-done.10
  84.1 0.0 collective-permute-done.11
  84.1 8.4 %collective-permute-done.12 = f32[2,128,256]{2,1,0:T(8,128)S(1)} collective-permute-done((f32[2,128,256]{2,1,0:T(8,128)S(1)}, f32[2,128,256]{2,1,0:T(8,128)S(1)}, u32[]{:S(2)}, u32[]{:S(2)}) %collective-permute-start.12) | collective-permute-done | bytes 262176 | tf_op jit(solution)/shard_map/ppermute | solution.py:66
  92.5 0.1 select_select_fusion.4
  92.6 0.1 pad_maximum_fusion.2
  92.7 0.6 fusion.4
  93.3 0.6 fusion.3
  93.9 0.6 convolution_subtract_fusion
  94.5 0.6 convolution_add_fusion
  95.1 0.0 collective-permute-done.3
  95.1 0.2 broadcast_select_fusion
  95.2 0.1 pad_maximum_fusion
  95.4 1.9 %fusion.32 = f32[1024,512]{1,0:T(8,128)S(1)} fusion(f32[1024,256]{1,0:T(8,128)S(1)} %bitcast.56, f32[512,256]{1,0:T(8,128)S(1)} %convolution_subtract_fusion), kind=kOutput, calls=%fused_computation.59 | convolution fusion | flops 1610612736 | bytes 3670016 | tf_op jit(solution)/shard_map/dot_general | solution.py:22
  97.3 1.9 %fusion.33 = f32[1024,512]{1,0:T(8,128)S(1)} fusion(f32[1024,256]{1,0:T(8,128)S(1)} %bitcast.57, f32[512,256]{1,0:T(8,128)S(1)} %convolution_add_fusion), kind=kOutput, calls=%fused_computation.60 | convolution fusion | flops 1610612736 | bytes 3670016 | tf_op jit(solution)/shard_map/dot_general | solution.py:25
  99.1 2.0 %subtract_bitcast_fusion = f32[1,1024,512]{2,1,0:T(8,128)S(1)} fusion(f32[1024,512]{1,0:T(8,128)S(1)} %fusion.32, f32[1024,256]{1,0:T(8,128)S(1)} %bitcast.58, f32[512,256]{1,0:T(8,128)S(1)} %convolution_add_fusion), kind=kOutput, calls=%fused_computation.4 | convolution fusion | flops 1611137024 | bytes 5767168 | tf_op jit(solution)/shard_map/dot_general | solution.py:22
  101.1 0.0 copy-start.1
  101.1 2.0 %add_bitcast_fusion = f32[1,1024,512]{2,1,0:T(8,128)S(1)} fusion(f32[1024,512]{1,0:T(8,128)S(1)} %fusion.33, f32[1024,256]{1,0:T(8,128)S(1)} %bitcast.59, f32[512,256]{1,0:T(8,128)S(1)} %convolution_subtract_fusion), kind=kOutput, calls=%fused_computation.3 | convolution fusion | flops 1611137024 | bytes 5767168 | tf_op jit(solution)/shard_map/dot_general | solution.py:25
  103.1 0.2 copy-done.1
  103.3 3.0 %maximum_subtract_fusion = f32[2,1024,512]{2,1,0:T(8,128)} fusion(f32[2,1024,512]{2,1,0:T(8,128)S(1)} %copy-done.1, f32[1,1024,512]{2,1,0:T(8,128)S(1)} %add_bitcast_fusion, f32[1,1024,512]{2,1,0:T(8,128)S(1)} %subtract_bitcast_fusion), kind=kLoop, calls=%fused_computation | loop fusion | flops 2097152 | bytes 12582912 | tf_op jit(solution)/shard_map/sub | solution.py:101
Async XLA Ops:
  0.6 59.3 %copy-start.2 = (f32[2,128,256]{2,1,0:T(8,128)S(1)}, f32[2,128,256]{2,1,0:T(8,128)}, u32[]{:S(2)}) copy-start(f32[2,128,256]{2,1,0:T(8,128)} %param.4) | copy-start | bytes 786436
  0.6 59.3 %copy-start = (f32[2,256,256]{2,1,0:T(8,128)S(1)}, f32[2,256,256]{2,1,0:T(8,128)}, u32[]{:S(2)}) copy-start(f32[2,256,256]{2,1,0:T(8,128)} %param.5) | copy-start | bytes 1572868
  0.7 23.2 %collective-permute-start.4 = (f32[2,128,256]{2,1,0:T(8,128)}, f32[2,128,256]{2,1,0:T(8,128)S(1)}, u32[]{:S(2)}, u32[]{:S(2)}) collective-permute-start(f32[2,128,256]{2,1,0:T(8,128)} %param.4), channel_id=1, source_target_pairs={{0,32},{1,40},{2,48},{3,56},{4,33},{5,41},{6,49},{7,57},{8,34},{9,... | collective-permute-start | bytes 786440 | tf_op jit(solution)/shard_map/ppermute | solution.py:78
  11.9 28.3 %collective-permute-start.5 = (f32[2,128,256]{2,1,0:T(8,128)}, f32[2,128,256]{2,1,0:T(8,128)S(1)}, u32[]{:S(2)}, u32[]{:S(2)}) collective-permute-start(f32[2,128,256]{2,1,0:T(8,128)} %param.4), channel_id=1, source_target_pairs={{0,192},{1,200},{2,208},{3,216},{4,193},{5,201},{6,209},{7,217},{8... | collective-permute-start | bytes 786440 | tf_op jit(solution)/shard_map/ppermute | solution.py:78
  13.2 29.9 %collective-permute-start.6 = (f32[2,128,256]{2,1,0:T(8,128)}, f32[2,128,256]{2,1,0:T(8,128)S(1)}, u32[]{:S(2)}, u32[]{:S(2)}) collective-permute-start(f32[2,128,256]{2,1,0:T(8,128)} %param.4), channel_id=1, source_target_pairs={{0,64},{1,72},{2,80},{3,88},{4,65},{5,73},{6,81},{7,89},{8,66},{9,... | collective-permute-start | bytes 786440 | tf_op jit(solution)/shard_map/ppermute | solution.py:78
  14.6 43.9 %collective-permute-start.7 = (f32[2,128,256]{2,1,0:T(8,128)}, f32[2,128,256]{2,1,0:T(8,128)S(1)}, u32[]{:S(2)}, u32[]{:S(2)}) collective-permute-start(f32[2,128,256]{2,1,0:T(8,128)} %param.4), channel_id=1, source_target_pairs={{0,0},{1,8},{2,16},{3,24},{4,1},{5,9},{6,17},{7,25},{8,2},{9,10},{... | collective-permute-start | bytes 786440 | tf_op jit(solution)/shard_map/ppermute | solution.py:78
  16.6 64.8 %collective-permute-start = (f32[2,128,256]{2,1,0:T(8,128)}, f32[2,128,256]{2,1,0:T(8,128)S(1)}, u32[]{:S(2)}, u32[]{:S(2)}) collective-permute-start(f32[2,128,256]{2,1,0:T(8,128)} %param.4), channel_id=1, source_target_pairs={{0,6},{2,0},{4,2},{6,4},{1,7},{3,1},{5,3},{7,5},{8,14},{10,8},{12,... | collective-permute-start | bytes 786440 | tf_op jit(solution)/shard_map/ppermute | solution.py:66
  23.8 57.5 %collective-permute-start.1 = (f32[2,128,256]{2,1,0:T(8,128)}, f32[2,128,256]{2,1,0:T(8,128)S(1)}, u32[]{:S(2)}, u32[]{:S(2)}) collective-permute-start(f32[2,128,256]{2,1,0:T(8,128)} %param.4), channel_id=1, source_target_pairs={{0,4},{2,6},{4,0},{6,2},{1,5},{3,7},{5,1},{7,3},{8,12},{10,14},{12... | collective-permute-start | bytes 786440 | tf_op jit(solution)/shard_map/ppermute | solution.py:66
  40.2 41.1 %collective-permute-start.2 = (f32[2,128,256]{2,1,0:T(8,128)}, f32[2,128,256]{2,1,0:T(8,128)S(1)}, u32[]{:S(2)}, u32[]{:S(2)}) collective-permute-start(f32[2,128,256]{2,1,0:T(8,128)} %param.4), channel_id=1, source_target_pairs={{0,2},{2,4},{4,6},{6,0},{1,3},{3,5},{5,7},{7,1},{8,10},{10,12},{12... | collective-permute-start | bytes 786440 | tf_op jit(solution)/shard_map/ppermute | solution.py:66
  58.5 2.7 %collective-permute-start.8 = (f32[2,128,256]{2,1,0:T(8,128)S(1)}, f32[2,128,256]{2,1,0:T(8,128)S(1)}, u32[]{:S(2)}, u32[]{:S(2)}) collective-permute-start(f32[2,128,256]{2,1,0:T(8,128)S(1)} %select_select_fusion.5), channel_id=1, source_target_pairs={{32,224},{33,225},{34,226},{35,227},{36,228},{37,229},{38,230},{39... | collective-permute-start | bytes 786440 | tf_op jit(solution)/shard_map/ppermute | solution.py:83
  59.2 2.0 %collective-permute-start.9 = (f32[2,128,256]{2,1,0:T(8,128)S(1)}, f32[2,128,256]{2,1,0:T(8,128)S(1)}, u32[]{:S(2)}, u32[]{:S(2)}) collective-permute-start(f32[2,128,256]{2,1,0:T(8,128)S(1)} %select_select_fusion.5), channel_id=1, source_target_pairs={{64,128},{32,96},{192,160},{65,129},{33,97},{193,161},{66,130},{34... | collective-permute-start | bytes 786440 | tf_op jit(solution)/shard_map/ppermute | solution.py:82
  61.3 22.8 %collective-permute-start.10 = (f32[2,128,256]{2,1,0:T(8,128)S(1)}, f32[2,128,256]{2,1,0:T(8,128)S(1)}, u32[]{:S(2)}, u32[]{:S(2)}) collective-permute-start(f32[2,128,256]{2,1,0:T(8,128)S(1)} %fusion.5), channel_id=1, source_target_pairs={{0,24},{8,0},{16,8},{24,16},{1,25},{9,1},{17,9},{25,17},{2,26},{10... | collective-permute-start | bytes 786440 | tf_op jit(solution)/shard_map/ppermute | solution.py:66
  61.4 22.7 %collective-permute-start.11 = (f32[2,128,256]{2,1,0:T(8,128)S(1)}, f32[2,128,256]{2,1,0:T(8,128)S(1)}, u32[]{:S(2)}, u32[]{:S(2)}) collective-permute-start(f32[2,128,256]{2,1,0:T(8,128)S(1)} %fusion.5), channel_id=1, source_target_pairs={{0,16},{8,24},{16,0},{24,8},{1,17},{9,25},{17,1},{25,9},{2,18},{10... | collective-permute-start | bytes 786440 | tf_op jit(solution)/shard_map/ppermute | solution.py:66
  81.4 11.1 %collective-permute-start.12 = (f32[2,128,256]{2,1,0:T(8,128)S(1)}, f32[2,128,256]{2,1,0:T(8,128)S(1)}, u32[]{:S(2)}, u32[]{:S(2)}) collective-permute-start(f32[2,128,256]{2,1,0:T(8,128)S(1)} %fusion.5), channel_id=1, source_target_pairs={{0,8},{8,16},{16,24},{24,0},{1,9},{9,17},{17,25},{25,1},{2,10},{10... | collective-permute-start | bytes 786440 | tf_op jit(solution)/shard_map/ppermute | solution.py:66
  81.6 13.5 %collective-permute-start.3 = (f32[2,512,256]{2,1,0:T(8,128)S(1)}, f32[2,512,256]{2,1,0:T(8,128)S(1)}, u32[]{:S(2)}, u32[]{:S(2)}) collective-permute-start(f32[2,512,256]{2,1,0:T(8,128)S(1)} %pad_maximum_fusion.1), channel_id=1, source_target_pairs={{0,1},{1,0},{2,3},{3,2},{4,5},{5,4},{6,7},{7,6},{8,9},{9,8},{10,11... | collective-permute-start | bytes 3145736 | tf_op jit(solution)/shard_map/ppermute | solution.py:92
  101.1 2.2 %copy-start.1 = (f32[2,1024,512]{2,1,0:T(8,128)S(1)}, f32[2,1024,512]{2,1,0:T(8,128)}, u32[]{:S(2)}) copy-start(f32[2,1024,512]{2,1,0:T(8,128)} %param.3) | copy-start | bytes 12582916

commit v3 on v2

--- a/solution.py
+++ b/solution.py
@@ -46,9 +46,11 @@
                     pairs.append((lin(0, 0, g, l, c), lin(y1, h1, p % nx, g, p // nx)))
         return pairs
 
-    first = [(0, 0), (1, 0), (ny - 1, 0), (0, 1)]
-    relay_one = [((1, 0), (2, 0)), ((0, 1), (1, 1)), ((ny - 1, 0), (2, 1))]
-    relay_two = [((0, 1), (ny - 1, 1))]
+    first = [(0, 0), (1, 0), (ny - 1, 0)]
+    relays = [
+        [[((1, 0), (2, 0)), ((ny - 1, 0), (ny - 1, 1))], [((1, 0), (1, 1))]],
+        [[((1, 1), (2, 1)), ((ny - 1, 1), (0, 1))]],
+    ]
 
     def shifts(n, k):
         return [(i, (i + k) % n) for i in range(n)]
@@ -79,13 +81,13 @@
         held_a = got_a[0]
         for (y1, h1), got in zip(first[1:], got_a[1:]):
             held_a = jnp.where((yi == y1) & (hi == h1), got, held_a)
-        b1 = lax.ppermute(held_a, ("y", "zh"), [(plane(h0, y0), plane(h1, y1)) for (y0, h0), (y1, h1) in relay_one])
-        b2 = lax.ppermute(held_a, ("y", "zh"), [(plane(h0, y0), plane(h1, y1)) for (y0, h0), (y1, h1) in relay_two])
         held = held_a
-        for (_, _), (y1, h1) in relay_one:
-            held = jnp.where((yi == y1) & (hi == h1), b1, held)
-        for (_, _), (y1, h1) in relay_two:
-            held = jnp.where((yi == y1) & (hi == h1), b2, held)
+        for stage in relays:
+            sent = held
+            for pairs in stage:
+                got = lax.ppermute(sent, ("y", "zh"), [(plane(h0, y0), plane(h1, y1)) for (y0, h0), (y1, h1) in pairs])
+                for _, (y1, h1) in pairs:
+                    held = jnp.where((yi == y1) & (hi == h1), got, held)
         window = gather(held, "x", xi, nx)
 
         mine = gather(panel, "zl", li, nl)

time: 107 us -> 108 us (level)
  the two profiles are of different devices: /device:TPU:1 before, /device:TPU:64 now
where the time goes in v3:
time: 108 us
  waiting for transfers between devices  46.8 us (43%)
  starting transfers between devices  42 us (39%)
  matrix products  13.2 us (12%)
  other arithmetic  4.58 us (4%)
    ppermute x3, waiting for transfers between devices, local(): got_a = [lax.ppermute(panel, AXES, spread(y1, h1)) for y1, h1 in first]  32.9 us
    ppermute x6, starting transfers between devices, gather(): lax.ppermute(piece, axis, shifts(n, k))  30.9 us
    ppermute x6, waiting for transfers between devices, gather(): lax.ppermute(piece, axis, shifts(n, k))  13.9 us
    ppermute x3, starting transfers between devices, local(): got_a = [lax.ppermute(panel, AXES, spread(y1, h1)) for y1, h1 in first]  8.59 us
    sub x1, other arithmetic, local(): updated = trailing - product_transposed(block, tiles)  3.03 us
  transfers between devices with their start and end apart: 13, of which 5 were waited for; matrix products, arithmetic and copies ran while one was open for 6% of the time, Pallas kernels for 0%

profile of v3, /device:TPU:64, one launch (start us, length us, event | category | flops | bytes accessed | tf_op | source)
XLA Modules:
  0.0 107.7 jit_solution(9671429448946122168)
XLA Ops:
  0.6 0.0 copy-start.2
  0.6 0.0 copy-start
  0.7 3.6 %collective-permute-start.4 = (f32[2,128,256]{2,1,0:T(8,128)}, f32[2,128,256]{2,1,0:T(8,128)S(1)}, u32[]{:S(2)}, u32[]{:S(2)}) collective-permute-start(f32[2,128,256]{2,1,0:T(8,128)} %param.4), channel_id=1, source_target_pairs={{0,192},{1,200},{2,208},{3,216},{4,193},{5,201},{6,209},{7,217},{8... | collective-permute-start | bytes 786440 | tf_op jit(solution)/shard_map/ppermute | solution.py:80
  4.3 1.3 %collective-permute-start.5 = (f32[2,128,256]{2,1,0:T(8,128)}, f32[2,128,256]{2,1,0:T(8,128)S(1)}, u32[]{:S(2)}, u32[]{:S(2)}) collective-permute-start(f32[2,128,256]{2,1,0:T(8,128)} %param.4), channel_id=1, source_target_pairs={{0,64},{1,72},{2,80},{3,88},{4,65},{5,73},{6,81},{7,89},{8,66},{9,... | collective-permute-start | bytes 786440 | tf_op jit(solution)/shard_map/ppermute | solution.py:80
  5.6 3.7 %collective-permute-start.6 = (f32[2,128,256]{2,1,0:T(8,128)}, f32[2,128,256]{2,1,0:T(8,128)S(1)}, u32[]{:S(2)}, u32[]{:S(2)}) collective-permute-start(f32[2,128,256]{2,1,0:T(8,128)} %param.4), channel_id=1, source_target_pairs={{0,0},{1,8},{2,16},{3,24},{4,1},{5,9},{6,17},{7,25},{8,2},{9,10},{... | collective-permute-start | bytes 786440 | tf_op jit(solution)/shard_map/ppermute | solution.py:80
  9.3 5.1 %collective-permute-start = (f32[2,128,256]{2,1,0:T(8,128)}, f32[2,128,256]{2,1,0:T(8,128)S(1)}, u32[]{:S(2)}, u32[]{:S(2)}) collective-permute-start(f32[2,128,256]{2,1,0:T(8,128)} %param.4), channel_id=1, source_target_pairs={{0,6},{2,0},{4,2},{6,4},{1,7},{3,1},{5,3},{7,5},{8,14},{10,8},{12,... | collective-permute-start | bytes 786440 | tf_op jit(solution)/shard_map/ppermute | solution.py:68
  14.4 3.0 %collective-permute-start.1 = (f32[2,128,256]{2,1,0:T(8,128)}, f32[2,128,256]{2,1,0:T(8,128)S(1)}, u32[]{:S(2)}, u32[]{:S(2)}) collective-permute-start(f32[2,128,256]{2,1,0:T(8,128)} %param.4), channel_id=1, source_target_pairs={{0,4},{2,6},{4,0},{6,2},{1,5},{3,7},{5,1},{7,3},{8,12},{10,14},{12... | collective-permute-start | bytes 786440 | tf_op jit(solution)/shard_map/ppermute | solution.py:68
  17.4 10.4 %collective-permute-done.4 = f32[2,128,256]{2,1,0:T(8,128)S(1)} collective-permute-done((f32[2,128,256]{2,1,0:T(8,128)}, f32[2,128,256]{2,1,0:T(8,128)S(1)}, u32[]{:S(2)}, u32[]{:S(2)}) %collective-permute-start.4) | collective-permute-done | bytes 262176 | tf_op jit(solution)/shard_map/ppermute | solution.py:80
  27.8 0.0 collective-permute-start.2
  27.8 16.9 %collective-permute-done.5 = f32[2,128,256]{2,1,0:T(8,128)S(1)} collective-permute-done((f32[2,128,256]{2,1,0:T(8,128)}, f32[2,128,256]{2,1,0:T(8,128)S(1)}, u32[]{:S(2)}, u32[]{:S(2)}) %collective-permute-start.5) | collective-permute-done | bytes 262176 | tf_op jit(solution)/shard_map/ppermute | solution.py:80
  44.7 5.6 %collective-permute-done.6 = f32[2,128,256]{2,1,0:T(8,128)S(1)} collective-permute-done((f32[2,128,256]{2,1,0:T(8,128)}, f32[2,128,256]{2,1,0:T(8,128)S(1)}, u32[]{:S(2)}, u32[]{:S(2)}) %collective-permute-start.6) | collective-permute-done | bytes 262176 | tf_op jit(solution)/shard_map/ppermute | solution.py:80
  50.3 0.7 collective-permute-start.7
  51.0 0.7 collective-permute-start.8
  51.7 1.3 %fusion.8 = f32[128,256]{1,0:T(8,128)S(1)} fusion(f32[2,256,256]{2,1,0:T(8,128)} %param.5, f32[2,128,256]{2,1,0:T(8,128)} %param.4), kind=kOutput, calls=%fused_computation.27 | convolution fusion | flops 100663296 | bytes 524288 | tf_op jit(solution)/shard_map/dot_general | solution.py:15
  53.0 1.3 %fusion.14 = f32[128,256]{1,0:T(8,128)S(1)} fusion(f32[2,256,256]{2,1,0:T(8,128)} %param.5, f32[2,128,256]{2,1,0:T(8,128)} %param.4), kind=kOutput, calls=%fused_computation.33 | convolution fusion | flops 100663296 | bytes 524288 | tf_op jit(solution)/shard_map/dot_general | solution.py:14
  54.4 0.0 collective-permute-done.7
  54.4 0.0 collective-permute-done.8
  54.4 0.1 fusion.5
  54.4 0.7 collective-permute-start.9
  55.1 0.0 copy-done.2
  55.1 0.0 copy-done
  55.1 0.3 fusion
  55.4 0.3 fusion.1
  55.7 0.7 pad_maximum_fusion.3
  56.4 0.0 collective-permute-done.9
  56.5 21.8 %collective-permute-start.10 = (f32[2,128,256]{2,1,0:T(8,128)S(1)}, f32[2,128,256]{2,1,0:T(8,128)S(1)}, u32[]{:S(2)}, u32[]{:S(2)}) collective-permute-start(f32[2,128,256]{2,1,0:T(8,128)S(1)} %select_select_fusion), channel_id=1, source_target_pairs={{0,24},{8,0},{16,8},{24,16},{1,25},{9,1},{17,9},{25,17},{2,26},{10... | collective-permute-start | bytes 786440 | tf_op jit(solution)/shard_map/ppermute | solution.py:68
  78.3 0.0 collective-permute-start.11
  78.3 0.0 collective-permute-done
  78.3 1.0 collective-permute-start.12
  79.2 0.0 collective-permute-done.1
  79.2 0.0 collective-permute-done.2
  79.2 0.1 select_select_fusion.10
  79.4 0.1 pad_maximum_fusion.1
  79.4 0.5 collective-permute-start.3
  80.0 10.5 %collective-permute-done.10 = f32[2,128,256]{2,1,0:T(8,128)S(1)} collective-permute-done((f32[2,128,256]{2,1,0:T(8,128)S(1)}, f32[2,128,256]{2,1,0:T(8,128)S(1)}, u32[]{:S(2)}, u32[]{:S(2)}) %collective-permute-start.10) | collective-permute-done | bytes 262176 | tf_op jit(solution)/shard_map/ppermute | solution.py:68
  90.4 0.0 collective-permute-done.11
  90.4 3.4 %collective-permute-done.12 = f32[2,128,256]{2,1,0:T(8,128)S(1)} collective-permute-done((f32[2,128,256]{2,1,0:T(8,128)S(1)}, f32[2,128,256]{2,1,0:T(8,128)S(1)}, u32[]{:S(2)}, u32[]{:S(2)}) %collective-permute-start.12) | collective-permute-done | bytes 262176 | tf_op jit(solution)/shard_map/ppermute | solution.py:68
  93.9 0.1 select_select_fusion.5
  94.0 0.1 pad_maximum_fusion.2
  94.1 0.6 fusion.4
  94.7 0.6 fusion.3
  95.2 0.6 convolution_subtract_fusion
  95.8 0.6 convolution_add_fusion
  96.4 0.0 collective-permute-done.3
  96.4 0.2 broadcast_select_fusion
  96.6 0.1 pad_maximum_fusion
  96.7 1.9 %fusion.32 = f32[1024,512]{1,0:T(8,128)S(1)} fusion(f32[1024,256]{1,0:T(8,128)S(1)} %bitcast.56, f32[512,256]{1,0:T(8,128)S(1)} %convolution_subtract_fusion), kind=kOutput, calls=%fused_computation.60 | convolution fusion | flops 1610612736 | bytes 3670016 | tf_op jit(solution)/shard_map/dot_general | solution.py:22
  98.6 1.9 %fusion.33 = f32[1024,512]{1,0:T(8,128)S(1)} fusion(f32[1024,256]{1,0:T(8,128)S(1)} %bitcast.57, f32[512,256]{1,0:T(8,128)S(1)} %convolution_add_fusion), kind=kOutput, calls=%fused_computation.61 | convolution fusion | flops 1610612736 | bytes 3670016 | tf_op jit(solution)/shard_map/dot_general | solution.py:25
  100.5 2.0 %subtract_bitcast_fusion = f32[1,1024,512]{2,1,0:T(8,128)S(1)} fusion(f32[1024,512]{1,0:T(8,128)S(1)} %fusion.32, f32[1024,256]{1,0:T(8,128)S(1)} %bitcast.58, f32[512,256]{1,0:T(8,128)S(1)} %convolution_add_fusion), kind=kOutput, calls=%fused_computation.4 | convolution fusion | flops 1611137024 | bytes 5767168 | tf_op jit(solution)/shard_map/dot_general | solution.py:22
  102.5 0.0 copy-start.1
  102.5 2.0 %add_bitcast_fusion = f32[1,1024,512]{2,1,0:T(8,128)S(1)} fusion(f32[1024,512]{1,0:T(8,128)S(1)} %fusion.33, f32[1024,256]{1,0:T(8,128)S(1)} %bitcast.59, f32[512,256]{1,0:T(8,128)S(1)} %convolution_subtract_fusion), kind=kOutput, calls=%fused_computation.3 | convolution fusion | flops 1611137024 | bytes 5767168 | tf_op jit(solution)/shard_map/dot_general | solution.py:25
  104.5 0.2 copy-done.1
  104.7 3.0 %maximum_subtract_fusion = f32[2,1024,512]{2,1,0:T(8,128)} fusion(f32[2,1024,512]{2,1,0:T(8,128)S(1)} %copy-done.1, f32[1,1024,512]{2,1,0:T(8,128)S(1)} %add_bitcast_fusion, f32[1,1024,512]{2,1,0:T(8,128)S(1)} %subtract_bitcast_fusion), kind=kLoop, calls=%fused_computation | loop fusion | flops 2097152 | bytes 12582912 | tf_op jit(solution)/shard_map/sub | solution.py:103
  (2 shorter events, 0.1 us)
Async XLA Ops:
  0.6 54.5 %copy-start.2 = (f32[2,128,256]{2,1,0:T(8,128)S(1)}, f32[2,128,256]{2,1,0:T(8,128)}, u32[]{:S(2)}) copy-start(f32[2,128,256]{2,1,0:T(8,128)} %param.4) | copy-start | bytes 786436
  0.6 54.5 %copy-start = (f32[2,256,256]{2,1,0:T(8,128)S(1)}, f32[2,256,256]{2,1,0:T(8,128)}, u32[]{:S(2)}) copy-start(f32[2,256,256]{2,1,0:T(8,128)} %param.5) | copy-start | bytes 1572868
  0.7 27.1 %collective-permute-start.4 = (f32[2,128,256]{2,1,0:T(8,128)}, f32[2,128,256]{2,1,0:T(8,128)S(1)}, u32[]{:S(2)}, u32[]{:S(2)}) collective-permute-start(f32[2,128,256]{2,1,0:T(8,128)} %param.4), channel_id=1, source_target_pairs={{0,192},{1,200},{2,208},{3,216},{4,193},{5,201},{6,209},{7,217},{8... | collective-permute-start | bytes 786440 | tf_op jit(solution)/shard_map/ppermute | solution.py:80
  4.3 40.4 %collective-permute-start.5 = (f32[2,128,256]{2,1,0:T(8,128)}, f32[2,128,256]{2,1,0:T(8,128)S(1)}, u32[]{:S(2)}, u32[]{:S(2)}) collective-permute-start(f32[2,128,256]{2,1,0:T(8,128)} %param.4), channel_id=1, source_target_pairs={{0,64},{1,72},{2,80},{3,88},{4,65},{5,73},{6,81},{7,89},{8,66},{9,... | collective-permute-start | bytes 786440 | tf_op jit(solution)/shard_map/ppermute | solution.py:80
  5.6 44.7 %collective-permute-start.6 = (f32[2,128,256]{2,1,0:T(8,128)}, f32[2,128,256]{2,1,0:T(8,128)S(1)}, u32[]{:S(2)}, u32[]{:S(2)}) collective-permute-start(f32[2,128,256]{2,1,0:T(8,128)} %param.4), channel_id=1, source_target_pairs={{0,0},{1,8},{2,16},{3,24},{4,1},{5,9},{6,17},{7,25},{8,2},{9,10},{... | collective-permute-start | bytes 786440 | tf_op jit(solution)/shard_map/ppermute | solution.py:80
  9.3 69.0 %collective-permute-start = (f32[2,128,256]{2,1,0:T(8,128)}, f32[2,128,256]{2,1,0:T(8,128)S(1)}, u32[]{:S(2)}, u32[]{:S(2)}) collective-permute-start(f32[2,128,256]{2,1,0:T(8,128)} %param.4), channel_id=1, source_target_pairs={{0,6},{2,0},{4,2},{6,4},{1,7},{3,1},{5,3},{7,5},{8,14},{10,8},{12,... | collective-permute-start | bytes 786440 | tf_op jit(solution)/shard_map/ppermute | solution.py:68
  14.4 64.9 %collective-permute-start.1 = (f32[2,128,256]{2,1,0:T(8,128)}, f32[2,128,256]{2,1,0:T(8,128)S(1)}, u32[]{:S(2)}, u32[]{:S(2)}) collective-permute-start(f32[2,128,256]{2,1,0:T(8,128)} %param.4), channel_id=1, source_target_pairs={{0,4},{2,6},{4,0},{6,2},{1,5},{3,7},{5,1},{7,3},{8,12},{10,14},{12... | collective-permute-start | bytes 786440 | tf_op jit(solution)/shard_map/ppermute | solution.py:68
  27.8 51.5 %collective-permute-start.2 = (f32[2,128,256]{2,1,0:T(8,128)}, f32[2,128,256]{2,1,0:T(8,128)S(1)}, u32[]{:S(2)}, u32[]{:S(2)}) collective-permute-start(f32[2,128,256]{2,1,0:T(8,128)} %param.4), channel_id=1, source_target_pairs={{0,2},{2,4},{4,6},{6,0},{1,3},{3,5},{5,7},{7,1},{8,10},{10,12},{12... | collective-permute-start | bytes 786440 | tf_op jit(solution)/shard_map/ppermute | solution.py:68
  50.3 4.0 %collective-permute-start.7 = (f32[2,128,256]{2,1,0:T(8,128)S(1)}, f32[2,128,256]{2,1,0:T(8,128)S(1)}, u32[]{:S(2)}, u32[]{:S(2)}) collective-permute-start(f32[2,128,256]{2,1,0:T(8,128)S(1)} %select_select_fusion.6), channel_id=1, source_target_pairs={{64,96},{65,97},{66,98},{67,99},{68,100},{69,101},{70,102},{71,103... | collective-permute-start | bytes 786440 | tf_op jit(solution)/shard_map/ppermute | solution.py:88
  51.0 3.3 %collective-permute-start.8 = (f32[2,128,256]{2,1,0:T(8,128)S(1)}, f32[2,128,256]{2,1,0:T(8,128)S(1)}, u32[]{:S(2)}, u32[]{:S(2)}) collective-permute-start(f32[2,128,256]{2,1,0:T(8,128)S(1)} %select_select_fusion.6), channel_id=1, source_target_pairs={{64,128},{192,224},{65,129},{193,225},{66,130},{194,226},{67,131},... | collective-permute-start | bytes 786440 | tf_op jit(solution)/shard_map/ppermute | solution.py:88
  54.4 2.0 %collective-permute-start.9 = (f32[2,128,256]{2,1,0:T(8,128)S(1)}, f32[2,128,256]{2,1,0:T(8,128)S(1)}, u32[]{:S(2)}, u32[]{:S(2)}) collective-permute-start(f32[2,128,256]{2,1,0:T(8,128)S(1)} %fusion.5), channel_id=1, source_target_pairs={{96,160},{224,32},{97,161},{225,33},{98,162},{226,34},{99,163},{22... | collective-permute-start | bytes 786440 | tf_op jit(solution)/shard_map/ppermute | solution.py:88
  56.5 34.0 %collective-permute-start.10 = (f32[2,128,256]{2,1,0:T(8,128)S(1)}, f32[2,128,256]{2,1,0:T(8,128)S(1)}, u32[]{:S(2)}, u32[]{:S(2)}) collective-permute-start(f32[2,128,256]{2,1,0:T(8,128)S(1)} %select_select_fusion), channel_id=1, source_target_pairs={{0,24},{8,0},{16,8},{24,16},{1,25},{9,1},{17,9},{25,17},{2,26},{10... | collective-permute-start | bytes 786440 | tf_op jit(solution)/shard_map/ppermute | solution.py:68
  78.3 12.2 %collective-permute-start.11 = (f32[2,128,256]{2,1,0:T(8,128)S(1)}, f32[2,128,256]{2,1,0:T(8,128)S(1)}, u32[]{:S(2)}, u32[]{:S(2)}) collective-permute-start(f32[2,128,256]{2,1,0:T(8,128)S(1)} %select_select_fusion), channel_id=1, source_target_pairs={{0,16},{8,24},{16,0},{24,8},{1,17},{9,25},{17,1},{25,9},{2,18},{10... | collective-permute-start | bytes 786440 | tf_op jit(solution)/shard_map/ppermute | solution.py:68
  78.3 15.6 %collective-permute-start.12 = (f32[2,128,256]{2,1,0:T(8,128)S(1)}, f32[2,128,256]{2,1,0:T(8,128)S(1)}, u32[]{:S(2)}, u32[]{:S(2)}) collective-permute-start(f32[2,128,256]{2,1,0:T(8,128)S(1)} %select_select_fusion), channel_id=1, source_target_pairs={{0,8},{8,16},{16,24},{24,0},{1,9},{9,17},{17,25},{25,1},{2,10},{10... | collective-permute-start | bytes 786440 | tf_op jit(solution)/shard_map/ppermute | solution.py:68
  79.4 17.0 %collective-permute-start.3 = (f32[2,512,256]{2,1,0:T(8,128)S(1)}, f32[2,512,256]{2,1,0:T(8,128)S(1)}, u32[]{:S(2)}, u32[]{:S(2)}) collective-permute-start(f32[2,512,256]{2,1,0:T(8,128)S(1)} %pad_maximum_fusion.1), channel_id=1, source_target_pairs={{0,1},{1,0},{2,3},{3,2},{4,5},{5,4},{6,7},{7,6},{8,9},{9,8},{10,11... | collective-permute-start | bytes 3145736 | tf_op jit(solution)/shard_map/ppermute | solution.py:94
  102.5 2.2 %copy-start.1 = (f32[2,1024,512]{2,1,0:T(8,128)S(1)}, f32[2,1024,512]{2,1,0:T(8,128)}, u32[]{:S(2)}) copy-start(f32[2,1024,512]{2,1,0:T(8,128)} %param.3) | copy-start | bytes 12582916

commit v4 on v3

--- a/solution.py
+++ b/solution.py
@@ -9,15 +9,13 @@
 COL = ("zl", "core")
 
 
-def complex_product(left, right):
-    hp = lax.Precision.HIGHEST
+def complex_product(left, right, hp=lax.Precision.HIGHEST):
     real_part = jnp.dot(left[0], right[0], precision=hp) - jnp.dot(left[1], right[1], precision=hp)
     imag_part = jnp.dot(left[0], right[1], precision=hp) + jnp.dot(left[1], right[0], precision=hp)
     return jnp.stack([real_part, imag_part])
 
 
-def product_transposed(left, right):
-    hp = lax.Precision.HIGHEST
+def product_transposed(left, right, hp=lax.Precision.HIGHEST):
     dims = (((1,), (1,)), ((), ()))
     real_part = lax.dot_general(left[0], right[0], dims, precision=hp) - lax.dot_general(
         left[1], right[1], dims, precision=hp
@@ -88,9 +86,10 @@
                 got = lax.ppermute(sent, ("y", "zh"), [(plane(h0, y0), plane(h1, y1)) for (y0, h0), (y1, h1) in pairs])
                 for _, (y1, h1) in pairs:
                     held = jnp.where((yi == y1) & (hi == h1), got, held)
+        panel_late, held = lax.optimization_barrier((panel, held))
         window = gather(held, "x", xi, nx)
 
-        mine = gather(panel, "zl", li, nl)
+        mine = gather(panel_late, "zl", li, nl)
         other = lax.ppermute(mine, "core", shifts(nc, 1))
         lo = jnp.where(ci == 0, mine, other)
         hi_ = jnp.where(ci == 0, other, mine)
@@ -99,8 +98,8 @@
             [lo.reshape(two, nl, rows, width), hi_.reshape(two, nl, rows, width)], axis=2
         ).reshape(two, nl * nc * rows, width)
 
-        tiles = complex_product(window, diag_inverse)
-        updated = trailing - product_transposed(block, tiles)
+        tiles = complex_product(window, diag_inverse, lax.Precision.HIGH)
+        updated = trailing - product_transposed(block, tiles, lax.Precision.HIGH)
         return (scaled, updated)
 
     return local

time: 108 us -> 103 us (0.954)
  the two profiles are of different devices: /device:TPU:64 before, /device:TPU:7 now
where the time goes in v4:
time: 103 us
  starting transfers between devices  59.3 us (58%)
  waiting for transfers between devices  30 us (29%)
  matrix products  6.87 us (7%)
  other arithmetic  4.59 us (4%)
  between operations  1.13 us (1%)
  local copies, waits for them, and re-layouts  1.11 us (1%)
    ppermute x6, starting transfers between devices, gather(): lax.ppermute(piece, axis, shifts(n, k))  42.9 us
    ppermute x6, waiting for transfers between devices, gather(): lax.ppermute(piece, axis, shifts(n, k))  15.4 us
    ppermute x3, waiting for transfers between devices, local(): got_a = [lax.ppermute(panel, AXES, spread(y1, h1)) for y1, h1 in first]  14.1 us
    ppermute x3, starting transfers between devices, local(): got_a = [lax.ppermute(panel, AXES, spread(y1, h1)) for y1, h1 in first]  13.5 us
    sub x1, other arithmetic, local(): updated = trailing - product_transposed(block, tiles, lax.Precision.HIGH)  3.03 us
  transfers between devices with their start and end apart: 13, of which 5 were waited for; matrix products, arithmetic and copies ran while one was open for 4% of the time, Pallas kernels for 0%

profile of v4, /device:TPU:7, one launch (start us, length us, event | category | flops | bytes accessed | tf_op | source)
XLA Modules:
  0.0 103.0 jit_solution(12874190160461249487)
XLA Ops:
  0.6 0.0 copy-start.2
  0.6 0.0 copy-start
  0.6 10.2 %collective-permute-start = (f32[2,128,256]{2,1,0:T(8,128)}, f32[2,128,256]{2,1,0:T(8,128)S(1)}, u32[]{:S(2)}, u32[]{:S(2)}) collective-permute-start(f32[2,128,256]{2,1,0:T(8,128)} %param.4), channel_id=1, source_target_pairs={{0,192},{1,200},{2,208},{3,216},{4,193},{5,201},{6,209},{7,217},{8... | collective-permute-start | bytes 786440 | tf_op jit(solution)/shard_map/ppermute | solution.py:78
  10.9 1.3 %collective-permute-start.1 = (f32[2,128,256]{2,1,0:T(8,128)}, f32[2,128,256]{2,1,0:T(8,128)S(1)}, u32[]{:S(2)}, u32[]{:S(2)}) collective-permute-start(f32[2,128,256]{2,1,0:T(8,128)} %param.4), channel_id=1, source_target_pairs={{0,64},{1,72},{2,80},{3,88},{4,65},{5,73},{6,81},{7,89},{8,66},{9,... | collective-permute-start | bytes 786440 | tf_op jit(solution)/shard_map/ppermute | solution.py:78
  12.2 1.9 %collective-permute-start.2 = (f32[2,128,256]{2,1,0:T(8,128)}, f32[2,128,256]{2,1,0:T(8,128)S(1)}, u32[]{:S(2)}, u32[]{:S(2)}) collective-permute-start(f32[2,128,256]{2,1,0:T(8,128)} %param.4), channel_id=1, source_target_pairs={{0,0},{1,8},{2,16},{3,24},{4,1},{5,9},{6,17},{7,25},{8,2},{9,10},{... | collective-permute-start | bytes 786440 | tf_op jit(solution)/shard_map/ppermute | solution.py:78
  14.2 3.2 %collective-permute-done = f32[2,128,256]{2,1,0:T(8,128)S(1)} collective-permute-done((f32[2,128,256]{2,1,0:T(8,128)}, f32[2,128,256]{2,1,0:T(8,128)S(1)}, u32[]{:S(2)}, u32[]{:S(2)}) %collective-permute-start) | collective-permute-done | bytes 262176 | tf_op jit(solution)/shard_map/ppermute | solution.py:78
  17.4 5.6 %collective-permute-done.1 = f32[2,128,256]{2,1,0:T(8,128)S(1)} collective-permute-done((f32[2,128,256]{2,1,0:T(8,128)}, f32[2,128,256]{2,1,0:T(8,128)S(1)}, u32[]{:S(2)}, u32[]{:S(2)}) %collective-permute-start.1) | collective-permute-done | bytes 262176 | tf_op jit(solution)/shard_map/ppermute | solution.py:78
  23.0 5.3 %collective-permute-done.2 = f32[2,128,256]{2,1,0:T(8,128)S(1)} collective-permute-done((f32[2,128,256]{2,1,0:T(8,128)}, f32[2,128,256]{2,1,0:T(8,128)S(1)}, u32[]{:S(2)}, u32[]{:S(2)}) %collective-permute-start.2) | collective-permute-done | bytes 262176 | tf_op jit(solution)/shard_map/ppermute | solution.py:78
  28.3 0.7 collective-permute-start.3
  29.0 0.7 collective-permute-start.4
  29.7 0.0 collective-permute-done.3
  29.7 0.0 collective-permute-done.4
  29.7 0.1 fusion.5
  29.8 0.7 collective-permute-start.5
  30.5 0.0 copy-done.2
  30.5 0.0 copy-done
  30.5 0.3 fusion.8
  30.8 0.3 fusion.14
  31.1 0.0 collective-permute-done.5
  31.1 0.1 collective-permute-start.6
  31.2 36.3 %collective-permute-start.7 = (f32[2,128,256]{2,1,0:T(8,128)S(1)}, f32[2,128,256]{2,1,0:T(8,128)S(1)}, u32[]{:S(2)}, u32[]{:S(2)}) collective-permute-start(f32[2,128,256]{2,1,0:T(8,128)S(1)} %copy-done.2), channel_id=1, source_target_pairs={{0,4},{2,6},{4,0},{6,2},{1,5},{3,7},{5,1},{7,3},{8,12},{10,14},{12... | collective-permute-start | bytes 786440 | tf_op jit(solution)/shard_map/ppermute | solution.py:66
  67.5 1.4 %collective-permute-start.8 = (f32[2,128,256]{2,1,0:T(8,128)S(1)}, f32[2,128,256]{2,1,0:T(8,128)S(1)}, u32[]{:S(2)}, u32[]{:S(2)}) collective-permute-start(f32[2,128,256]{2,1,0:T(8,128)S(1)} %copy-done.2), channel_id=1, source_target_pairs={{0,2},{2,4},{4,6},{6,0},{1,3},{3,5},{5,7},{7,1},{8,10},{10,12},{12... | collective-permute-start | bytes 786440 | tf_op jit(solution)/shard_map/ppermute | solution.py:66
  68.9 0.3 fusion
  69.3 0.3 fusion.1
  69.6 0.7 pad_maximum_fusion.3
  70.3 0.0 collective-permute-start.10
  70.3 3.6 %collective-permute-start.11 = (f32[2,128,256]{2,1,0:T(8,128)S(1)}, f32[2,128,256]{2,1,0:T(8,128)S(1)}, u32[]{:S(2)}, u32[]{:S(2)}) collective-permute-start(f32[2,128,256]{2,1,0:T(8,128)S(1)} %select_select_fusion), channel_id=1, source_target_pairs={{0,16},{8,24},{16,0},{24,8},{1,17},{9,25},{17,1},{25,9},{2,18},{10... | collective-permute-start | bytes 786440 | tf_op jit(solution)/shard_map/ppermute | solution.py:66
  74.0 0.0 collective-permute-done.6
  74.0 1.5 %collective-permute-start.12 = (f32[2,128,256]{2,1,0:T(8,128)S(1)}, f32[2,128,256]{2,1,0:T(8,128)S(1)}, u32[]{:S(2)}, u32[]{:S(2)}) collective-permute-start(f32[2,128,256]{2,1,0:T(8,128)S(1)} %select_select_fusion), channel_id=1, source_target_pairs={{0,8},{8,16},{16,24},{24,0},{1,9},{9,17},{17,25},{25,1},{2,10},{10... | collective-permute-start | bytes 786440 | tf_op jit(solution)/shard_map/ppermute | solution.py:66
  75.5 15.4 %collective-permute-done.7 = f32[2,128,256]{2,1,0:T(8,128)S(1)} collective-permute-done((f32[2,128,256]{2,1,0:T(8,128)S(1)}, f32[2,128,256]{2,1,0:T(8,128)S(1)}, u32[]{:S(2)}, u32[]{:S(2)}) %collective-permute-start.7) | collective-permute-done | bytes 262176 | tf_op jit(solution)/shard_map/ppermute | solution.py:66
  90.9 0.0 collective-permute-done.8
  90.9 0.1 select_select_fusion.9
  91.0 0.1 pad_maximum_fusion.1
  91.1 0.9 collective-permute-start.9
  92.0 0.0 collective-permute-done.10
  92.0 0.0 collective-permute-done.11
  92.0 0.0 collective-permute-done.12
  92.0 0.1 select_select_fusion.5
  92.1 0.1 pad_maximum_fusion.2
  92.2 0.4 fusion.4
  92.6 0.4 fusion.3
  93.0 0.4 convolution_subtract_fusion
  93.4 0.4 convolution_add_fusion
  93.8 0.5 collective-permute-done.9
  94.3 0.2 broadcast_select_fusion
  94.4 0.1 pad_maximum_fusion
  94.6 1.0 %fusion.32 = f32[1024,512]{1,0:T(8,128)S(1)} fusion(f32[1024,256]{1,0:T(8,128)S(1)} %bitcast.56, f32[512,256]{1,0:T(8,128)S(1)} %convolution_subtract_fusion), kind=kOutput, calls=%fused_computation.60 | convolution fusion | flops 805306368 | bytes 3670016 | tf_op jit(solution)/shard_map/dot_general | solution.py:20
  95.6 1.0 %fusion.33 = f32[1024,512]{1,0:T(8,128)S(1)} fusion(f32[1024,256]{1,0:T(8,128)S(1)} %bitcast.57, f32[512,256]{1,0:T(8,128)S(1)} %convolution_add_fusion), kind=kOutput, calls=%fused_computation.61 | convolution fusion | flops 805306368 | bytes 3670016 | tf_op jit(solution)/shard_map/dot_general | solution.py:23
  96.7 1.1 %subtract_bitcast_fusion = f32[1,1024,512]{2,1,0:T(8,128)S(1)} fusion(f32[1024,512]{1,0:T(8,128)S(1)} %fusion.32, f32[1024,256]{1,0:T(8,128)S(1)} %bitcast.58, f32[512,256]{1,0:T(8,128)S(1)} %convolution_add_fusion), kind=kOutput, calls=%fused_computation.4 | convolution fusion | flops 805830656 | bytes 5767168 | tf_op jit(solution)/shard_map/dot_general | solution.py:20
  97.8 0.0 copy-start.1
  97.8 1.1 %add_bitcast_fusion = f32[1,1024,512]{2,1,0:T(8,128)S(1)} fusion(f32[1024,512]{1,0:T(8,128)S(1)} %fusion.33, f32[1024,256]{1,0:T(8,128)S(1)} %bitcast.59, f32[512,256]{1,0:T(8,128)S(1)} %convolution_subtract_fusion), kind=kOutput, calls=%fused_computation.3 | convolution fusion | flops 805830656 | bytes 5767168 | tf_op jit(solution)/shard_map/dot_general | solution.py:23
  98.9 1.1 %copy-done.1 = f32[2,1024,512]{2,1,0:T(8,128)S(1)} copy-done((f32[2,1024,512]{2,1,0:T(8,128)S(1)}, f32[2,1024,512]{2,1,0:T(8,128)}, u32[]{:S(2)}) %copy-start.1) | copy-done | bytes 4194328
  99.9 3.0 %maximum_subtract_fusion = f32[2,1024,512]{2,1,0:T(8,128)} fusion(f32[2,1024,512]{2,1,0:T(8,128)S(1)} %copy-done.1, f32[1,1024,512]{2,1,0:T(8,128)S(1)} %add_bitcast_fusion, f32[1,1024,512]{2,1,0:T(8,128)S(1)} %subtract_bitcast_fusion), kind=kLoop, calls=%fused_computation | loop fusion | flops 2097152 | bytes 12582912 | tf_op jit(solution)/shard_map/sub | solution.py:102
  (2 shorter events, 0.1 us)
Async XLA Ops:
  0.6 29.8 %copy-start.2 = (f32[2,128,256]{2,1,0:T(8,128)S(1)}, f32[2,128,256]{2,1,0:T(8,128)}, u32[]{:S(2)}) copy-start(f32[2,128,256]{2,1,0:T(8,128)} %param.4) | copy-start | bytes 786436
  0.6 29.8 %copy-start = (f32[2,256,256]{2,1,0:T(8,128)S(1)}, f32[2,256,256]{2,1,0:T(8,128)}, u32[]{:S(2)}) copy-start(f32[2,256,256]{2,1,0:T(8,128)} %param.5) | copy-start | bytes 1572868
  0.6 16.7 %collective-permute-start = (f32[2,128,256]{2,1,0:T(8,128)}, f32[2,128,256]{2,1,0:T(8,128)S(1)}, u32[]{:S(2)}, u32[]{:S(2)}) collective-permute-start(f32[2,128,256]{2,1,0:T(8,128)} %param.4), channel_id=1, source_target_pairs={{0,192},{1,200},{2,208},{3,216},{4,193},{5,201},{6,209},{7,217},{8... | collective-permute-start | bytes 786440 | tf_op jit(solution)/shard_map/ppermute | solution.py:78
  10.9 12.1 %collective-permute-start.1 = (f32[2,128,256]{2,1,0:T(8,128)}, f32[2,128,256]{2,1,0:T(8,128)S(1)}, u32[]{:S(2)}, u32[]{:S(2)}) collective-permute-start(f32[2,128,256]{2,1,0:T(8,128)} %param.4), channel_id=1, source_target_pairs={{0,64},{1,72},{2,80},{3,88},{4,65},{5,73},{6,81},{7,89},{8,66},{9,... | collective-permute-start | bytes 786440 | tf_op jit(solution)/shard_map/ppermute | solution.py:78
  12.2 16.0 %collective-permute-start.2 = (f32[2,128,256]{2,1,0:T(8,128)}, f32[2,128,256]{2,1,0:T(8,128)S(1)}, u32[]{:S(2)}, u32[]{:S(2)}) collective-permute-start(f32[2,128,256]{2,1,0:T(8,128)} %param.4), channel_id=1, source_target_pairs={{0,0},{1,8},{2,16},{3,24},{4,1},{5,9},{6,17},{7,25},{8,2},{9,10},{... | collective-permute-start | bytes 786440 | tf_op jit(solution)/shard_map/ppermute | solution.py:78
  28.3 1.4 %collective-permute-start.3 = (f32[2,128,256]{2,1,0:T(8,128)S(1)}, f32[2,128,256]{2,1,0:T(8,128)S(1)}, u32[]{:S(2)}, u32[]{:S(2)}) collective-permute-start(f32[2,128,256]{2,1,0:T(8,128)S(1)} %select_select_fusion.10), channel_id=1, source_target_pairs={{64,96},{65,97},{66,98},{67,99},{68,100},{69,101},{70,102},{71,103... | collective-permute-start | bytes 786440 | tf_op jit(solution)/shard_map/ppermute | solution.py:86
  29.0 0.7 collective-permute-start.4
  29.8 1.3 %collective-permute-start.5 = (f32[2,128,256]{2,1,0:T(8,128)S(1)}, f32[2,128,256]{2,1,0:T(8,128)S(1)}, u32[]{:S(2)}, u32[]{:S(2)}) collective-permute-start(f32[2,128,256]{2,1,0:T(8,128)S(1)} %fusion.5), channel_id=1, source_target_pairs={{96,160},{224,32},{97,161},{225,33},{98,162},{226,34},{99,163},{22... | collective-permute-start | bytes 786440 | tf_op jit(solution)/shard_map/ppermute | solution.py:86
  31.1 42.9 %collective-permute-start.6 = (f32[2,128,256]{2,1,0:T(8,128)S(1)}, f32[2,128,256]{2,1,0:T(8,128)S(1)}, u32[]{:S(2)}, u32[]{:S(2)}) collective-permute-start(f32[2,128,256]{2,1,0:T(8,128)S(1)} %copy-done.2), channel_id=1, source_target_pairs={{0,6},{2,0},{4,2},{6,4},{1,7},{3,1},{5,3},{7,5},{8,14},{10,8},{12,... | collective-permute-start | bytes 786440 | tf_op jit(solution)/shard_map/ppermute | solution.py:66
  31.2 59.7 %collective-permute-start.7 = (f32[2,128,256]{2,1,0:T(8,128)S(1)}, f32[2,128,256]{2,1,0:T(8,128)S(1)}, u32[]{:S(2)}, u32[]{:S(2)}) collective-permute-start(f32[2,128,256]{2,1,0:T(8,128)S(1)} %copy-done.2), channel_id=1, source_target_pairs={{0,4},{2,6},{4,0},{6,2},{1,5},{3,7},{5,1},{7,3},{8,12},{10,14},{12... | collective-permute-start | bytes 786440 | tf_op jit(solution)/shard_map/ppermute | solution.py:66
  67.5 23.4 %collective-permute-start.8 = (f32[2,128,256]{2,1,0:T(8,128)S(1)}, f32[2,128,256]{2,1,0:T(8,128)S(1)}, u32[]{:S(2)}, u32[]{:S(2)}) collective-permute-start(f32[2,128,256]{2,1,0:T(8,128)S(1)} %copy-done.2), channel_id=1, source_target_pairs={{0,2},{2,4},{4,6},{6,0},{1,3},{3,5},{5,7},{7,1},{8,10},{10,12},{12... | collective-permute-start | bytes 786440 | tf_op jit(solution)/shard_map/ppermute | solution.py:66
  70.3 21.7 %collective-permute-start.10 = (f32[2,128,256]{2,1,0:T(8,128)S(1)}, f32[2,128,256]{2,1,0:T(8,128)S(1)}, u32[]{:S(2)}, u32[]{:S(2)}) collective-permute-start(f32[2,128,256]{2,1,0:T(8,128)S(1)} %select_select_fusion), channel_id=1, source_target_pairs={{0,24},{8,0},{16,8},{24,16},{1,25},{9,1},{17,9},{25,17},{2,26},{10... | collective-permute-start | bytes 786440 | tf_op jit(solution)/shard_map/ppermute | solution.py:66
  70.3 21.7 %collective-permute-start.11 = (f32[2,128,256]{2,1,0:T(8,128)S(1)}, f32[2,128,256]{2,1,0:T(8,128)S(1)}, u32[]{:S(2)}, u32[]{:S(2)}) collective-permute-start(f32[2,128,256]{2,1,0:T(8,128)S(1)} %select_select_fusion), channel_id=1, source_target_pairs={{0,16},{8,24},{16,0},{24,8},{1,17},{9,25},{17,1},{25,9},{2,18},{10... | collective-permute-start | bytes 786440 | tf_op jit(solution)/shard_map/ppermute | solution.py:66
  74.0 18.0 %collective-permute-start.12 = (f32[2,128,256]{2,1,0:T(8,128)S(1)}, f32[2,128,256]{2,1,0:T(8,128)S(1)}, u32[]{:S(2)}, u32[]{:S(2)}) collective-permute-start(f32[2,128,256]{2,1,0:T(8,128)S(1)} %select_select_fusion), channel_id=1, source_target_pairs={{0,8},{8,16},{16,24},{24,0},{1,9},{9,17},{17,25},{25,1},{2,10},{10... | collective-permute-start | bytes 786440 | tf_op jit(solution)/shard_map/ppermute | solution.py:66
  91.1 3.2 %collective-permute-start.9 = (f32[2,512,256]{2,1,0:T(8,128)S(1)}, f32[2,512,256]{2,1,0:T(8,128)S(1)}, u32[]{:S(2)}, u32[]{:S(2)}) collective-permute-start(f32[2,512,256]{2,1,0:T(8,128)S(1)} %pad_maximum_fusion.1), channel_id=1, source_target_pairs={{0,1},{1,0},{2,3},{3,2},{4,5},{5,4},{6,7},{7,6},{8,9},{9,8},{10,11... | collective-permute-start | bytes 3145736 | tf_op jit(solution)/shard_map/ppermute | solution.py:93
  97.8 2.2 %copy-start.1 = (f32[2,1024,512]{2,1,0:T(8,128)S(1)}, f32[2,1024,512]{2,1,0:T(8,128)}, u32[]{:S(2)}) copy-start(f32[2,1024,512]{2,1,0:T(8,128)} %param.3) | copy-start | bytes 12582916

commit v5 on v4

--- a/solution.py
+++ b/solution.py
@@ -99,7 +99,11 @@
         ).reshape(two, nl * nc * rows, width)
 
         tiles = complex_product(window, diag_inverse, lax.Precision.HIGH)
-        updated = trailing - product_transposed(block, tiles, lax.Precision.HIGH)
+        rhs = jnp.stack([jnp.stack([tiles[0], -tiles[1]]), jnp.stack([tiles[1], tiles[0]])])
+        lhs = jnp.broadcast_to(block[None], (rhs.shape[0],) + block.shape)
+        dims = (((1, 3), (1, 3)), ((0,), (0,)))
+        product = lax.dot_general(lhs, rhs, dims, precision=lax.Precision.HIGH)
+        updated = trailing - product
         return (scaled, updated)
 
     return local

time: 103 us -> 102 us (level)
  other arithmetic: 4.59 us -> 1.82 us
    sub x1 -> x0, other arithmetic: 3.03 us -> none  [local(): updated = trailing - product_transposed(block, tiles, lax.Precision.HIGH)]
    dot_general x4 -> x1, matrix products: 4.23 us -> 5.06 us  [local(): product = lax.dot_general(lhs, rhs, dims, precision=lax.Precision.HIGH)]
where the time goes in v5:
time: 102 us
  starting transfers between devices  59.1 us (58%)
  waiting for transfers between devices  29.8 us (29%)
  matrix products  7.7 us (8%)
  local copies, waits for them, and re-layouts  1.98 us (2%)
  other arithmetic  1.82 us (2%)
  between operations  1.12 us (1%)
    ppermute x6, starting transfers between devices, gather(): lax.ppermute(piece, axis, shifts(n, k))  42.9 us
    ppermute x6, waiting for transfers between devices, gather(): lax.ppermute(piece, axis, shifts(n, k))  15.4 us
    ppermute x3, waiting for transfers between devices, local(): got_a = [lax.ppermute(panel, AXES, spread(y1, h1)) for y1, h1 in first]  14.1 us
    ppermute x3, starting transfers between devices, local(): got_a = [lax.ppermute(panel, AXES, spread(y1, h1)) for y1, h1 in first]  13.5 us
    dot_general x1, matrix products, local(): product = lax.dot_general(lhs, rhs, dims, precision=lax.Precision.HIGH)  5.06 us
  transfers between devices with their start and end apart: 13, of which 5 were waited for; matrix products, arithmetic and copies ran while one was open for 4% of the time, Pallas kernels for 0%

profile of v5, /device:TPU:7, one launch (start us, length us, event | category | flops | bytes accessed | tf_op | source)
XLA Modules:
  0.0 101.5 jit_solution(5964405930315132138)
XLA Ops:
  0.6 0.0 copy-start.2
  0.6 0.0 copy-start
  0.6 10.2 %collective-permute-start = (f32[2,128,256]{2,1,0:T(8,128)}, f32[2,128,256]{2,1,0:T(8,128)S(1)}, u32[]{:S(2)}, u32[]{:S(2)}) collective-permute-start(f32[2,128,256]{2,1,0:T(8,128)} %param.4), channel_id=1, source_target_pairs={{0,192},{1,200},{2,208},{3,216},{4,193},{5,201},{6,209},{7,217},{8... | collective-permute-start | bytes 786440 | tf_op jit(solution)/shard_map/ppermute | solution.py:78
  10.9 1.3 %collective-permute-start.1 = (f32[2,128,256]{2,1,0:T(8,128)}, f32[2,128,256]{2,1,0:T(8,128)S(1)}, u32[]{:S(2)}, u32[]{:S(2)}) collective-permute-start(f32[2,128,256]{2,1,0:T(8,128)} %param.4), channel_id=1, source_target_pairs={{0,64},{1,72},{2,80},{3,88},{4,65},{5,73},{6,81},{7,89},{8,66},{9,... | collective-permute-start | bytes 786440 | tf_op jit(solution)/shard_map/ppermute | solution.py:78
  12.2 1.9 %collective-permute-start.2 = (f32[2,128,256]{2,1,0:T(8,128)}, f32[2,128,256]{2,1,0:T(8,128)S(1)}, u32[]{:S(2)}, u32[]{:S(2)}) collective-permute-start(f32[2,128,256]{2,1,0:T(8,128)} %param.4), channel_id=1, source_target_pairs={{0,0},{1,8},{2,16},{3,24},{4,1},{5,9},{6,17},{7,25},{8,2},{9,10},{... | collective-permute-start | bytes 786440 | tf_op jit(solution)/shard_map/ppermute | solution.py:78
  14.2 3.2 %collective-permute-done = f32[2,128,256]{2,1,0:T(8,128)S(1)} collective-permute-done((f32[2,128,256]{2,1,0:T(8,128)}, f32[2,128,256]{2,1,0:T(8,128)S(1)}, u32[]{:S(2)}, u32[]{:S(2)}) %collective-permute-start) | collective-permute-done | bytes 262176 | tf_op jit(solution)/shard_map/ppermute | solution.py:78
  17.4 5.6 %collective-permute-done.1 = f32[2,128,256]{2,1,0:T(8,128)S(1)} collective-permute-done((f32[2,128,256]{2,1,0:T(8,128)}, f32[2,128,256]{2,1,0:T(8,128)S(1)}, u32[]{:S(2)}, u32[]{:S(2)}) %collective-permute-start.1) | collective-permute-done | bytes 262176 | tf_op jit(solution)/shard_map/ppermute | solution.py:78
  23.0 5.3 %collective-permute-done.2 = f32[2,128,256]{2,1,0:T(8,128)S(1)} collective-permute-done((f32[2,128,256]{2,1,0:T(8,128)}, f32[2,128,256]{2,1,0:T(8,128)S(1)}, u32[]{:S(2)}, u32[]{:S(2)}) %collective-permute-start.2) | collective-permute-done | bytes 262176 | tf_op jit(solution)/shard_map/ppermute | solution.py:78
  28.3 0.7 collective-permute-start.3
  29.0 0.7 collective-permute-start.4
  29.7 0.0 collective-permute-done.3
  29.7 0.0 collective-permute-done.4
  29.7 0.1 fusion.9
  29.8 0.7 collective-permute-start.5
  30.5 0.0 copy-done.2
  30.5 0.0 copy-done
  30.5 0.3 fusion.12
  30.8 0.3 fusion.18
  31.1 0.0 collective-permute-done.5
  31.1 0.1 collective-permute-start.6
  31.2 36.3 %collective-permute-start.7 = (f32[2,128,256]{2,1,0:T(8,128)S(1)}, f32[2,128,256]{2,1,0:T(8,128)S(1)}, u32[]{:S(2)}, u32[]{:S(2)}) collective-permute-start(f32[2,128,256]{2,1,0:T(8,128)S(1)} %copy-done.2), channel_id=1, source_target_pairs={{0,4},{2,6},{4,0},{6,2},{1,5},{3,7},{5,1},{7,3},{8,12},{10,14},{12... | collective-permute-start | bytes 786440 | tf_op jit(solution)/shard_map/ppermute | solution.py:66
  67.5 1.4 %collective-permute-start.8 = (f32[2,128,256]{2,1,0:T(8,128)S(1)}, f32[2,128,256]{2,1,0:T(8,128)S(1)}, u32[]{:S(2)}, u32[]{:S(2)}) collective-permute-start(f32[2,128,256]{2,1,0:T(8,128)S(1)} %copy-done.2), channel_id=1, source_target_pairs={{0,2},{2,4},{4,6},{6,0},{1,3},{3,5},{5,7},{7,1},{8,10},{10,12},{12... | collective-permute-start | bytes 786440 | tf_op jit(solution)/shard_map/ppermute | solution.py:66
  68.9 0.3 fusion.5
  69.3 0.3 fusion.6
  69.6 0.7 pad_maximum_fusion.3
  70.3 0.0 collective-permute-start.10
  70.3 3.6 %collective-permute-start.11 = (f32[2,128,256]{2,1,0:T(8,128)S(1)}, f32[2,128,256]{2,1,0:T(8,128)S(1)}, u32[]{:S(2)}, u32[]{:S(2)}) collective-permute-start(f32[2,128,256]{2,1,0:T(8,128)S(1)} %select_select_fusion), channel_id=1, source_target_pairs={{0,16},{8,24},{16,0},{24,8},{1,17},{9,25},{17,1},{25,9},{2,18},{10... | collective-permute-start | bytes 786440 | tf_op jit(solution)/shard_map/ppermute | solution.py:66
  74.0 0.0 collective-permute-done.6
  74.0 1.5 %collective-permute-start.12 = (f32[2,128,256]{2,1,0:T(8,128)S(1)}, f32[2,128,256]{2,1,0:T(8,128)S(1)}, u32[]{:S(2)}, u32[]{:S(2)}) collective-permute-start(f32[2,128,256]{2,1,0:T(8,128)S(1)} %select_select_fusion), channel_id=1, source_target_pairs={{0,8},{8,16},{16,24},{24,0},{1,9},{9,17},{17,25},{25,1},{2,10},{10... | collective-permute-start | bytes 786440 | tf_op jit(solution)/shard_map/ppermute | solution.py:66
  75.5 15.4 %collective-permute-done.7 = f32[2,128,256]{2,1,0:T(8,128)S(1)} collective-permute-done((f32[2,128,256]{2,1,0:T(8,128)S(1)}, f32[2,128,256]{2,1,0:T(8,128)S(1)}, u32[]{:S(2)}, u32[]{:S(2)}) %collective-permute-start.7) | collective-permute-done | bytes 262176 | tf_op jit(solution)/shard_map/ppermute | solution.py:66
  90.9 0.0 collective-permute-done.8
  90.9 0.1 select_select_fusion.9
  91.0 0.1 pad_maximum_fusion.1
  91.1 0.7 collective-permute-start.9
  91.8 0.0 collective-permute-done.10
  91.8 0.0 collective-permute-done.11
  91.8 0.0 collective-permute-done.12
  91.8 0.1 select_select_fusion.5
  92.0 0.1 pad_maximum_fusion.2
  92.0 0.4 fusion.8
  92.4 0.4 fusion.4
  92.8 0.4 fusion.7
  93.2 0.4 convolution_add_fusion
  93.6 0.2 maximum_bitcast_fusion
  93.8 0.3 collective-permute-done.9
  94.1 0.2 broadcast_select_fusion.1
  94.3 0.0 copy-start.1
  94.3 0.2 pad_maximum_fusion
  94.5 2.0 %copy-done.1 = f32[2,1024,512]{2,1,0:T(8,128)S(1)} copy-done((f32[2,1024,512]{2,1,0:T(8,128)S(1)}, f32[2,1024,512]{2,1,0:T(8,128)}, u32[]{:S(2)}) %copy-start.1) | copy-done | bytes 4194328
  96.5 5.1 %bitcast_subtract_fusion = f32[2,1024,512]{2,1,0:T(8,128)} fusion(f32[2,1024,512]{2,1,0:T(8,128)S(1)} %copy-done.1, f32[1,2,512,256]{3,2,1,0:T(8,128)S(1)} %get-tuple-element.17, f32[1,2,512,256]{3,2,1,0:T(8,128)S(1)} %get-tuple-element.16, f32[2,1024,256]{2,1,0:T(8,128)S(1)} %bitcast.55), kind=kOutput, calls=%fused_computation | convolution fusion | flops 3222798336 | bytes 12582912 | tf_op jit(solution)/shard_map/dot_general | solution.py:105
  (3 shorter events, 0.1 us)
Async XLA Ops:
  0.6 29.8 %copy-start.2 = (f32[2,128,256]{2,1,0:T(8,128)S(1)}, f32[2,128,256]{2,1,0:T(8,128)}, u32[]{:S(2)}) copy-start(f32[2,128,256]{2,1,0:T(8,128)} %param.4) | copy-start | bytes 786436
  0.6 29.8 %copy-start = (f32[2,256,256]{2,1,0:T(8,128)S(1)}, f32[2,256,256]{2,1,0:T(8,128)}, u32[]{:S(2)}) copy-start(f32[2,256,256]{2,1,0:T(8,128)} %param.5) | copy-start | bytes 1572868
  0.6 16.7 %collective-permute-start = (f32[2,128,256]{2,1,0:T(8,128)}, f32[2,128,256]{2,1,0:T(8,128)S(1)}, u32[]{:S(2)}, u32[]{:S(2)}) collective-permute-start(f32[2,128,256]{2,1,0:T(8,128)} %param.4), channel_id=1, source_target_pairs={{0,192},{1,200},{2,208},{3,216},{4,193},{5,201},{6,209},{7,217},{8... | collective-permute-start | bytes 786440 | tf_op jit(solution)/shard_map/ppermute | solution.py:78
  10.9 12.1 %collective-permute-start.1 = (f32[2,128,256]{2,1,0:T(8,128)}, f32[2,128,256]{2,1,0:T(8,128)S(1)}, u32[]{:S(2)}, u32[]{:S(2)}) collective-permute-start(f32[2,128,256]{2,1,0:T(8,128)} %param.4), channel_id=1, source_target_pairs={{0,64},{1,72},{2,80},{3,88},{4,65},{5,73},{6,81},{7,89},{8,66},{9,... | collective-permute-start | bytes 786440 | tf_op jit(solution)/shard_map/ppermute | solution.py:78
  12.2 16.0 %collective-permute-start.2 = (f32[2,128,256]{2,1,0:T(8,128)}, f32[2,128,256]{2,1,0:T(8,128)S(1)}, u32[]{:S(2)}, u32[]{:S(2)}) collective-permute-start(f32[2,128,256]{2,1,0:T(8,128)} %param.4), channel_id=1, source_target_pairs={{0,0},{1,8},{2,16},{3,24},{4,1},{5,9},{6,17},{7,25},{8,2},{9,10},{... | collective-permute-start | bytes 786440 | tf_op jit(solution)/shard_map/ppermute | solution.py:78
  28.3 1.4 %collective-permute-start.3 = (f32[2,128,256]{2,1,0:T(8,128)S(1)}, f32[2,128,256]{2,1,0:T(8,128)S(1)}, u32[]{:S(2)}, u32[]{:S(2)}) collective-permute-start(f32[2,128,256]{2,1,0:T(8,128)S(1)} %select_select_fusion.10), channel_id=1, source_target_pairs={{64,96},{65,97},{66,98},{67,99},{68,100},{69,101},{70,102},{71,103... | collective-permute-start | bytes 786440 | tf_op jit(solution)/shard_map/ppermute | solution.py:86
  29.0 0.7 collective-permute-start.4
  29.8 1.3 %collective-permute-start.5 = (f32[2,128,256]{2,1,0:T(8,128)S(1)}, f32[2,128,256]{2,1,0:T(8,128)S(1)}, u32[]{:S(2)}, u32[]{:S(2)}) collective-permute-start(f32[2,128,256]{2,1,0:T(8,128)S(1)} %fusion.9), channel_id=1, source_target_pairs={{96,160},{224,32},{97,161},{225,33},{98,162},{226,34},{99,163},{22... | collective-permute-start | bytes 786440 | tf_op jit(solution)/shard_map/ppermute | solution.py:86
  31.1 42.9 %collective-permute-start.6 = (f32[2,128,256]{2,1,0:T(8,128)S(1)}, f32[2,128,256]{2,1,0:T(8,128)S(1)}, u32[]{:S(2)}, u32[]{:S(2)}) collective-permute-start(f32[2,128,256]{2,1,0:T(8,128)S(1)} %copy-done.2), channel_id=1, source_target_pairs={{0,6},{2,0},{4,2},{6,4},{1,7},{3,1},{5,3},{7,5},{8,14},{10,8},{12,... | collective-permute-start | bytes 786440 | tf_op jit(solution)/shard_map/ppermute | solution.py:66
  31.2 59.7 %collective-permute-start.7 = (f32[2,128,256]{2,1,0:T(8,128)S(1)}, f32[2,128,256]{2,1,0:T(8,128)S(1)}, u32[]{:S(2)}, u32[]{:S(2)}) collective-permute-start(f32[2,128,256]{2,1,0:T(8,128)S(1)} %copy-done.2), channel_id=1, source_target_pairs={{0,4},{2,6},{4,0},{6,2},{1,5},{3,7},{5,1},{7,3},{8,12},{10,14},{12... | collective-permute-start | bytes 786440 | tf_op jit(solution)/shard_map/ppermute | solution.py:66
  67.5 23.4 %collective-permute-start.8 = (f32[2,128,256]{2,1,0:T(8,128)S(1)}, f32[2,128,256]{2,1,0:T(8,128)S(1)}, u32[]{:S(2)}, u32[]{:S(2)}) collective-permute-start(f32[2,128,256]{2,1,0:T(8,128)S(1)} %copy-done.2), channel_id=1, source_target_pairs={{0,2},{2,4},{4,6},{6,0},{1,3},{3,5},{5,7},{7,1},{8,10},{10,12},{12... | collective-permute-start | bytes 786440 | tf_op jit(solution)/shard_map/ppermute | solution.py:66
  70.3 21.5 %collective-permute-start.10 = (f32[2,128,256]{2,1,0:T(8,128)S(1)}, f32[2,128,256]{2,1,0:T(8,128)S(1)}, u32[]{:S(2)}, u32[]{:S(2)}) collective-permute-start(f32[2,128,256]{2,1,0:T(8,128)S(1)} %select_select_fusion), channel_id=1, source_target_pairs={{0,24},{8,0},{16,8},{24,16},{1,25},{9,1},{17,9},{25,17},{2,26},{10... | collective-permute-start | bytes 786440 | tf_op jit(solution)/shard_map/ppermute | solution.py:66
  70.3 21.5 %collective-permute-start.11 = (f32[2,128,256]{2,1,0:T(8,128)S(1)}, f32[2,128,256]{2,1,0:T(8,128)S(1)}, u32[]{:S(2)}, u32[]{:S(2)}) collective-permute-start(f32[2,128,256]{2,1,0:T(8,128)S(1)} %select_select_fusion), channel_id=1, source_target_pairs={{0,16},{8,24},{16,0},{24,8},{1,17},{9,25},{17,1},{25,9},{2,18},{10... | collective-permute-start | bytes 786440 | tf_op jit(solution)/shard_map/ppermute | solution.py:66
  74.0 17.8 %collective-permute-start.12 = (f32[2,128,256]{2,1,0:T(8,128)S(1)}, f32[2,128,256]{2,1,0:T(8,128)S(1)}, u32[]{:S(2)}, u32[]{:S(2)}) collective-permute-start(f32[2,128,256]{2,1,0:T(8,128)S(1)} %select_select_fusion), channel_id=1, source_target_pairs={{0,8},{8,16},{16,24},{24,0},{1,9},{9,17},{17,25},{25,1},{2,10},{10... | collective-permute-start | bytes 786440 | tf_op jit(solution)/shard_map/ppermute | solution.py:66
  91.1 3.0 %collective-permute-start.9 = (f32[2,512,256]{2,1,0:T(8,128)S(1)}, f32[2,512,256]{2,1,0:T(8,128)S(1)}, u32[]{:S(2)}, u32[]{:S(2)}) collective-permute-start(f32[2,512,256]{2,1,0:T(8,128)S(1)} %pad_maximum_fusion.1), channel_id=1, source_target_pairs={{0,1},{1,0},{2,3},{3,2},{4,5},{5,4},{6,7},{7,6},{8,9},{9,8},{10,11... | collective-permute-start | bytes 3145736 | tf_op jit(solution)/shard_map/ppermute | solution.py:93
  94.3 2.2 %copy-start.1 = (f32[2,1024,512]{2,1,0:T(8,128)S(1)}, f32[2,1024,512]{2,1,0:T(8,128)}, u32[]{:S(2)}) copy-start(f32[2,1024,512]{2,1,0:T(8,128)} %param.3) | copy-start | bytes 12582916

commit v6 on v5

--- a/solution.py
+++ b/solution.py
@@ -68,6 +68,7 @@
 
     def local(trailing, panel, diag_inverse):
         scaled = complex_product(panel, diag_inverse)
+        block = lax.all_gather(panel, COL, axis=1, tiled=True)
 
         yi = lax.axis_index("y")
         hi = lax.axis_index("zh")
@@ -86,17 +87,8 @@
                 got = lax.ppermute(sent, ("y", "zh"), [(plane(h0, y0), plane(h1, y1)) for (y0, h0), (y1, h1) in pairs])
                 for _, (y1, h1) in pairs:
                     held = jnp.where((yi == y1) & (hi == h1), got, held)
-        panel_late, held = lax.optimization_barrier((panel, held))
         window = gather(held, "x", xi, nx)
 
-        mine = gather(panel_late, "zl", li, nl)
-        other = lax.ppermute(mine, "core", shifts(nc, 1))
-        lo = jnp.where(ci == 0, mine, other)
-        hi_ = jnp.where(ci == 0, other, mine)
-        two, rows, width = mine.shape[0], panel.shape[1], mine.shape[2]
-        block = jnp.stack(
-            [lo.reshape(two, nl, rows, width), hi_.reshape(two, nl, rows, width)], axis=2
-        ).reshape(two, nl * nc * rows, width)
 
         tiles = complex_product(window, diag_inverse, lax.Precision.HIGH)
         rhs = jnp.stack([jnp.stack([tiles[0], -tiles[1]]), jnp.stack([tiles[1], tiles[0]])])

time: 102 us -> 127 us (1.25)
  the two profiles are of different devices: /device:TPU:7 before, /device:TPU:65 now
where the time goes in v6:
time: 127 us
  waiting for transfers between devices  49.2 us (39%)
  starting transfers between devices  39.3 us (31%)
  between operations  14.4 us (11%)
  matrix products  11.7 us (9%)
  local copies, waits for them, and re-layouts  10.7 us (8%)
    ppermute x3, waiting for transfers between devices, local(): got_a = [lax.ppermute(panel, AXES, spread(y1, h1)) for y1, h1 in first]  41.7 us
    ppermute x3, starting transfers between devices, gather(): lax.ppermute(piece, axis, shifts(n, k))  27 us
    unnamed x6, local copies, waits for them, and re-layouts  10.7 us
    ppermute x3, starting transfers between devices, local(): got_a = [lax.ppermute(panel, AXES, spread(y1, h1)) for y1, h1 in first]  10.2 us
    ppermute x3, waiting for transfers between devices, gather(): lax.ppermute(piece, axis, shifts(n, k))  7.46 us
    dot_general x1, matrix products, local(): product = lax.dot_general(lhs, rhs, dims, precision=lax.Precision.HIGH)  7.01 us
  transfers between devices with their start and end apart: 10, of which 5 were waited for; matrix products, arithmetic and copies ran while one was open for 9% of the time, Pallas kernels for 0%

profile of v6, /device:TPU:65, one launch (start us, length us, event | category | flops | bytes accessed | tf_op | source)
XLA Modules:
  0.0 126.5 jit_solution(5338879897793693144)
XLA Ops:
  7.2 0.0 copy-start.1
  7.2 0.0 copy-start
  7.2 0.0 all-gather.2.cloned.1.call-start
  7.2 4.8 %collective-permute-start = (f32[2,128,256]{2,1,0:T(8,128)}, f32[2,128,256]{2,1,0:T(8,128)S(1)}, u32[]{:S(2)}, u32[]{:S(2)}) collective-permute-start(f32[2,128,256]{2,1,0:T(8,128)} %param.4), channel_id=1, source_target_pairs={{0,192},{1,200},{2,208},{3,216},{4,193},{5,201},{6,209},{7,217},{8... | collective-permute-start | bytes 786440 | tf_op jit(solution)/shard_map/ppermute | solution.py:79
  12.0 1.3 %collective-permute-start.1 = (f32[2,128,256]{2,1,0:T(8,128)}, f32[2,128,256]{2,1,0:T(8,128)S(1)}, u32[]{:S(2)}, u32[]{:S(2)}) collective-permute-start(f32[2,128,256]{2,1,0:T(8,128)} %param.4), channel_id=1, source_target_pairs={{0,64},{1,72},{2,80},{3,88},{4,65},{5,73},{6,81},{7,89},{8,66},{9,... | collective-permute-start | bytes 786440 | tf_op jit(solution)/shard_map/ppermute | solution.py:79
  13.4 4.1 %collective-permute-start.2 = (f32[2,128,256]{2,1,0:T(8,128)}, f32[2,128,256]{2,1,0:T(8,128)S(1)}, u32[]{:S(2)}, u32[]{:S(2)}) collective-permute-start(f32[2,128,256]{2,1,0:T(8,128)} %param.4), channel_id=1, source_target_pairs={{0,0},{1,8},{2,16},{3,24},{4,1},{5,9},{6,17},{7,25},{8,2},{9,10},{... | collective-permute-start | bytes 786440 | tf_op jit(solution)/shard_map/ppermute | solution.py:79
  17.5 0.0 all-gather.2.cloned.1.call-update
  17.5 23.4 %collective-permute-done = f32[2,128,256]{2,1,0:T(8,128)S(1)} collective-permute-done((f32[2,128,256]{2,1,0:T(8,128)}, f32[2,128,256]{2,1,0:T(8,128)S(1)}, u32[]{:S(2)}, u32[]{:S(2)}) %collective-permute-start) | collective-permute-done | bytes 262176 | tf_op jit(solution)/shard_map/ppermute | solution.py:79
  40.9 9.4 %collective-permute-done.1 = f32[2,128,256]{2,1,0:T(8,128)S(1)} collective-permute-done((f32[2,128,256]{2,1,0:T(8,128)}, f32[2,128,256]{2,1,0:T(8,128)S(1)}, u32[]{:S(2)}, u32[]{:S(2)}) %collective-permute-start.1) | collective-permute-done | bytes 262176 | tf_op jit(solution)/shard_map/ppermute | solution.py:79
  50.4 8.9 %collective-permute-done.2 = f32[2,128,256]{2,1,0:T(8,128)S(1)} collective-permute-done((f32[2,128,256]{2,1,0:T(8,128)}, f32[2,128,256]{2,1,0:T(8,128)S(1)}, u32[]{:S(2)}, u32[]{:S(2)}) %collective-permute-start.2) | collective-permute-done | bytes 262176 | tf_op jit(solution)/shard_map/ppermute | solution.py:79
  59.3 0.7 collective-permute-start.3
  60.0 0.7 collective-permute-start.4
  60.7 0.0 collective-permute-done.3
  60.7 0.0 collective-permute-done.4
  60.7 0.1 fusion.9
  60.7 0.7 collective-permute-start.5
  61.4 1.3 %fusion.12 = f32[128,256]{1,0:T(8,128)S(1)} fusion(f32[2,256,256]{2,1,0:T(8,128)} %param.5, f32[2,128,256]{2,1,0:T(8,128)} %param.4), kind=kOutput, calls=%fused_computation.26 | convolution fusion | flops 100663296 | bytes 524288 | tf_op jit(solution)/shard_map/dot_general | solution.py:14
  62.8 1.3 %fusion.18 = f32[128,256]{1,0:T(8,128)S(1)} fusion(f32[2,256,256]{2,1,0:T(8,128)} %param.5, f32[2,128,256]{2,1,0:T(8,128)} %param.4), kind=kOutput, calls=%fused_computation.32 | convolution fusion | flops 100663296 | bytes 524288 | tf_op jit(solution)/shard_map/dot_general | solution.py:13
  64.1 0.0 collective-permute-done.5
  64.1 26.3 %collective-permute-start.6 = (f32[2,128,256]{2,1,0:T(8,128)S(1)}, f32[2,128,256]{2,1,0:T(8,128)S(1)}, u32[]{:S(2)}, u32[]{:S(2)}) collective-permute-start(f32[2,128,256]{2,1,0:T(8,128)S(1)} %select_select_fusion), channel_id=1, source_target_pairs={{0,24},{8,0},{16,8},{24,16},{1,25},{9,1},{17,9},{25,17},{2,26},{10... | collective-permute-start | bytes 786440 | tf_op jit(solution)/shard_map/ppermute | solution.py:66
  90.4 0.0 collective-permute-start.7
  90.4 0.7 collective-permute-start.8
  91.1 0.0 copy-done.1
  91.1 0.0 copy-done
  91.1 0.3 fusion.5
  91.5 5.4 %copy.5 = f32[2,1024,512]{1,2,0:T(8,128)} copy(f32[2,1024,512]{2,1,0:T(8,128)} %param.3) | data formatting | bytes 8388608 | tf_op args[0]
  96.8 0.3 fusion.6
  97.1 0.7 pad_maximum_fusion.1
  97.9 4.3 %collective-permute-done.6 = f32[2,128,256]{2,1,0:T(8,128)S(1)} collective-permute-done((f32[2,128,256]{2,1,0:T(8,128)S(1)}, f32[2,128,256]{2,1,0:T(8,128)S(1)}, u32[]{:S(2)}, u32[]{:S(2)}) %collective-permute-start.6) | collective-permute-done | bytes 262176 | tf_op jit(solution)/shard_map/ppermute | solution.py:66
  102.2 0.0 collective-permute-done.7
  102.2 3.1 %collective-permute-done.8 = f32[2,128,256]{2,1,0:T(8,128)S(1)} collective-permute-done((f32[2,128,256]{2,1,0:T(8,128)S(1)}, f32[2,128,256]{2,1,0:T(8,128)S(1)}, u32[]{:S(2)}, u32[]{:S(2)}) %collective-permute-start.8) | collective-permute-done | bytes 262176 | tf_op jit(solution)/shard_map/ppermute | solution.py:66
  105.3 0.1 select_select_fusion.5
  105.4 0.1 pad_maximum_fusion
  105.5 0.4 fusion.8
  105.9 0.4 fusion.4
  106.3 0.4 fusion.7
  106.7 0.4 convolution_add_fusion
  107.1 0.2 maximum_bitcast_fusion
  107.3 0.0 all-gather.2.cloned.1.call-done
  107.3 7.0 %bitcast_subtract_fusion = f32[2,1024,512]{1,2,0:T(8,128)} fusion(f32[2,1024,512]{1,2,0:T(8,128)} %copy.5, f32[1,2,512,256]{3,2,1,0:T(8,128)S(1)} %get-tuple-element.9, f32[1,2,512,256]{3,2,1,0:T(8,128)S(1)} %get-tuple-element.8, f32[2,1024,256]{2,1,0:T(8,128)} %all-gather.2.cloned.1.call-done), kind=kOutput, calls=%fused_computation | convolution fusion | flops 3222798336 | bytes 12582912 | tf_op jit(solution)/shard_map/dot_general | solution.py:97
  114.3 5.4 %copy.6 = f32[2,1024,512]{2,1,0:T(8,128)} copy(f32[2,1024,512]{1,2,0:T(8,128)} %bitcast_subtract_fusion) | data formatting | bytes 8388608
  (3 shorter events, 0.1 us)
Async XLA Ops:
  7.2 83.9 %copy-start.1 = (f32[2,128,256]{2,1,0:T(8,128)S(1)}, f32[2,128,256]{2,1,0:T(8,128)}, u32[]{:S(2)}) copy-start(f32[2,128,256]{2,1,0:T(8,128)} %param.4) | copy-start | bytes 786436
  7.2 83.9 %copy-start = (f32[2,256,256]{2,1,0:T(8,128)S(1)}, f32[2,256,256]{2,1,0:T(8,128)}, u32[]{:S(2)}) copy-start(f32[2,256,256]{2,1,0:T(8,128)} %param.5) | copy-start | bytes 1572868
  7.2 100.1 %all-gather.2.cloned.1.call-start = ((), (), s32[]{:S(2)}) async-start(), calls=%async_computation | async-start | bytes 2359296 | tf_op jit(solution)/shard_map/all_gather | solution.py:71
  7.2 33.7 %collective-permute-start = (f32[2,128,256]{2,1,0:T(8,128)}, f32[2,128,256]{2,1,0:T(8,128)S(1)}, u32[]{:S(2)}, u32[]{:S(2)}) collective-permute-start(f32[2,128,256]{2,1,0:T(8,128)} %param.4), channel_id=1, source_target_pairs={{0,192},{1,200},{2,208},{3,216},{4,193},{5,201},{6,209},{7,217},{8... | collective-permute-start | bytes 786440 | tf_op jit(solution)/shard_map/ppermute | solution.py:79
  12.0 38.3 %collective-permute-start.1 = (f32[2,128,256]{2,1,0:T(8,128)}, f32[2,128,256]{2,1,0:T(8,128)S(1)}, u32[]{:S(2)}, u32[]{:S(2)}) collective-permute-start(f32[2,128,256]{2,1,0:T(8,128)} %param.4), channel_id=1, source_target_pairs={{0,64},{1,72},{2,80},{3,88},{4,65},{5,73},{6,81},{7,89},{8,66},{9,... | collective-permute-start | bytes 786440 | tf_op jit(solution)/shard_map/ppermute | solution.py:79
  13.4 45.9 %collective-permute-start.2 = (f32[2,128,256]{2,1,0:T(8,128)}, f32[2,128,256]{2,1,0:T(8,128)S(1)}, u32[]{:S(2)}, u32[]{:S(2)}) collective-permute-start(f32[2,128,256]{2,1,0:T(8,128)} %param.4), channel_id=1, source_target_pairs={{0,0},{1,8},{2,16},{3,24},{4,1},{5,9},{6,17},{7,25},{8,2},{9,10},{... | collective-permute-start | bytes 786440 | tf_op jit(solution)/shard_map/ppermute | solution.py:79
  59.3 1.4 %collective-permute-start.3 = (f32[2,128,256]{2,1,0:T(8,128)S(1)}, f32[2,128,256]{2,1,0:T(8,128)S(1)}, u32[]{:S(2)}, u32[]{:S(2)}) collective-permute-start(f32[2,128,256]{2,1,0:T(8,128)S(1)} %select_select_fusion.6), channel_id=1, source_target_pairs={{64,96},{65,97},{66,98},{67,99},{68,100},{69,101},{70,102},{71,103... | collective-permute-start | bytes 786440 | tf_op jit(solution)/shard_map/ppermute | solution.py:87
  60.0 0.7 collective-permute-start.4
  60.7 3.3 %collective-permute-start.5 = (f32[2,128,256]{2,1,0:T(8,128)S(1)}, f32[2,128,256]{2,1,0:T(8,128)S(1)}, u32[]{:S(2)}, u32[]{:S(2)}) collective-permute-start(f32[2,128,256]{2,1,0:T(8,128)S(1)} %fusion.9), channel_id=1, source_target_pairs={{96,160},{224,32},{97,161},{225,33},{98,162},{226,34},{99,163},{22... | collective-permute-start | bytes 786440 | tf_op jit(solution)/shard_map/ppermute | solution.py:87
  64.1 38.1 %collective-permute-start.6 = (f32[2,128,256]{2,1,0:T(8,128)S(1)}, f32[2,128,256]{2,1,0:T(8,128)S(1)}, u32[]{:S(2)}, u32[]{:S(2)}) collective-permute-start(f32[2,128,256]{2,1,0:T(8,128)S(1)} %select_select_fusion), channel_id=1, source_target_pairs={{0,24},{8,0},{16,8},{24,16},{1,25},{9,1},{17,9},{25,17},{2,26},{10... | collective-permute-start | bytes 786440 | tf_op jit(solution)/shard_map/ppermute | solution.py:66
  90.4 11.7 %collective-permute-start.7 = (f32[2,128,256]{2,1,0:T(8,128)S(1)}, f32[2,128,256]{2,1,0:T(8,128)S(1)}, u32[]{:S(2)}, u32[]{:S(2)}) collective-permute-start(f32[2,128,256]{2,1,0:T(8,128)S(1)} %select_select_fusion), channel_id=1, source_target_pairs={{0,16},{8,24},{16,0},{24,8},{1,17},{9,25},{17,1},{25,9},{2,18},{10... | collective-permute-start | bytes 786440 | tf_op jit(solution)/shard_map/ppermute | solution.py:66
  90.4 14.9 %collective-permute-start.8 = (f32[2,128,256]{2,1,0:T(8,128)S(1)}, f32[2,128,256]{2,1,0:T(8,128)S(1)}, u32[]{:S(2)}, u32[]{:S(2)}) collective-permute-start(f32[2,128,256]{2,1,0:T(8,128)S(1)} %select_select_fusion), channel_id=1, source_target_pairs={{0,8},{8,16},{16,24},{24,0},{1,9},{9,17},{17,25},{25,1},{2,10},{10... | collective-permute-start | bytes 786440 | tf_op jit(solution)/shard_map/ppermute | solution.py:66
Sparse Core Ops, SparseCore 0:
  17.6 59.1 all-gather.1

commit v7 on v5

--- a/solution.py
+++ b/solution.py
@@ -66,6 +66,20 @@
         got = [piece] + [lax.ppermute(piece, axis, shifts(n, k)) for k in range(1, n)]
         return reorder(got, idx, n)
 
+    def line_gather(piece, axis, idx, n):
+        from_left, from_right = [piece], [piece]
+        for d in range(1, n):
+            from_left.append(lax.ppermute(from_left[-1], axis, [(i, i + 1) for i in range(d - 1, n - 1)]))
+            from_right.append(lax.ppermute(from_right[-1], axis, [(i + 1, i) for i in range(0, n - d)]))
+        out = []
+        for j in range(n):
+            val = piece
+            for d in range(1, n):
+                val = jnp.where(idx - j == d, from_left[d], val)
+                val = jnp.where(j - idx == d, from_right[d], val)
+            out.append(val)
+        return jnp.concatenate(out, axis=1)
+
     def local(trailing, panel, diag_inverse):
         scaled = complex_product(panel, diag_inverse)
 
@@ -89,7 +103,7 @@
         panel_late, held = lax.optimization_barrier((panel, held))
         window = gather(held, "x", xi, nx)
 
-        mine = gather(panel_late, "zl", li, nl)
+        mine = line_gather(panel_late, "zl", li, nl)
         other = lax.ppermute(mine, "core", shifts(nc, 1))
         lo = jnp.where(ci == 0, mine, other)
         hi_ = jnp.where(ci == 0, other, mine)

time: 102 us -> 109 us (1.069); the launches traced: 102 us -> 107 us
  waiting for transfers between devices: 29.8 us -> 38.3 us
  starting transfers between devices: 59.1 us -> 55.9 us
    ppermute x6 -> x3, starting transfers between devices: 42.9 us -> 16.8 us  [gather(): lax.ppermute(piece, axis, shifts(n, k))]
    ppermute x0 -> x6, starting transfers between devices: none -> 22.9 us  [the longest x3 19.1 us: line_gather(): lax.ppermute(from_left[-1], axis, [(i, i + 1) for i in range(d - 1, n - 1)])]
    ppermute x0 -> x6, waiting for transfers between devices: none -> 21.4 us  [the longest x3 21.4 us: line_gather(): lax.ppermute(from_right[-1], axis, [(i + 1, i) for i in range(0, n - d)])]
    ppermute x6 -> x3, waiting for transfers between devices: 15.4 us -> 1.92 us  [gather(): lax.ppermute(piece, axis, shifts(n, k))]
  transfers between devices with their start and end apart: 13 -> 16, of which waited for: 5 -> 8; matrix products, arithmetic and copies ran while one was open for 4% -> 4% of each run, Pallas kernels for 0% -> 0%
where the time goes in v7:
time: 109 us; the launch traced here: 107 us
  starting transfers between devices  55.9 us (51%)
  waiting for transfers between devices  38.3 us (35%)
  matrix products  7.7 us (7%)
  local copies, waits for them, and re-layouts  1.98 us (2%)
  other arithmetic  1.94 us (2%)
  between operations  1.16 us (1%)
    ppermute x3, waiting for transfers between devices, line_gather(): lax.ppermute(from_right[-1], axis, [(i + 1, i) for i in range(0, n - d)])  21.4 us
    ppermute x3, starting transfers between devices, line_gather(): lax.ppermute(from_left[-1], axis, [(i, i + 1) for i in range(d - 1, n - 1)])  19.1 us
    ppermute x3, starting transfers between devices, gather(): lax.ppermute(piece, axis, shifts(n, k))  16.8 us
    ppermute x3, waiting for transfers between devices, local(): got_a = [lax.ppermute(panel, AXES, spread(y1, h1)) for y1, h1 in first]  14.1 us
    ppermute x3, starting transfers between devices, local(): got_a = [lax.ppermute(panel, AXES, spread(y1, h1)) for y1, h1 in first]  13.5 us
    dot_general x1, matrix products, local(): product = lax.dot_general(lhs, rhs, dims, precision=lax.Precision.HIGH)  5.06 us
    ppermute x3, starting transfers between devices, line_gather(): lax.ppermute(from_right[-1], axis, [(i + 1, i) for i in range(0, n - d)])  3.85 us
  transfers between devices with their start and end apart: 16, of which 8 were waited for; matrix products, arithmetic and copies ran while one was open for 4% of the time, Pallas kernels for 0%

profile of v7, /device:TPU:7, one launch (start us, length us, event | category | flops | bytes accessed | tf_op | source)
XLA Modules:
  0.0 107.0 jit_solution(10709585799076736338)
XLA Ops:
  0.6 0.0 copy-start.2
  0.6 0.0 copy-start
  0.6 10.2 %collective-permute-start = (f32[2,128,256]{2,1,0:T(8,128)}, f32[2,128,256]{2,1,0:T(8,128)S(1)}, u32[]{:S(2)}, u32[]{:S(2)}) collective-permute-start(f32[2,128,256]{2,1,0:T(8,128)} %param.4), channel_id=1, source_target_pairs={{0,192},{1,200},{2,208},{3,216},{4,193},{5,201},{6,209},{7,217},{8... | collective-permute-start | bytes 786440 | tf_op jit(solution)/shard_map/ppermute | solution.py:92
  10.9 1.3 %collective-permute-start.1 = (f32[2,128,256]{2,1,0:T(8,128)}, f32[2,128,256]{2,1,0:T(8,128)S(1)}, u32[]{:S(2)}, u32[]{:S(2)}) collective-permute-start(f32[2,128,256]{2,1,0:T(8,128)} %param.4), channel_id=1, source_target_pairs={{0,64},{1,72},{2,80},{3,88},{4,65},{5,73},{6,81},{7,89},{8,66},{9,... | collective-permute-start | bytes 786440 | tf_op jit(solution)/shard_map/ppermute | solution.py:92
  12.2 1.9 %collective-permute-start.2 = (f32[2,128,256]{2,1,0:T(8,128)}, f32[2,128,256]{2,1,0:T(8,128)S(1)}, u32[]{:S(2)}, u32[]{:S(2)}) collective-permute-start(f32[2,128,256]{2,1,0:T(8,128)} %param.4), channel_id=1, source_target_pairs={{0,0},{1,8},{2,16},{3,24},{4,1},{5,9},{6,17},{7,25},{8,2},{9,10},{... | collective-permute-start | bytes 786440 | tf_op jit(solution)/shard_map/ppermute | solution.py:92
  14.2 3.2 %collective-permute-done = f32[2,128,256]{2,1,0:T(8,128)S(1)} collective-permute-done((f32[2,128,256]{2,1,0:T(8,128)}, f32[2,128,256]{2,1,0:T(8,128)S(1)}, u32[]{:S(2)}, u32[]{:S(2)}) %collective-permute-start) | collective-permute-done | bytes 262176 | tf_op jit(solution)/shard_map/ppermute | solution.py:92
  17.4 5.6 %collective-permute-done.1 = f32[2,128,256]{2,1,0:T(8,128)S(1)} collective-permute-done((f32[2,128,256]{2,1,0:T(8,128)}, f32[2,128,256]{2,1,0:T(8,128)S(1)}, u32[]{:S(2)}, u32[]{:S(2)}) %collective-permute-start.1) | collective-permute-done | bytes 262176 | tf_op jit(solution)/shard_map/ppermute | solution.py:92
  23.0 5.3 %collective-permute-done.2 = f32[2,128,256]{2,1,0:T(8,128)S(1)} collective-permute-done((f32[2,128,256]{2,1,0:T(8,128)}, f32[2,128,256]{2,1,0:T(8,128)S(1)}, u32[]{:S(2)}, u32[]{:S(2)}) %collective-permute-start.2) | collective-permute-done | bytes 262176 | tf_op jit(solution)/shard_map/ppermute | solution.py:92
  28.3 0.7 collective-permute-start.3
  29.0 0.7 collective-permute-start.4
  29.7 0.0 collective-permute-done.3
  29.7 0.0 collective-permute-done.4
  29.7 0.1 fusion.9
  29.8 0.7 collective-permute-start.5
  30.5 0.0 copy-done.2
  30.5 0.0 copy-done
  30.5 0.3 fusion.12
  30.8 0.3 fusion.18
  31.1 0.0 collective-permute-done.5
  31.1 17.7 %collective-permute-start.9 = (f32[2,128,256]{2,1,0:T(8,128)S(1)}, f32[2,128,256]{2,1,0:T(8,128)S(1)}, u32[]{:S(2)}, u32[]{:S(2)}) collective-permute-start(f32[2,128,256]{2,1,0:T(8,128)S(1)} %copy-done.2), channel_id=1, source_target_pairs={{0,2},{2,4},{4,6},{1,3},{3,5},{5,7},{8,10},{10,12},{12,14},{9,11},... | collective-permute-start | bytes 786440 | tf_op jit(solution)/shard_map/ppermute | solution.py:72
  48.8 1.3 %collective-permute-start.6 = (f32[2,128,256]{2,1,0:T(8,128)S(1)}, f32[2,128,256]{2,1,0:T(8,128)S(1)}, u32[]{:S(2)}, u32[]{:S(2)}) collective-permute-start(f32[2,128,256]{2,1,0:T(8,128)S(1)} %copy-done.2), channel_id=1, source_target_pairs={{2,0},{4,2},{6,4},{3,1},{5,3},{7,5},{10,8},{12,10},{14,12},{11,9},... | collective-permute-start | bytes 786440 | tf_op jit(solution)/shard_map/ppermute | solution.py:73
  50.1 0.7 collective-permute-start.13
  50.9 16.1 %collective-permute-start.14 = (f32[2,128,256]{2,1,0:T(8,128)S(1)}, f32[2,128,256]{2,1,0:T(8,128)S(1)}, u32[]{:S(2)}, u32[]{:S(2)}) collective-permute-start(f32[2,128,256]{2,1,0:T(8,128)S(1)} %select_select_fusion), channel_id=1, source_target_pairs={{0,16},{8,24},{16,0},{24,8},{1,17},{9,25},{17,1},{25,9},{2,18},{10... | collective-permute-start | bytes 786440 | tf_op jit(solution)/shard_map/ppermute | solution.py:66
  66.9 0.0 collective-permute-start.15
  66.9 0.3 fusion.5
  67.4 0.3 fusion.6
  67.7 0.7 pad_maximum_fusion.3
  68.4 0.0 collective-permute-done.9
  68.4 0.7 collective-permute-start.10
  69.0 5.9 %collective-permute-done.6 = f32[2,128,256]{2,1,0:T(8,128)S(1)} collective-permute-done((f32[2,128,256]{2,1,0:T(8,128)S(1)}, f32[2,128,256]{2,1,0:T(8,128)S(1)}, u32[]{:S(2)}, u32[]{:S(2)}) %collective-permute-start.6) | collective-permute-done | bytes 262176 | tf_op jit(solution)/shard_map/ppermute | solution.py:73
  75.0 1.3 %collective-permute-start.7 = (f32[2,128,256]{2,1,0:T(8,128)S(1)}, f32[2,128,256]{2,1,0:T(8,128)S(1)}, u32[]{:S(2)}, u32[]{:S(2)}) collective-permute-start(f32[2,128,256]{2,1,0:T(8,128)S(1)} %collective-permute-done.6), channel_id=1, source_target_pairs={{2,0},{4,2},{3,1},{5,3},{10,8},{12,10},{11,9},{13,11},{18,16},{20,... | collective-permute-start | bytes 786440 | tf_op jit(solution)/shard_map/ppermute | solution.py:73
  76.3 0.0 collective-permute-done.13
  76.3 1.9 %collective-permute-done.14 = f32[2,128,256]{2,1,0:T(8,128)S(1)} collective-permute-done((f32[2,128,256]{2,1,0:T(8,128)S(1)}, f32[2,128,256]{2,1,0:T(8,128)S(1)}, u32[]{:S(2)}, u32[]{:S(2)}) %collective-permute-start.14) | collective-permute-done | bytes 262176 | tf_op jit(solution)/shard_map/ppermute | solution.py:66
  78.2 0.0 collective-permute-done.15
  78.2 0.1 select_select_fusion.5
  78.3 0.0 collective-permute-done.10
  78.3 0.7 collective-permute-start.11
  79.0 7.3 %collective-permute-done.7 = f32[2,128,256]{2,1,0:T(8,128)S(1)} collective-permute-done((f32[2,128,256]{2,1,0:T(8,128)S(1)}, f32[2,128,256]{2,1,0:T(8,128)S(1)}, u32[]{:S(2)}, u32[]{:S(2)}) %collective-permute-start.7) | collective-permute-done | bytes 262176 | tf_op jit(solution)/shard_map/ppermute | solution.py:73
  86.3 1.3 %collective-permute-start.8 = (f32[2,128,256]{2,1,0:T(8,128)S(1)}, f32[2,128,256]{2,1,0:T(8,128)S(1)}, u32[]{:S(2)}, u32[]{:S(2)}) collective-permute-start(f32[2,128,256]{2,1,0:T(8,128)S(1)} %collective-permute-done.7), channel_id=1, source_target_pairs={{2,0},{3,1},{10,8},{11,9},{18,16},{19,17},{26,24},{27,25},{34,32},... | collective-permute-start | bytes 786440 | tf_op jit(solution)/shard_map/ppermute | solution.py:73
  87.6 0.1 pad_maximum_fusion.2
  87.7 0.4 fusion.8
  88.1 0.0 collective-permute-done.11
  88.1 8.2 %collective-permute-done.8 = f32[2,128,256]{2,1,0:T(8,128)S(1)} collective-permute-done((f32[2,128,256]{2,1,0:T(8,128)S(1)}, f32[2,128,256]{2,1,0:T(8,128)S(1)}, u32[]{:S(2)}, u32[]{:S(2)}) %collective-permute-start.8) | collective-permute-done | bytes 262176 | tf_op jit(solution)/shard_map/ppermute | solution.py:73
  96.3 0.1 select_select_fusion.8
  96.4 0.1 select_select_fusion.9
  96.5 0.1 pad_maximum_fusion.1
  96.6 0.7 collective-permute-start.12
  97.3 0.4 fusion.4
  97.7 0.4 fusion.7
  98.1 0.4 convolution_add_fusion
  98.5 0.2 maximum_bitcast_fusion
  98.7 0.9 collective-permute-done.12
  99.6 0.2 broadcast_select_fusion.1
  99.8 0.0 copy-start.1
  99.8 0.2 pad_maximum_fusion
  100.0 2.0 %copy-done.1 = f32[2,1024,512]{2,1,0:T(8,128)S(1)} copy-done((f32[2,1024,512]{2,1,0:T(8,128)S(1)}, f32[2,1024,512]{2,1,0:T(8,128)}, u32[]{:S(2)}) %copy-start.1) | copy-done | bytes 4194328
  102.0 5.1 %bitcast_subtract_fusion = f32[2,1024,512]{2,1,0:T(8,128)} fusion(f32[2,1024,512]{2,1,0:T(8,128)S(1)} %copy-done.1, f32[1,2,512,256]{3,2,1,0:T(8,128)S(1)} %get-tuple-element.17, f32[1,2,512,256]{3,2,1,0:T(8,128)S(1)} %get-tuple-element.16, f32[2,1024,256]{2,1,0:T(8,128)S(1)} %bitcast.55), kind=kOutput, calls=%fused_computation | convolution fusion | flops 3222798336 | bytes 12582912 | tf_op jit(solution)/shard_map/dot_general | solution.py:119
  (3 shorter events, 0.1 us)
Async XLA Ops:
  0.6 29.8 %copy-start.2 = (f32[2,128,256]{2,1,0:T(8,128)S(1)}, f32[2,128,256]{2,1,0:T(8,128)}, u32[]{:S(2)}) copy-start(f32[2,128,256]{2,1,0:T(8,128)} %param.4) | copy-start | bytes 786436
  0.6 29.8 %copy-start = (f32[2,256,256]{2,1,0:T(8,128)S(1)}, f32[2,256,256]{2,1,0:T(8,128)}, u32[]{:S(2)}) copy-start(f32[2,256,256]{2,1,0:T(8,128)} %param.5) | copy-start | bytes 1572868
  0.6 16.7 %collective-permute-start = (f32[2,128,256]{2,1,0:T(8,128)}, f32[2,128,256]{2,1,0:T(8,128)S(1)}, u32[]{:S(2)}, u32[]{:S(2)}) collective-permute-start(f32[2,128,256]{2,1,0:T(8,128)} %param.4), channel_id=1, source_target_pairs={{0,192},{1,200},{2,208},{3,216},{4,193},{5,201},{6,209},{7,217},{8... | collective-permute-start | bytes 786440 | tf_op jit(solution)/shard_map/ppermute | solution.py:92
  10.9 12.1 %collective-permute-start.1 = (f32[2,128,256]{2,1,0:T(8,128)}, f32[2,128,256]{2,1,0:T(8,128)S(1)}, u32[]{:S(2)}, u32[]{:S(2)}) collective-permute-start(f32[2,128,256]{2,1,0:T(8,128)} %param.4), channel_id=1, source_target_pairs={{0,64},{1,72},{2,80},{3,88},{4,65},{5,73},{6,81},{7,89},{8,66},{9,... | collective-permute-start | bytes 786440 | tf_op jit(solution)/shard_map/ppermute | solution.py:92
  12.2 16.0 %collective-permute-start.2 = (f32[2,128,256]{2,1,0:T(8,128)}, f32[2,128,256]{2,1,0:T(8,128)S(1)}, u32[]{:S(2)}, u32[]{:S(2)}) collective-permute-start(f32[2,128,256]{2,1,0:T(8,128)} %param.4), channel_id=1, source_target_pairs={{0,0},{1,8},{2,16},{3,24},{4,1},{5,9},{6,17},{7,25},{8,2},{9,10},{... | collective-permute-start | bytes 786440 | tf_op jit(solution)/shard_map/ppermute | solution.py:92
  28.3 1.4 %collective-permute-start.3 = (f32[2,128,256]{2,1,0:T(8,128)S(1)}, f32[2,128,256]{2,1,0:T(8,128)S(1)}, u32[]{:S(2)}, u32[]{:S(2)}) collective-permute-start(f32[2,128,256]{2,1,0:T(8,128)S(1)} %select_select_fusion.10), channel_id=1, source_target_pairs={{64,96},{65,97},{66,98},{67,99},{68,100},{69,101},{70,102},{71,103... | collective-permute-start | bytes 786440 | tf_op jit(solution)/shard_map/ppermute | solution.py:100
  29.0 0.7 collective-permute-start.4
  29.8 1.3 %collective-permute-start.5 = (f32[2,128,256]{2,1,0:T(8,128)S(1)}, f32[2,128,256]{2,1,0:T(8,128)S(1)}, u32[]{:S(2)}, u32[]{:S(2)}) collective-permute-start(f32[2,128,256]{2,1,0:T(8,128)S(1)} %fusion.9), channel_id=1, source_target_pairs={{96,160},{224,32},{97,161},{225,33},{98,162},{226,34},{99,163},{22... | collective-permute-start | bytes 786440 | tf_op jit(solution)/shard_map/ppermute | solution.py:100
  31.1 37.3 %collective-permute-start.9 = (f32[2,128,256]{2,1,0:T(8,128)S(1)}, f32[2,128,256]{2,1,0:T(8,128)S(1)}, u32[]{:S(2)}, u32[]{:S(2)}) collective-permute-start(f32[2,128,256]{2,1,0:T(8,128)S(1)} %copy-done.2), channel_id=1, source_target_pairs={{0,2},{2,4},{4,6},{1,3},{3,5},{5,7},{8,10},{10,12},{12,14},{9,11},... | collective-permute-start | bytes 786440 | tf_op jit(solution)/shard_map/ppermute | solution.py:72
  48.8 26.1 %collective-permute-start.6 = (f32[2,128,256]{2,1,0:T(8,128)S(1)}, f32[2,128,256]{2,1,0:T(8,128)S(1)}, u32[]{:S(2)}, u32[]{:S(2)}) collective-permute-start(f32[2,128,256]{2,1,0:T(8,128)S(1)} %copy-done.2), channel_id=1, source_target_pairs={{2,0},{4,2},{6,4},{3,1},{5,3},{7,5},{10,8},{12,10},{14,12},{11,9},... | collective-permute-start | bytes 786440 | tf_op jit(solution)/shard_map/ppermute | solution.py:73
  50.1 26.1 %collective-permute-start.13 = (f32[2,128,256]{2,1,0:T(8,128)S(1)}, f32[2,128,256]{2,1,0:T(8,128)S(1)}, u32[]{:S(2)}, u32[]{:S(2)}) collective-permute-start(f32[2,128,256]{2,1,0:T(8,128)S(1)} %select_select_fusion), channel_id=1, source_target_pairs={{0,24},{8,0},{16,8},{24,16},{1,25},{9,1},{17,9},{25,17},{2,26},{10... | collective-permute-start | bytes 786440 | tf_op jit(solution)/shard_map/ppermute | solution.py:66
  50.9 27.3 %collective-permute-start.14 = (f32[2,128,256]{2,1,0:T(8,128)S(1)}, f32[2,128,256]{2,1,0:T(8,128)S(1)}, u32[]{:S(2)}, u32[]{:S(2)}) collective-permute-start(f32[2,128,256]{2,1,0:T(8,128)S(1)} %select_select_fusion), channel_id=1, source_target_pairs={{0,16},{8,24},{16,0},{24,8},{1,17},{9,25},{17,1},{25,9},{2,18},{10... | collective-permute-start | bytes 786440 | tf_op jit(solution)/shard_map/ppermute | solution.py:66
  66.9 11.3 %collective-permute-start.15 = (f32[2,128,256]{2,1,0:T(8,128)S(1)}, f32[2,128,256]{2,1,0:T(8,128)S(1)}, u32[]{:S(2)}, u32[]{:S(2)}) collective-permute-start(f32[2,128,256]{2,1,0:T(8,128)S(1)} %select_select_fusion), channel_id=1, source_target_pairs={{0,8},{8,16},{16,24},{24,0},{1,9},{9,17},{17,25},{25,1},{2,10},{10... | collective-permute-start | bytes 786440 | tf_op jit(solution)/shard_map/ppermute | solution.py:66
  68.4 9.9 %collective-permute-start.10 = (f32[2,128,256]{2,1,0:T(8,128)S(1)}, f32[2,128,256]{2,1,0:T(8,128)S(1)}, u32[]{:S(2)}, u32[]{:S(2)}) collective-permute-start(f32[2,128,256]{2,1,0:T(8,128)S(1)} %collective-permute-done.9), channel_id=1, source_target_pairs={{2,4},{4,6},{3,5},{5,7},{10,12},{12,14},{11,13},{13,15},{18,20},{2... | collective-permute-start | bytes 786440 | tf_op jit(solution)/shard_map/ppermute | solution.py:72
  75.0 11.3 %collective-permute-start.7 = (f32[2,128,256]{2,1,0:T(8,128)S(1)}, f32[2,128,256]{2,1,0:T(8,128)S(1)}, u32[]{:S(2)}, u32[]{:S(2)}) collective-permute-start(f32[2,128,256]{2,1,0:T(8,128)S(1)} %collective-permute-done.6), channel_id=1, source_target_pairs={{2,0},{4,2},{3,1},{5,3},{10,8},{12,10},{11,9},{13,11},{18,16},{20,... | collective-permute-start | bytes 786440 | tf_op jit(solution)/shard_map/ppermute | solution.py:73
  78.3 9.7 %collective-permute-start.11 = (f32[2,128,256]{2,1,0:T(8,128)S(1)}, f32[2,128,256]{2,1,0:T(8,128)S(1)}, u32[]{:S(2)}, u32[]{:S(2)}) collective-permute-start(f32[2,128,256]{2,1,0:T(8,128)S(1)} %collective-permute-done.10), channel_id=1, source_target_pairs={{4,6},{5,7},{12,14},{13,15},{20,22},{21,23},{28,30},{29,31},{36,38... | collective-permute-start | bytes 786440 | tf_op jit(solution)/shard_map/ppermute | solution.py:72
  86.3 10.0 %collective-permute-start.8 = (f32[2,128,256]{2,1,0:T(8,128)S(1)}, f32[2,128,256]{2,1,0:T(8,128)S(1)}, u32[]{:S(2)}, u32[]{:S(2)}) collective-permute-start(f32[2,128,256]{2,1,0:T(8,128)S(1)} %collective-permute-done.7), channel_id=1, source_target_pairs={{2,0},{3,1},{10,8},{11,9},{18,16},{19,17},{26,24},{27,25},{34,32},... | collective-permute-start | bytes 786440 | tf_op jit(solution)/shard_map/ppermute | solution.py:73
  96.6 3.0 %collective-permute-start.12 = (f32[2,512,256]{2,1,0:T(8,128)S(1)}, f32[2,512,256]{2,1,0:T(8,128)S(1)}, u32[]{:S(2)}, u32[]{:S(2)}) collective-permute-start(f32[2,512,256]{2,1,0:T(8,128)S(1)} %pad_maximum_fusion.1), channel_id=1, source_target_pairs={{0,1},{1,0},{2,3},{3,2},{4,5},{5,4},{6,7},{7,6},{8,9},{9,8},{10,11... | collective-permute-start | bytes 3145736 | tf_op jit(solution)/shard_map/ppermute | solution.py:107
  99.8 2.2 %copy-start.1 = (f32[2,1024,512]{2,1,0:T(8,128)S(1)}, f32[2,1024,512]{2,1,0:T(8,128)}, u32[]{:S(2)}) copy-start(f32[2,1024,512]{2,1,0:T(8,128)} %param.3) | copy-start | bytes 12582916

commit v8 on v5

--- a/solution.py
+++ b/solution.py
@@ -86,10 +86,9 @@
                 got = lax.ppermute(sent, ("y", "zh"), [(plane(h0, y0), plane(h1, y1)) for (y0, h0), (y1, h1) in pairs])
                 for _, (y1, h1) in pairs:
                     held = jnp.where((yi == y1) & (hi == h1), got, held)
-        panel_late, held = lax.optimization_barrier((panel, held))
         window = gather(held, "x", xi, nx)
 
-        mine = gather(panel_late, "zl", li, nl)
+        mine = gather(panel, "zl", li, nl)
         other = lax.ppermute(mine, "core", shifts(nc, 1))
         lo = jnp.where(ci == 0, mine, other)
         hi_ = jnp.where(ci == 0, other, mine)

time: 102 us -> 104 us (1.020)
  the two profiles are of different devices: /device:TPU:7 before, /device:TPU:64 now
where the time goes in v8:
time: 104 us; the launch traced here: 103 us
  waiting for transfers between devices  47 us (45%)
  starting transfers between devices  41.8 us (40%)
  matrix products  9.74 us (9%)
  local copies, waits for them, and re-layouts  1.99 us (2%)
  other arithmetic  1.82 us (2%)
    ppermute x3, waiting for transfers between devices, local(): got_a = [lax.ppermute(panel, AXES, spread(y1, h1)) for y1, h1 in first]  32.9 us
    ppermute x6, starting transfers between devices, gather(): lax.ppermute(piece, axis, shifts(n, k))  30.9 us
    ppermute x6, waiting for transfers between devices, gather(): lax.ppermute(piece, axis, shifts(n, k))  14.1 us
    ppermute x3, starting transfers between devices, local(): got_a = [lax.ppermute(panel, AXES, spread(y1, h1)) for y1, h1 in first]  8.59 us
    dot_general x1, matrix products, local(): product = lax.dot_general(lhs, rhs, dims, precision=lax.Precision.HIGH)  5.05 us
  transfers between devices with their start and end apart: 13, of which 5 were waited for; matrix products, arithmetic and copies ran while one was open for 6% of the time, Pallas kernels for 0%

profile of v8, /device:TPU:64, one launch (start us, length us, event | category | flops | bytes accessed | tf_op | source)
XLA Modules:
  0.0 103.3 jit_solution(16940612379716406566)
XLA Ops:
  0.6 0.0 copy-start.2
  0.6 0.0 copy-start
  0.7 3.6 %collective-permute-start.4 = (f32[2,128,256]{2,1,0:T(8,128)}, f32[2,128,256]{2,1,0:T(8,128)S(1)}, u32[]{:S(2)}, u32[]{:S(2)}) collective-permute-start(f32[2,128,256]{2,1,0:T(8,128)} %param.4), channel_id=1, source_target_pairs={{0,192},{1,200},{2,208},{3,216},{4,193},{5,201},{6,209},{7,217},{8... | collective-permute-start | bytes 786440 | tf_op jit(solution)/shard_map/ppermute | solution.py:78
  4.3 1.3 %collective-permute-start.5 = (f32[2,128,256]{2,1,0:T(8,128)}, f32[2,128,256]{2,1,0:T(8,128)S(1)}, u32[]{:S(2)}, u32[]{:S(2)}) collective-permute-start(f32[2,128,256]{2,1,0:T(8,128)} %param.4), channel_id=1, source_target_pairs={{0,64},{1,72},{2,80},{3,88},{4,65},{5,73},{6,81},{7,89},{8,66},{9,... | collective-permute-start | bytes 786440 | tf_op jit(solution)/shard_map/ppermute | solution.py:78
  5.6 3.7 %collective-permute-start.6 = (f32[2,128,256]{2,1,0:T(8,128)}, f32[2,128,256]{2,1,0:T(8,128)S(1)}, u32[]{:S(2)}, u32[]{:S(2)}) collective-permute-start(f32[2,128,256]{2,1,0:T(8,128)} %param.4), channel_id=1, source_target_pairs={{0,0},{1,8},{2,16},{3,24},{4,1},{5,9},{6,17},{7,25},{8,2},{9,10},{... | collective-permute-start | bytes 786440 | tf_op jit(solution)/shard_map/ppermute | solution.py:78
  9.3 5.1 %collective-permute-start = (f32[2,128,256]{2,1,0:T(8,128)}, f32[2,128,256]{2,1,0:T(8,128)S(1)}, u32[]{:S(2)}, u32[]{:S(2)}) collective-permute-start(f32[2,128,256]{2,1,0:T(8,128)} %param.4), channel_id=1, source_target_pairs={{0,6},{2,0},{4,2},{6,4},{1,7},{3,1},{5,3},{7,5},{8,14},{10,8},{12,... | collective-permute-start | bytes 786440 | tf_op jit(solution)/shard_map/ppermute | solution.py:66
  14.4 3.0 %collective-permute-start.1 = (f32[2,128,256]{2,1,0:T(8,128)}, f32[2,128,256]{2,1,0:T(8,128)S(1)}, u32[]{:S(2)}, u32[]{:S(2)}) collective-permute-start(f32[2,128,256]{2,1,0:T(8,128)} %param.4), channel_id=1, source_target_pairs={{0,4},{2,6},{4,0},{6,2},{1,5},{3,7},{5,1},{7,3},{8,12},{10,14},{12... | collective-permute-start | bytes 786440 | tf_op jit(solution)/shard_map/ppermute | solution.py:66
  17.4 10.4 %collective-permute-done.4 = f32[2,128,256]{2,1,0:T(8,128)S(1)} collective-permute-done((f32[2,128,256]{2,1,0:T(8,128)}, f32[2,128,256]{2,1,0:T(8,128)S(1)}, u32[]{:S(2)}, u32[]{:S(2)}) %collective-permute-start.4) | collective-permute-done | bytes 262176 | tf_op jit(solution)/shard_map/ppermute | solution.py:78
  27.8 0.0 collective-permute-start.2
  27.8 16.9 %collective-permute-done.5 = f32[2,128,256]{2,1,0:T(8,128)S(1)} collective-permute-done((f32[2,128,256]{2,1,0:T(8,128)}, f32[2,128,256]{2,1,0:T(8,128)S(1)}, u32[]{:S(2)}, u32[]{:S(2)}) %collective-permute-start.5) | collective-permute-done | bytes 262176 | tf_op jit(solution)/shard_map/ppermute | solution.py:78
  44.7 5.6 %collective-permute-done.6 = f32[2,128,256]{2,1,0:T(8,128)S(1)} collective-permute-done((f32[2,128,256]{2,1,0:T(8,128)}, f32[2,128,256]{2,1,0:T(8,128)S(1)}, u32[]{:S(2)}, u32[]{:S(2)}) %collective-permute-start.6) | collective-permute-done | bytes 262176 | tf_op jit(solution)/shard_map/ppermute | solution.py:78
  50.3 0.7 collective-permute-start.7
  51.0 0.7 collective-permute-start.8
  51.7 1.3 %fusion.12 = f32[128,256]{1,0:T(8,128)S(1)} fusion(f32[2,256,256]{2,1,0:T(8,128)} %param.5, f32[2,128,256]{2,1,0:T(8,128)} %param.4), kind=kOutput, calls=%fused_computation.30 | convolution fusion | flops 100663296 | bytes 524288 | tf_op jit(solution)/shard_map/dot_general | solution.py:14
  53.0 1.3 %fusion.18 = f32[128,256]{1,0:T(8,128)S(1)} fusion(f32[2,256,256]{2,1,0:T(8,128)} %param.5, f32[2,128,256]{2,1,0:T(8,128)} %param.4), kind=kOutput, calls=%fused_computation.36 | convolution fusion | flops 100663296 | bytes 524288 | tf_op jit(solution)/shard_map/dot_general | solution.py:13
  54.4 0.0 collective-permute-done.7
  54.4 0.0 collective-permute-done.8
  54.4 0.1 fusion.9
  54.4 0.7 collective-permute-start.9
  55.1 0.0 copy-done.2
  55.1 0.0 copy-done
  55.1 0.3 fusion.5
  55.4 0.3 fusion.6
  55.7 0.7 pad_maximum_fusion.3
  56.4 0.0 collective-permute-done.9
  56.5 21.8 %collective-permute-start.10 = (f32[2,128,256]{2,1,0:T(8,128)S(1)}, f32[2,128,256]{2,1,0:T(8,128)S(1)}, u32[]{:S(2)}, u32[]{:S(2)}) collective-permute-start(f32[2,128,256]{2,1,0:T(8,128)S(1)} %select_select_fusion), channel_id=1, source_target_pairs={{0,24},{8,0},{16,8},{24,16},{1,25},{9,1},{17,9},{25,17},{2,26},{10... | collective-permute-start | bytes 786440 | tf_op jit(solution)/shard_map/ppermute | solution.py:66
  78.3 0.0 collective-permute-start.11
  78.3 0.0 collective-permute-done
  78.3 1.0 collective-permute-start.12
  79.2 0.0 collective-permute-done.1
  79.2 0.0 collective-permute-done.2
  79.2 0.1 select_select_fusion.10
  79.4 0.1 pad_maximum_fusion.1
  79.5 0.4 collective-permute-start.3
  79.8 10.6 %collective-permute-done.10 = f32[2,128,256]{2,1,0:T(8,128)S(1)} collective-permute-done((f32[2,128,256]{2,1,0:T(8,128)S(1)}, f32[2,128,256]{2,1,0:T(8,128)S(1)}, u32[]{:S(2)}, u32[]{:S(2)}) %collective-permute-start.10) | collective-permute-done | bytes 262176 | tf_op jit(solution)/shard_map/ppermute | solution.py:66
  90.4 0.0 collective-permute-done.11
  90.4 3.4 %collective-permute-done.12 = f32[2,128,256]{2,1,0:T(8,128)S(1)} collective-permute-done((f32[2,128,256]{2,1,0:T(8,128)S(1)}, f32[2,128,256]{2,1,0:T(8,128)S(1)}, u32[]{:S(2)}, u32[]{:S(2)}) %collective-permute-start.12) | collective-permute-done | bytes 262176 | tf_op jit(solution)/shard_map/ppermute | solution.py:66
  93.9 0.1 select_select_fusion.5
  94.0 0.1 pad_maximum_fusion.2
  94.1 0.4 fusion.8
  94.4 0.4 fusion.4
  94.8 0.4 fusion.7
  95.2 0.4 convolution_add_fusion
  95.7 0.2 maximum_bitcast_fusion
  95.8 0.0 collective-permute-done.3
  95.8 0.2 broadcast_select_fusion.1
  96.0 0.0 copy-start.1
  96.0 0.2 pad_maximum_fusion
  96.2 2.0 %copy-done.1 = f32[2,1024,512]{2,1,0:T(8,128)S(1)} copy-done((f32[2,1024,512]{2,1,0:T(8,128)S(1)}, f32[2,1024,512]{2,1,0:T(8,128)}, u32[]{:S(2)}) %copy-start.1) | copy-done | bytes 4194328
  98.2 5.1 %bitcast_subtract_fusion = f32[2,1024,512]{2,1,0:T(8,128)} fusion(f32[2,1024,512]{2,1,0:T(8,128)S(1)} %copy-done.1, f32[1,2,512,256]{3,2,1,0:T(8,128)S(1)} %get-tuple-element.13, f32[1,2,512,256]{3,2,1,0:T(8,128)S(1)} %get-tuple-element.12, f32[2,1024,256]{2,1,0:T(8,128)S(1)} %bitcast.55), kind=kOutput, calls=%fused_computation | convolution fusion | flops 3222798336 | bytes 12582912 | tf_op jit(solution)/shard_map/dot_general | solution.py:104
  (3 shorter events, 0.1 us)
Async XLA Ops:
  0.6 54.5 %copy-start.2 = (f32[2,128,256]{2,1,0:T(8,128)S(1)}, f32[2,128,256]{2,1,0:T(8,128)}, u32[]{:S(2)}) copy-start(f32[2,128,256]{2,1,0:T(8,128)} %param.4) | copy-start | bytes 786436
  0.6 54.5 %copy-start = (f32[2,256,256]{2,1,0:T(8,128)S(1)}, f32[2,256,256]{2,1,0:T(8,128)}, u32[]{:S(2)}) copy-start(f32[2,256,256]{2,1,0:T(8,128)} %param.5) | copy-start | bytes 1572868
  0.7 27.1 %collective-permute-start.4 = (f32[2,128,256]{2,1,0:T(8,128)}, f32[2,128,256]{2,1,0:T(8,128)S(1)}, u32[]{:S(2)}, u32[]{:S(2)}) collective-permute-start(f32[2,128,256]{2,1,0:T(8,128)} %param.4), channel_id=1, source_target_pairs={{0,192},{1,200},{2,208},{3,216},{4,193},{5,201},{6,209},{7,217},{8... | collective-permute-start | bytes 786440 | tf_op jit(solution)/shard_map/ppermute | solution.py:78
  4.3 40.4 %collective-permute-start.5 = (f32[2,128,256]{2,1,0:T(8,128)}, f32[2,128,256]{2,1,0:T(8,128)S(1)}, u32[]{:S(2)}, u32[]{:S(2)}) collective-permute-start(f32[2,128,256]{2,1,0:T(8,128)} %param.4), channel_id=1, source_target_pairs={{0,64},{1,72},{2,80},{3,88},{4,65},{5,73},{6,81},{7,89},{8,66},{9,... | collective-permute-start | bytes 786440 | tf_op jit(solution)/shard_map/ppermute | solution.py:78
  5.6 44.7 %collective-permute-start.6 = (f32[2,128,256]{2,1,0:T(8,128)}, f32[2,128,256]{2,1,0:T(8,128)S(1)}, u32[]{:S(2)}, u32[]{:S(2)}) collective-permute-start(f32[2,128,256]{2,1,0:T(8,128)} %param.4), channel_id=1, source_target_pairs={{0,0},{1,8},{2,16},{3,24},{4,1},{5,9},{6,17},{7,25},{8,2},{9,10},{... | collective-permute-start | bytes 786440 | tf_op jit(solution)/shard_map/ppermute | solution.py:78
  9.3 69.0 %collective-permute-start = (f32[2,128,256]{2,1,0:T(8,128)}, f32[2,128,256]{2,1,0:T(8,128)S(1)}, u32[]{:S(2)}, u32[]{:S(2)}) collective-permute-start(f32[2,128,256]{2,1,0:T(8,128)} %param.4), channel_id=1, source_target_pairs={{0,6},{2,0},{4,2},{6,4},{1,7},{3,1},{5,3},{7,5},{8,14},{10,8},{12,... | collective-permute-start | bytes 786440 | tf_op jit(solution)/shard_map/ppermute | solution.py:66
  14.4 64.9 %collective-permute-start.1 = (f32[2,128,256]{2,1,0:T(8,128)}, f32[2,128,256]{2,1,0:T(8,128)S(1)}, u32[]{:S(2)}, u32[]{:S(2)}) collective-permute-start(f32[2,128,256]{2,1,0:T(8,128)} %param.4), channel_id=1, source_target_pairs={{0,4},{2,6},{4,0},{6,2},{1,5},{3,7},{5,1},{7,3},{8,12},{10,14},{12... | collective-permute-start | bytes 786440 | tf_op jit(solution)/shard_map/ppermute | solution.py:66
  27.8 51.5 %collective-permute-start.2 = (f32[2,128,256]{2,1,0:T(8,128)}, f32[2,128,256]{2,1,0:T(8,128)S(1)}, u32[]{:S(2)}, u32[]{:S(2)}) collective-permute-start(f32[2,128,256]{2,1,0:T(8,128)} %param.4), channel_id=1, source_target_pairs={{0,2},{2,4},{4,6},{6,0},{1,3},{3,5},{5,7},{7,1},{8,10},{10,12},{12... | collective-permute-start | bytes 786440 | tf_op jit(solution)/shard_map/ppermute | solution.py:66
  50.3 4.0 %collective-permute-start.7 = (f32[2,128,256]{2,1,0:T(8,128)S(1)}, f32[2,128,256]{2,1,0:T(8,128)S(1)}, u32[]{:S(2)}, u32[]{:S(2)}) collective-permute-start(f32[2,128,256]{2,1,0:T(8,128)S(1)} %select_select_fusion.6), channel_id=1, source_target_pairs={{64,96},{65,97},{66,98},{67,99},{68,100},{69,101},{70,102},{71,103... | collective-permute-start | bytes 786440 | tf_op jit(solution)/shard_map/ppermute | solution.py:86
  51.0 3.3 %collective-permute-start.8 = (f32[2,128,256]{2,1,0:T(8,128)S(1)}, f32[2,128,256]{2,1,0:T(8,128)S(1)}, u32[]{:S(2)}, u32[]{:S(2)}) collective-permute-start(f32[2,128,256]{2,1,0:T(8,128)S(1)} %select_select_fusion.6), channel_id=1, source_target_pairs={{64,128},{192,224},{65,129},{193,225},{66,130},{194,226},{67,131},... | collective-permute-start | bytes 786440 | tf_op jit(solution)/shard_map/ppermute | solution.py:86
  54.4 2.0 %collective-permute-start.9 = (f32[2,128,256]{2,1,0:T(8,128)S(1)}, f32[2,128,256]{2,1,0:T(8,128)S(1)}, u32[]{:S(2)}, u32[]{:S(2)}) collective-permute-start(f32[2,128,256]{2,1,0:T(8,128)S(1)} %fusion.9), channel_id=1, source_target_pairs={{96,160},{224,32},{97,161},{225,33},{98,162},{226,34},{99,163},{22... | collective-permute-start | bytes 786440 | tf_op jit(solution)/shard_map/ppermute | solution.py:86
  56.5 34.0 %collective-permute-start.10 = (f32[2,128,256]{2,1,0:T(8,128)S(1)}, f32[2,128,256]{2,1,0:T(8,128)S(1)}, u32[]{:S(2)}, u32[]{:S(2)}) collective-permute-start(f32[2,128,256]{2,1,0:T(8,128)S(1)} %select_select_fusion), channel_id=1, source_target_pairs={{0,24},{8,0},{16,8},{24,16},{1,25},{9,1},{17,9},{25,17},{2,26},{10... | collective-permute-start | bytes 786440 | tf_op jit(solution)/shard_map/ppermute | solution.py:66
  78.3 12.2 %collective-permute-start.11 = (f32[2,128,256]{2,1,0:T(8,128)S(1)}, f32[2,128,256]{2,1,0:T(8,128)S(1)}, u32[]{:S(2)}, u32[]{:S(2)}) collective-permute-start(f32[2,128,256]{2,1,0:T(8,128)S(1)} %select_select_fusion), channel_id=1, source_target_pairs={{0,16},{8,24},{16,0},{24,8},{1,17},{9,25},{17,1},{25,9},{2,18},{10... | collective-permute-start | bytes 786440 | tf_op jit(solution)/shard_map/ppermute | solution.py:66
  78.3 15.6 %collective-permute-start.12 = (f32[2,128,256]{2,1,0:T(8,128)S(1)}, f32[2,128,256]{2,1,0:T(8,128)S(1)}, u32[]{:S(2)}, u32[]{:S(2)}) collective-permute-start(f32[2,128,256]{2,1,0:T(8,128)S(1)} %select_select_fusion), channel_id=1, source_target_pairs={{0,8},{8,16},{16,24},{24,0},{1,9},{9,17},{17,25},{25,1},{2,10},{10... | collective-permute-start | bytes 786440 | tf_op jit(solution)/shard_map/ppermute | solution.py:66
  79.5 16.4 %collective-permute-start.3 = (f32[2,512,256]{2,1,0:T(8,128)S(1)}, f32[2,512,256]{2,1,0:T(8,128)S(1)}, u32[]{:S(2)}, u32[]{:S(2)}) collective-permute-start(f32[2,512,256]{2,1,0:T(8,128)S(1)} %pad_maximum_fusion.1), channel_id=1, source_target_pairs={{0,1},{1,0},{2,3},{3,2},{4,5},{5,4},{6,7},{7,6},{8,9},{9,8},{10,11... | collective-permute-start | bytes 3145736 | tf_op jit(solution)/shard_map/ppermute | solution.py:92
  96.0 2.2 %copy-start.1 = (f32[2,1024,512]{2,1,0:T(8,128)S(1)}, f32[2,1024,512]{2,1,0:T(8,128)}, u32[]{:S(2)}) copy-start(f32[2,1024,512]{2,1,0:T(8,128)} %param.3) | copy-start | bytes 12582916

commit v9 on v6

--- a/solution.py
+++ b/solution.py
@@ -66,9 +66,14 @@
         got = [piece] + [lax.ppermute(piece, axis, shifts(n, k)) for k in range(1, n)]
         return reorder(got, idx, n)
 
+    def spread_all(piece, axis, n):
+        two, rows, width = piece.shape
+        copies = jnp.broadcast_to(piece[:, None], (two, n, rows, width))
+        got = lax.all_to_all(copies, axis, 1, 1, tiled=True)
+        return got.reshape(two, n * rows, width)
+
     def local(trailing, panel, diag_inverse):
         scaled = complex_product(panel, diag_inverse)
-        block = lax.all_gather(panel, COL, axis=1, tiled=True)
 
         yi = lax.axis_index("y")
         hi = lax.axis_index("zh")
@@ -87,8 +92,10 @@
                 got = lax.ppermute(sent, ("y", "zh"), [(plane(h0, y0), plane(h1, y1)) for (y0, h0), (y1, h1) in pairs])
                 for _, (y1, h1) in pairs:
                     held = jnp.where((yi == y1) & (hi == h1), got, held)
-        window = gather(held, "x", xi, nx)
+        panel_late, held = lax.optimization_barrier((panel, held))
+        window = spread_all(held, "x", nx)
 
+        block = spread_all(panel_late, COL, nl * nc)
 
         tiles = complex_product(window, diag_inverse, lax.Precision.HIGH)
         rhs = jnp.stack([jnp.stack([tiles[0], -tiles[1]]), jnp.stack([tiles[1], tiles[0]])])

time: 127 us -> 144 us (1.13)
  the two profiles are of different devices: /device:TPU:65 before, /device:TPU:7 now
where the time goes in v9:
time: 144 us; the launch traced here: 141 us
  waiting for transfers between devices  57.5 us (40%)
  starting transfers between devices  38.9 us (27%)
  blocking collectives  29.6 us (21%)
  matrix products  9.28 us (6%)
  local copies, waits for them, and re-layouts  2.91 us (2%)
  other arithmetic  2.03 us (1%)
    all_to_all x1, waiting for transfers between devices, spread_all(): got = lax.all_to_all(copies, axis, 1, 1, tiled=True)  43.4 us
    all_to_all x1, blocking collectives, spread_all(): got = lax.all_to_all(copies, axis, 1, 1, tiled=True)  29.6 us
    all_to_all x1, starting transfers between devices, spread_all(): got = lax.all_to_all(copies, axis, 1, 1, tiled=True)  23.5 us
    ppermute x3, waiting for transfers between devices, local(): got_a = [lax.ppermute(panel, AXES, spread(y1, h1)) for y1, h1 in first]  14.1 us
    ppermute x3, starting transfers between devices, local(): got_a = [lax.ppermute(panel, AXES, spread(y1, h1)) for y1, h1 in first]  13.4 us
    dot_general x1, matrix products, local(): product = lax.dot_general(lhs, rhs, dims, precision=lax.Precision.HIGH)  6.65 us
  transfers between devices with their start and end apart: 7, of which 4 were waited for; matrix products, arithmetic and copies ran while one was open for 3% of the time, Pallas kernels for 0%

profile of v9, /device:TPU:7, one launch (start us, length us, event | category | flops | bytes accessed | tf_op | source)
XLA Modules:
  0.0 141.1 jit_solution(4131775166185462037)
XLA Ops:
  0.6 10.1 %collective-permute-start = (f32[2,128,256]{2,1,0:T(8,128)}, f32[2,128,256]{2,1,0:T(8,128)S(1)}, u32[]{:S(2)}, u32[]{:S(2)}) collective-permute-start(f32[2,128,256]{2,1,0:T(8,128)} %param.4), channel_id=1, source_target_pairs={{0,192},{1,200},{2,208},{3,216},{4,193},{5,201},{6,209},{7,217},{8... | collective-permute-start | bytes 786440 | tf_op jit(solution)/shard_map/ppermute | solution.py:84
  10.8 1.3 collective-permute-start.1
  12.1 1.9 %collective-permute-start.2 = (f32[2,128,256]{2,1,0:T(8,128)}, f32[2,128,256]{2,1,0:T(8,128)S(1)}, u32[]{:S(2)}, u32[]{:S(2)}) collective-permute-start(f32[2,128,256]{2,1,0:T(8,128)} %param.4), channel_id=1, source_target_pairs={{0,0},{1,8},{2,16},{3,24},{4,1},{5,9},{6,17},{7,25},{8,2},{9,10},{... | collective-permute-start | bytes 786440 | tf_op jit(solution)/shard_map/ppermute | solution.py:84
  14.0 3.2 %collective-permute-done = f32[2,128,256]{2,1,0:T(8,128)S(1)} collective-permute-done((f32[2,128,256]{2,1,0:T(8,128)}, f32[2,128,256]{2,1,0:T(8,128)S(1)}, u32[]{:S(2)}, u32[]{:S(2)}) %collective-permute-start) | collective-permute-done | bytes 262176 | tf_op jit(solution)/shard_map/ppermute | solution.py:84
  17.2 5.6 %collective-permute-done.1 = f32[2,128,256]{2,1,0:T(8,128)S(1)} collective-permute-done((f32[2,128,256]{2,1,0:T(8,128)}, f32[2,128,256]{2,1,0:T(8,128)S(1)}, u32[]{:S(2)}, u32[]{:S(2)}) %collective-permute-start.1) | collective-permute-done | bytes 262176 | tf_op jit(solution)/shard_map/ppermute | solution.py:84
  22.8 5.3 %collective-permute-done.2 = f32[2,128,256]{2,1,0:T(8,128)S(1)} collective-permute-done((f32[2,128,256]{2,1,0:T(8,128)}, f32[2,128,256]{2,1,0:T(8,128)S(1)}, u32[]{:S(2)}, u32[]{:S(2)}) %collective-permute-start.2) | collective-permute-done | bytes 262176 | tf_op jit(solution)/shard_map/ppermute | solution.py:84
  28.1 0.7 collective-permute-start.3
  28.8 0.7 collective-permute-start.4
  29.5 0.0 collective-permute-done.3
  29.5 0.0 collective-permute-done.4
  29.6 0.1 fusion.7
  29.6 0.7 collective-permute-start.5
  30.3 0.0 copy-start.3
  30.3 0.0 collective-permute-done.5
  30.4 0.1 broadcast_in_dim.22
  30.5 29.6 %all_to_all.10 = f32[2,4,128,256]{3,2,0,1:T(8,128)} all-to-all(f32[2,4,128,256]{3,2,0,1:T(8,128)S(1)} %broadcast_in_dim.22), channel_id=1, replica_groups=mesh['y'=4,'zh'=2,'x'=4,'zl'=4,'core'=2] {'x'}, dimensions={1} | all-to-all | bytes 2097152 | tf_op jit(solution)/shard_map/all_to_all | solution.py:72
  60.1 0.0 copy-done.3
  60.1 1.5 %broadcast_in_dim.8 = f32[2,8,128,256]{3,2,0,1:T(8,128)} broadcast(f32[2,128,256]{2,1,0:T(8,128)S(1)} %copy-done.3), dimensions={0,2,3} | broadcast | bytes 2359296 | tf_op jit(solution)/shard_map/broadcast_in_dim | solution.py:71
  61.6 0.0 copy-start
  61.6 23.5 %all-to-all-start = ((f32[2,8,128,256]{3,2,0,1:T(8,128)}), f32[2,8,128,256]{3,2,0,1:T(8,128)S(1)}, u32[]{:S(2)}, u32[]{:S(2)}) async-start(f32[2,8,128,256]{3,2,0,1:T(8,128)} %broadcast_in_dim.8), calls=%async_computation | async-start | bytes 4194304 | tf_op jit(solution)/shard_map/all_to_all | solution.py:72
  85.2 0.0 copy-done
  85.2 0.0 copy-start.2
  85.2 0.3 fusion.11
  85.5 0.3 fusion.5
  85.8 0.3 fusion.18
  86.1 0.3 fusion.6
  86.3 0.7 pad_maximum_fusion
  87.1 0.0 copy-done.2
  87.1 0.1 fusion.37
  87.1 0.4 fusion.15
  87.5 0.4 fusion.4
  87.9 0.4 fusion.8
  88.3 0.4 convolution_add_fusion
  88.7 1.1 maximum_bitcast_fusion
  89.9 43.4 %all-to-all-done = f32[2,8,128,256]{3,2,0,1:T(8,128)S(1)} async-done(((f32[2,8,128,256]{3,2,0,1:T(8,128)}), f32[2,8,128,256]{3,2,0,1:T(8,128)S(1)}, u32[]{:S(2)}, u32[]{:S(2)}) %all-to-all-start) | async-done | bytes 2097184 | tf_op jit(solution)/shard_map/all_to_all | solution.py:72
  133.3 0.0 copy-start.1
  133.3 0.2 copy.5
  133.5 1.0 copy-done.1
  134.5 6.7 %bitcast_subtract_fusion = f32[2,1024,512]{2,1,0:T(8,128)} fusion(f32[2,1024,512]{2,1,0:T(8,128)} %param.3, f32[1,2,512,256]{3,2,1,0:T(8,128)S(1)} %copy-done.1, f32[1,2,512,256]{3,2,1,0:T(8,128)S(1)} %get-tuple-element.8, f32[2,1024,256]{2,1,0:T(8,128)S(1)} %bitcast.51), kind=kOutput, calls=%fused_computation | convolution fusion | flops 3222798336 | bytes 12582912 | tf_op jit(solution)/shard_map/dot_general | solution.py:104
  (3 shorter events, 0.1 us)
Async XLA Ops:
  0.6 16.6 %collective-permute-start = (f32[2,128,256]{2,1,0:T(8,128)}, f32[2,128,256]{2,1,0:T(8,128)S(1)}, u32[]{:S(2)}, u32[]{:S(2)}) collective-permute-start(f32[2,128,256]{2,1,0:T(8,128)} %param.4), channel_id=1, source_target_pairs={{0,192},{1,200},{2,208},{3,216},{4,193},{5,201},{6,209},{7,217},{8... | collective-permute-start | bytes 786440 | tf_op jit(solution)/shard_map/ppermute | solution.py:84
  10.8 12.1 %collective-permute-start.1 = (f32[2,128,256]{2,1,0:T(8,128)}, f32[2,128,256]{2,1,0:T(8,128)S(1)}, u32[]{:S(2)}, u32[]{:S(2)}) collective-permute-start(f32[2,128,256]{2,1,0:T(8,128)} %param.4), channel_id=1, source_target_pairs={{0,64},{1,72},{2,80},{3,88},{4,65},{5,73},{6,81},{7,89},{8,66},{9,... | collective-permute-start | bytes 786440 | tf_op jit(solution)/shard_map/ppermute | solution.py:84
  12.1 16.0 %collective-permute-start.2 = (f32[2,128,256]{2,1,0:T(8,128)}, f32[2,128,256]{2,1,0:T(8,128)S(1)}, u32[]{:S(2)}, u32[]{:S(2)}) collective-permute-start(f32[2,128,256]{2,1,0:T(8,128)} %param.4), channel_id=1, source_target_pairs={{0,0},{1,8},{2,16},{3,24},{4,1},{5,9},{6,17},{7,25},{8,2},{9,10},{... | collective-permute-start | bytes 786440 | tf_op jit(solution)/shard_map/ppermute | solution.py:84
  28.1 1.4 collective-permute-start.3
  28.8 0.7 collective-permute-start.4
  29.6 0.7 collective-permute-start.5
  30.3 29.8 %copy-start.3 = (f32[2,128,256]{2,1,0:T(8,128)S(1)}, f32[2,128,256]{2,1,0:T(8,128)}, u32[]{:S(2)}) copy-start(f32[2,128,256]{2,1,0:T(8,128)} %param.4) | copy-start | bytes 786436
  61.6 23.5 %copy-start = (f32[2,256,256]{2,1,0:T(8,128)S(1)}, f32[2,256,256]{2,1,0:T(8,128)}, u32[]{:S(2)}) copy-start(f32[2,256,256]{2,1,0:T(8,128)} %param.5) | copy-start | bytes 1572868
  61.6 71.6 %all-to-all-start = ((f32[2,8,128,256]{3,2,0,1:T(8,128)}), f32[2,8,128,256]{3,2,0,1:T(8,128)S(1)}, u32[]{:S(2)}, u32[]{:S(2)}) async-start(f32[2,8,128,256]{3,2,0,1:T(8,128)} %broadcast_in_dim.8), calls=%async_computation | async-start | bytes 4194304 | tf_op jit(solution)/shard_map/all_to_all | solution.py:72
  85.2 1.9 %copy-start.2 = (f32[2,4,128,256]{3,2,0,1:T(8,128)S(1)}, f32[2,4,128,256]{3,2,0,1:T(8,128)}, u32[]{:S(2)}) copy-start(f32[2,4,128,256]{3,2,0,1:T(8,128)} %all_to_all.10) | copy-start | bytes 3145732
  133.3 1.2 copy-start.1

commit v10 on v5

--- a/solution.py
+++ b/solution.py
@@ -44,7 +44,16 @@
                     pairs.append((lin(0, 0, g, l, c), lin(y1, h1, p % nx, g, p // nx)))
         return pairs
 
-    first = [(0, 0), (1, 0), (ny - 1, 0)]
+    first = [(1, 0), (ny - 1, 0)]
+
+    def deal(d):
+        pairs = []
+        for x in range(nx):
+            for l in range(nl):
+                for c in range(nc):
+                    q = nc * (l % 2) + c
+                    pairs.append(((x * nl + l) * nc + c, (((q + d) % nx) * nl + x) * nc + l // 2))
+        return pairs
     relays = [
         [[((1, 0), (2, 0)), ((ny - 1, 0), (ny - 1, 1))], [((1, 0), (1, 1))]],
         [[((1, 1), (2, 1)), ((ny - 1, 1), (0, 1))]],
@@ -75,9 +84,9 @@
         li = lax.axis_index("zl")
         ci = lax.axis_index("core")
 
-        got_a = [lax.ppermute(panel, AXES, spread(y1, h1)) for y1, h1 in first]
-        held_a = got_a[0]
-        for (y1, h1), got in zip(first[1:], got_a[1:]):
+        held_a = panel
+        for y1, h1 in first:
+            got = lax.ppermute(panel, ("y", "zh"), [(plane(0, 0), plane(h1, y1))])
             held_a = jnp.where((yi == y1) & (hi == h1), got, held_a)
         held = held_a
         for stage in relays:
@@ -87,7 +96,8 @@
                 for _, (y1, h1) in pairs:
                     held = jnp.where((yi == y1) & (hi == h1), got, held)
         panel_late, held = lax.optimization_barrier((panel, held))
-        window = gather(held, "x", xi, nx)
+        dealt = [lax.ppermute(held, ("x", "zl", "core"), deal(d)) for d in range(nx)]
+        window = reorder(dealt, xi, nx)
 
         mine = gather(panel_late, "zl", li, nl)
         other = lax.ppermute(mine, "core", shifts(nc, 1))

time: 102 us -> 138 us (1.35)
  the two profiles are of different devices: /device:TPU:7 before, /device:TPU:132 now
where the time goes in v10:
time: 138 us
  waiting for transfers between devices  71.4 us (52%)
  starting transfers between devices  53 us (38%)
  matrix products  7.7 us (6%)
  other arithmetic  2.78 us (2%)
  local copies, waits for them, and re-layouts  1.98 us (1%)
    ppermute x4, waiting for transfers between devices, local(): lax.ppermute(held, ('x', 'zl', 'core'), deal(d))  39.2 us
    ppermute x3, waiting for transfers between devices, local(): lax.ppermute(sent, ('y', 'zh'), [(plane(h0, y0), plane(h1, y1)) for (y0,...  21.9 us
    ppermute x1, starting transfers between devices, local(): other = lax.ppermute(mine, 'core', shifts(nc, 1))  20.6 us
    ppermute x3, starting transfers between devices, gather(): lax.ppermute(piece, axis, shifts(n, k))  17.3 us
    ppermute x4, starting transfers between devices, local(): lax.ppermute(held, ('x', 'zl', 'core'), deal(d))  11 us
    ppermute x3, waiting for transfers between devices, gather(): lax.ppermute(piece, axis, shifts(n, k))  10.3 us
    dot_general x1, matrix products, local(): product = lax.dot_general(lhs, rhs, dims, precision=lax.Precision.HIGH)  5.06 us
  transfers between devices with their start and end apart: 13, of which 4 were waited for; matrix products, arithmetic and copies ran while one was open for 3% of the time, Pallas kernels for 0%

profile of v10, /device:TPU:132, one launch (start us, length us, event | category | flops | bytes accessed | tf_op | source)
XLA Modules:
  0.0 138.0 jit_solution(8829257946657177534)
XLA Ops:
  0.6 0.0 copy-start.2
  0.6 0.0 copy-start
  0.6 0.8 collective-permute-start
  1.5 0.7 collective-permute-start.1
  2.2 0.0 collective-permute-done
  2.2 0.0 collective-permute-done.1
  2.2 1.0 select_select_fusion.10
  3.2 0.7 collective-permute-start.2
  3.9 0.7 collective-permute-start.3
  4.6 0.0 collective-permute-done.2
  4.6 0.0 collective-permute-done.3
  4.6 0.1 fusion.9
  4.7 1.3 collective-permute-start.4
  6.0 0.0 copy-done.2
  6.0 0.0 copy-done
  6.0 0.3 fusion.12
  6.3 0.3 fusion.18
  6.6 21.9 %collective-permute-done.4 = f32[2,128,256]{2,1,0:T(8,128)S(1)} collective-permute-done((f32[2,128,256]{2,1,0:T(8,128)S(1)}, f32[2,128,256]{2,1,0:T(8,128)S(1)}, u32[]{:S(2)}, u32[]{:S(2)}) %collective-permute-start.4) | collective-permute-done | bytes 262176 | tf_op jit(solution)/shard_map/ppermute | solution.py:95
  28.6 4.7 %collective-permute-start.5 = (f32[2,128,256]{2,1,0:T(8,128)S(1)}, f32[2,128,256]{2,1,0:T(8,128)S(1)}, u32[]{:S(2)}, u32[]{:S(2)}) collective-permute-start(f32[2,128,256]{2,1,0:T(8,128)S(1)} %copy-done.2), channel_id=1, source_target_pairs={{0,6},{2,0},{4,2},{6,4},{1,7},{3,1},{5,3},{7,5},{8,14},{10,8},{12,... | collective-permute-start | bytes 786440 | tf_op jit(solution)/shard_map/ppermute | solution.py:75
  33.3 10.7 %collective-permute-start.6 = (f32[2,128,256]{2,1,0:T(8,128)S(1)}, f32[2,128,256]{2,1,0:T(8,128)S(1)}, u32[]{:S(2)}, u32[]{:S(2)}) collective-permute-start(f32[2,128,256]{2,1,0:T(8,128)S(1)} %copy-done.2), channel_id=1, source_target_pairs={{0,4},{2,6},{4,0},{6,2},{1,5},{3,7},{5,1},{7,3},{8,12},{10,14},{12... | collective-permute-start | bytes 786440 | tf_op jit(solution)/shard_map/ppermute | solution.py:75
  43.9 1.9 %collective-permute-start.7 = (f32[2,128,256]{2,1,0:T(8,128)S(1)}, f32[2,128,256]{2,1,0:T(8,128)S(1)}, u32[]{:S(2)}, u32[]{:S(2)}) collective-permute-start(f32[2,128,256]{2,1,0:T(8,128)S(1)} %copy-done.2), channel_id=1, source_target_pairs={{0,2},{2,4},{4,6},{6,0},{1,3},{3,5},{5,7},{7,1},{8,10},{10,12},{12... | collective-permute-start | bytes 786440 | tf_op jit(solution)/shard_map/ppermute | solution.py:75
  45.9 0.3 fusion.5
  46.3 0.3 fusion.6
  46.6 0.7 pad_maximum_fusion.3
  47.3 0.0 collective-permute-start.10
  47.3 2.6 %collective-permute-start.11 = (f32[2,128,256]{2,1,0:T(8,128)S(1)}, f32[2,128,256]{2,1,0:T(8,128)S(1)}, u32[]{:S(2)}, u32[]{:S(2)}) collective-permute-start(f32[2,128,256]{2,1,0:T(8,128)S(1)} %select_select_fusion), channel_id=1, source_target_pairs={{0,8},{1,16},{2,24},{3,0},{4,9},{5,17},{6,25},{7,1},{8,10},{9,18},... | collective-permute-start | bytes 786440 | tf_op jit(solution)/shard_map/ppermute | solution.py:99
  50.0 0.0 collective-permute-done.5
  50.0 6.2 %collective-permute-start.12 = (f32[2,128,256]{2,1,0:T(8,128)S(1)}, f32[2,128,256]{2,1,0:T(8,128)S(1)}, u32[]{:S(2)}, u32[]{:S(2)}) collective-permute-start(f32[2,128,256]{2,1,0:T(8,128)S(1)} %select_select_fusion), channel_id=1, source_target_pairs={{0,0},{1,8},{2,16},{3,24},{4,1},{5,9},{6,17},{7,25},{8,2},{9,10},{... | collective-permute-start | bytes 786440 | tf_op jit(solution)/shard_map/ppermute | solution.py:99
  56.2 10.3 %collective-permute-done.6 = f32[2,128,256]{2,1,0:T(8,128)S(1)} collective-permute-done((f32[2,128,256]{2,1,0:T(8,128)S(1)}, f32[2,128,256]{2,1,0:T(8,128)S(1)}, u32[]{:S(2)}, u32[]{:S(2)}) %collective-permute-start.6) | collective-permute-done | bytes 262176 | tf_op jit(solution)/shard_map/ppermute | solution.py:75
  66.5 2.1 %collective-permute-start.9 = (f32[2,128,256]{2,1,0:T(8,128)S(1)}, f32[2,128,256]{2,1,0:T(8,128)S(1)}, u32[]{:S(2)}, u32[]{:S(2)}) collective-permute-start(f32[2,128,256]{2,1,0:T(8,128)S(1)} %select_select_fusion), channel_id=1, source_target_pairs={{0,24},{1,0},{2,8},{3,16},{4,25},{5,1},{6,9},{7,17},{8,26},{9,2},{... | collective-permute-start | bytes 786440 | tf_op jit(solution)/shard_map/ppermute | solution.py:99
  68.6 0.0 collective-permute-done.7
  68.6 0.1 select_select_fusion.9
  68.7 0.1 pad_maximum_fusion.1
  68.8 20.6 %collective-permute-start.8 = (f32[2,512,256]{2,1,0:T(8,128)S(1)}, f32[2,512,256]{2,1,0:T(8,128)S(1)}, u32[]{:S(2)}, u32[]{:S(2)}) collective-permute-start(f32[2,512,256]{2,1,0:T(8,128)S(1)} %pad_maximum_fusion.1), channel_id=1, source_target_pairs={{0,1},{1,0},{2,3},{3,2},{4,5},{5,4},{6,7},{7,6},{8,9},{9,8},{10,11... | collective-permute-start | bytes 3145736 | tf_op jit(solution)/shard_map/ppermute | solution.py:103
  89.4 0.0 collective-permute-done.10
  89.4 0.0 collective-permute-done.11
  89.4 33.3 %collective-permute-done.12 = f32[2,128,256]{2,1,0:T(8,128)S(1)} collective-permute-done((f32[2,128,256]{2,1,0:T(8,128)S(1)}, f32[2,128,256]{2,1,0:T(8,128)S(1)}, u32[]{:S(2)}, u32[]{:S(2)}) %collective-permute-start.12) | collective-permute-done | bytes 262176 | tf_op jit(solution)/shard_map/ppermute | solution.py:99
  122.7 5.9 %collective-permute-done.9 = f32[2,128,256]{2,1,0:T(8,128)S(1)} collective-permute-done((f32[2,128,256]{2,1,0:T(8,128)S(1)}, f32[2,128,256]{2,1,0:T(8,128)S(1)}, u32[]{:S(2)}, u32[]{:S(2)}) %collective-permute-start.9) | collective-permute-done | bytes 262176 | tf_op jit(solution)/shard_map/ppermute | solution.py:99
  128.6 0.1 select_select_fusion.5
  128.7 0.1 pad_maximum_fusion.2
  128.8 0.4 fusion.8
  129.2 0.4 fusion.4
  129.6 0.4 fusion.7
  130.0 0.4 convolution_add_fusion
  130.4 0.2 maximum_bitcast_fusion
  130.6 0.0 collective-permute-done.8
  130.6 0.2 broadcast_select_fusion.1
  130.8 0.0 copy-start.1
  130.8 0.2 pad_maximum_fusion
  131.0 2.0 %copy-done.1 = f32[2,1024,512]{2,1,0:T(8,128)S(1)} copy-done((f32[2,1024,512]{2,1,0:T(8,128)S(1)}, f32[2,1024,512]{2,1,0:T(8,128)}, u32[]{:S(2)}) %copy-start.1) | copy-done | bytes 4194328
  133.0 5.1 %bitcast_subtract_fusion = f32[2,1024,512]{2,1,0:T(8,128)} fusion(f32[2,1024,512]{2,1,0:T(8,128)S(1)} %copy-done.1, f32[1,2,512,256]{3,2,1,0:T(8,128)S(1)} %get-tuple-element.17, f32[1,2,512,256]{3,2,1,0:T(8,128)S(1)} %get-tuple-element.16, f32[2,1024,256]{2,1,0:T(8,128)S(1)} %bitcast.55), kind=kOutput, calls=%fused_computation | convolution fusion | flops 3222798336 | bytes 12582912 | tf_op jit(solution)/shard_map/dot_general | solution.py:115
  (2 shorter events, 0.1 us)
Async XLA Ops:
  0.6 5.3 %copy-start.2 = (f32[2,128,256]{2,1,0:T(8,128)S(1)}, f32[2,128,256]{2,1,0:T(8,128)}, u32[]{:S(2)}) copy-start(f32[2,128,256]{2,1,0:T(8,128)} %param.4) | copy-start | bytes 786436
  0.6 5.3 %copy-start = (f32[2,256,256]{2,1,0:T(8,128)S(1)}, f32[2,256,256]{2,1,0:T(8,128)}, u32[]{:S(2)}) copy-start(f32[2,256,256]{2,1,0:T(8,128)} %param.5) | copy-start | bytes 1572868
  0.6 1.5 %collective-permute-start = (f32[2,128,256]{2,1,0:T(8,128)}, f32[2,128,256]{2,1,0:T(8,128)S(1)}, u32[]{:S(2)}, u32[]{:S(2)}) collective-permute-start(f32[2,128,256]{2,1,0:T(8,128)} %param.4), channel_id=1, source_target_pairs={{0,192},{1,193},{2,194},{3,195},{4,196},{5,197},{6,198},{7,199},{8... | collective-permute-start | bytes 786440 | tf_op jit(solution)/shard_map/ppermute | solution.py:89
  1.5 0.7 collective-permute-start.1
  3.2 1.4 %collective-permute-start.2 = (f32[2,128,256]{2,1,0:T(8,128)S(1)}, f32[2,128,256]{2,1,0:T(8,128)S(1)}, u32[]{:S(2)}, u32[]{:S(2)}) collective-permute-start(f32[2,128,256]{2,1,0:T(8,128)S(1)} %select_select_fusion.10), channel_id=1, source_target_pairs={{64,96},{65,97},{66,98},{67,99},{68,100},{69,101},{70,102},{71,103... | collective-permute-start | bytes 786440 | tf_op jit(solution)/shard_map/ppermute | solution.py:95
  3.9 0.7 collective-permute-start.3
  4.7 23.8 %collective-permute-start.4 = (f32[2,128,256]{2,1,0:T(8,128)S(1)}, f32[2,128,256]{2,1,0:T(8,128)S(1)}, u32[]{:S(2)}, u32[]{:S(2)}) collective-permute-start(f32[2,128,256]{2,1,0:T(8,128)S(1)} %fusion.9), channel_id=1, source_target_pairs={{96,160},{224,32},{97,161},{225,33},{98,162},{226,34},{99,163},{22... | collective-permute-start | bytes 786440 | tf_op jit(solution)/shard_map/ppermute | solution.py:95
  28.6 21.4 %collective-permute-start.5 = (f32[2,128,256]{2,1,0:T(8,128)S(1)}, f32[2,128,256]{2,1,0:T(8,128)S(1)}, u32[]{:S(2)}, u32[]{:S(2)}) collective-permute-start(f32[2,128,256]{2,1,0:T(8,128)S(1)} %copy-done.2), channel_id=1, source_target_pairs={{0,6},{2,0},{4,2},{6,4},{1,7},{3,1},{5,3},{7,5},{8,14},{10,8},{12,... | collective-permute-start | bytes 786440 | tf_op jit(solution)/shard_map/ppermute | solution.py:75
  33.3 33.2 %collective-permute-start.6 = (f32[2,128,256]{2,1,0:T(8,128)S(1)}, f32[2,128,256]{2,1,0:T(8,128)S(1)}, u32[]{:S(2)}, u32[]{:S(2)}) collective-permute-start(f32[2,128,256]{2,1,0:T(8,128)S(1)} %copy-done.2), channel_id=1, source_target_pairs={{0,4},{2,6},{4,0},{6,2},{1,5},{3,7},{5,1},{7,3},{8,12},{10,14},{12... | collective-permute-start | bytes 786440 | tf_op jit(solution)/shard_map/ppermute | solution.py:75
  43.9 24.6 %collective-permute-start.7 = (f32[2,128,256]{2,1,0:T(8,128)S(1)}, f32[2,128,256]{2,1,0:T(8,128)S(1)}, u32[]{:S(2)}, u32[]{:S(2)}) collective-permute-start(f32[2,128,256]{2,1,0:T(8,128)S(1)} %copy-done.2), channel_id=1, source_target_pairs={{0,2},{2,4},{4,6},{6,0},{1,3},{3,5},{5,7},{7,1},{8,10},{10,12},{12... | collective-permute-start | bytes 786440 | tf_op jit(solution)/shard_map/ppermute | solution.py:75
  47.3 42.0 %collective-permute-start.10 = (f32[2,128,256]{2,1,0:T(8,128)S(1)}, f32[2,128,256]{2,1,0:T(8,128)S(1)}, u32[]{:S(2)}, u32[]{:S(2)}) collective-permute-start(f32[2,128,256]{2,1,0:T(8,128)S(1)} %select_select_fusion), channel_id=1, source_target_pairs={{0,16},{1,24},{2,0},{3,8},{4,17},{5,25},{6,1},{7,9},{8,18},{9,26},... | collective-permute-start | bytes 786440 | tf_op jit(solution)/shard_map/ppermute | solution.py:99
  47.3 42.0 %collective-permute-start.11 = (f32[2,128,256]{2,1,0:T(8,128)S(1)}, f32[2,128,256]{2,1,0:T(8,128)S(1)}, u32[]{:S(2)}, u32[]{:S(2)}) collective-permute-start(f32[2,128,256]{2,1,0:T(8,128)S(1)} %select_select_fusion), channel_id=1, source_target_pairs={{0,8},{1,16},{2,24},{3,0},{4,9},{5,17},{6,25},{7,1},{8,10},{9,18},... | collective-permute-start | bytes 786440 | tf_op jit(solution)/shard_map/ppermute | solution.py:99
  50.0 72.7 %collective-permute-start.12 = (f32[2,128,256]{2,1,0:T(8,128)S(1)}, f32[2,128,256]{2,1,0:T(8,128)S(1)}, u32[]{:S(2)}, u32[]{:S(2)}) collective-permute-start(f32[2,128,256]{2,1,0:T(8,128)S(1)} %select_select_fusion), channel_id=1, source_target_pairs={{0,0},{1,8},{2,16},{3,24},{4,1},{5,9},{6,17},{7,25},{8,2},{9,10},{... | collective-permute-start | bytes 786440 | tf_op jit(solution)/shard_map/ppermute | solution.py:99
  66.5 62.1 %collective-permute-start.9 = (f32[2,128,256]{2,1,0:T(8,128)S(1)}, f32[2,128,256]{2,1,0:T(8,128)S(1)}, u32[]{:S(2)}, u32[]{:S(2)}) collective-permute-start(f32[2,128,256]{2,1,0:T(8,128)S(1)} %select_select_fusion), channel_id=1, source_target_pairs={{0,24},{1,0},{2,8},{3,16},{4,25},{5,1},{6,9},{7,17},{8,26},{9,2},{... | collective-permute-start | bytes 786440 | tf_op jit(solution)/shard_map/ppermute | solution.py:99
  68.8 61.8 %collective-permute-start.8 = (f32[2,512,256]{2,1,0:T(8,128)S(1)}, f32[2,512,256]{2,1,0:T(8,128)S(1)}, u32[]{:S(2)}, u32[]{:S(2)}) collective-permute-start(f32[2,512,256]{2,1,0:T(8,128)S(1)} %pad_maximum_fusion.1), channel_id=1, source_target_pairs={{0,1},{1,0},{2,3},{3,2},{4,5},{5,4},{6,7},{7,6},{8,9},{9,8},{10,11... | collective-permute-start | bytes 3145736 | tf_op jit(solution)/shard_map/ppermute | solution.py:103
  130.8 2.2 %copy-start.1 = (f32[2,1024,512]{2,1,0:T(8,128)S(1)}, f32[2,1024,512]{2,1,0:T(8,128)}, u32[]{:S(2)}) copy-start(f32[2,1024,512]{2,1,0:T(8,128)} %param.3) | copy-start | bytes 12582916

commit v11 on v5

--- a/solution.py
+++ b/solution.py
@@ -24,6 +24,12 @@
         left[1], right[0], dims, precision=hp
     )
     return jnp.stack([real_part, imag_part])
+
+
+def permute(value, axis, pairs, parts=2):
+    rows = value.shape[1] // parts
+    got = [lax.ppermute(value[:, i * rows:(i + 1) * rows], axis, pairs) for i in range(parts)]
+    return jnp.concatenate(got, axis=1)
 
 
 def make_local(sizes):
@@ -63,7 +69,7 @@
         return jnp.concatenate(out, axis=1)
 
     def gather(piece, axis, idx, n):
-        got = [piece] + [lax.ppermute(piece, axis, shifts(n, k)) for k in range(1, n)]
+        got = [piece] + [permute(piece, axis, shifts(n, k)) for k in range(1, n)]
         return reorder(got, idx, n)
 
     def local(trailing, panel, diag_inverse):
@@ -75,7 +81,7 @@
         li = lax.axis_index("zl")
         ci = lax.axis_index("core")
 
-        got_a = [lax.ppermute(panel, AXES, spread(y1, h1)) for y1, h1 in first]
+        got_a = [permute(panel, AXES, spread(y1, h1)) for y1, h1 in first]
         held_a = got_a[0]
         for (y1, h1), got in zip(first[1:], got_a[1:]):
             held_a = jnp.where((yi == y1) & (hi == h1), got, held_a)
@@ -83,14 +89,14 @@
         for stage in relays:
             sent = held
             for pairs in stage:
-                got = lax.ppermute(sent, ("y", "zh"), [(plane(h0, y0), plane(h1, y1)) for (y0, h0), (y1, h1) in pairs])
+                got = permute(sent, ("y", "zh"), [(plane(h0, y0), plane(h1, y1)) for (y0, h0), (y1, h1) in pairs])
                 for _, (y1, h1) in pairs:
                     held = jnp.where((yi == y1) & (hi == h1), got, held)
         panel_late, held = lax.optimization_barrier((panel, held))
         window = gather(held, "x", xi, nx)
 
         mine = gather(panel_late, "zl", li, nl)
-        other = lax.ppermute(mine, "core", shifts(nc, 1))
+        other = permute(mine, "core", shifts(nc, 1))
         lo = jnp.where(ci == 0, mine, other)
         hi_ = jnp.where(ci == 0, other, mine)
         two, rows, width = mine.shape[0], panel.shape[1], mine.shape[2]

time: 102 us -> 114 us (1.12)
  the two profiles are of different devices: /device:TPU:7 before, /device:TPU:145 now
where the time goes in v11:
time: 114 us
  waiting for transfers between devices  51.6 us (45%)
  starting transfers between devices  46.2 us (41%)
  matrix products  9.74 us (9%)
  local copies, waits for them, and re-layouts  3.36 us (3%)
  other arithmetic  1.85 us (2%)
  between operations  1.22 us (1%)
    ppermute x26, waiting for transfers between devices, permute(): lax.ppermute(value[:, i * rows:(i + 1) * rows], axis, pairs)  51.6 us
    ppermute x26, starting transfers between devices, permute(): lax.ppermute(value[:, i * rows:(i + 1) * rows], axis, pairs)  46.2 us
    dot_general x1, matrix products, local(): product = lax.dot_general(lhs, rhs, dims, precision=lax.Precision.HIGH)  5.06 us
  transfers between devices with their start and end apart: 26, of which 7 were waited for; matrix products, arithmetic and copies ran while one was open for 5% of the time, Pallas kernels for 0%

profile of v11, /device:TPU:145, one launch (start us, length us, event | category | flops | bytes accessed | tf_op | source)
XLA Modules:
  0.0 113.9 jit_solution(5949907252855121992)
XLA Ops:
  0.6 0.0 copy-start.1
  0.6 0.0 copy-start
  0.7 1.1 fusion.43
  1.7 0.7 collective-permute-start
  2.4 0.7 collective-permute-start.2
  3.1 0.7 collective-permute-start.1
  3.7 0.7 collective-permute-start.3
  4.4 0.7 collective-permute-start.4
  5.1 1.3 %fusion.14 = f32[128,256]{1,0:T(8,128)S(1)} fusion(f32[2,256,256]{2,1,0:T(8,128)} %param.5, f32[2,128,256]{2,1,0:T(8,128)} %param.4), kind=kOutput, calls=%fused_computation.34 | convolution fusion | flops 100663296 | bytes 524288 | tf_op jit(solution)/shard_map/dot_general | solution.py:14
  6.4 0.7 collective-permute-start.5
  7.1 1.3 %fusion.20 = f32[128,256]{1,0:T(8,128)S(1)} fusion(f32[2,256,256]{2,1,0:T(8,128)} %param.5, f32[2,128,256]{2,1,0:T(8,128)} %param.4), kind=kOutput, calls=%fused_computation.40 | convolution fusion | flops 100663296 | bytes 524288 | tf_op jit(solution)/shard_map/dot_general | solution.py:13
  8.4 0.0 collective-permute-done.1
  8.4 0.0 collective-permute-done.2
  8.5 0.0 collective-permute-done.4
  8.5 0.0 collective-permute-done.5
  8.5 0.1 maximum_select_fusion
  8.6 0.7 collective-permute-start.8
  9.2 0.7 collective-permute-start.9
  9.9 0.3 fusion.5
  10.3 0.7 collective-permute-start.6
  10.9 0.7 collective-permute-start.7
  11.6 0.0 collective-permute-done.9
  11.7 0.0 collective-permute-done.6
  11.7 0.0 collective-permute-done.7
  11.7 0.1 fusion.11
  11.8 1.3 %collective-permute-start.10 = (f32[2,64,256]{2,1,0:T(8,128)S(1)}, f32[2,64,256]{2,1,0:T(8,128)S(1)}, u32[]{:S(2)}, u32[]{:S(2)}) collective-permute-start(f32[2,64,256]{2,1,0:T(8,128)S(1)} %get-tuple-element.23), channel_id=1, source_target_pairs={{96,160},{224,32},{97,161},{225,33},{98,162},{226,34},{99,163},{22... | collective-permute-start | bytes 393224 | tf_op jit(solution)/shard_map/ppermute | solution.py:31
  13.1 0.3 fusion.6
  13.4 1.3 %collective-permute-start.11 = (f32[2,64,256]{2,1,0:T(8,128)S(1)}, f32[2,64,256]{2,1,0:T(8,128)S(1)}, u32[]{:S(2)}, u32[]{:S(2)}) collective-permute-start(f32[2,64,256]{2,1,0:T(8,128)S(1)} %get-tuple-element.22), channel_id=1, source_target_pairs={{96,160},{224,32},{97,161},{225,33},{98,162},{226,34},{99,163},{22... | collective-permute-start | bytes 393224 | tf_op jit(solution)/shard_map/ppermute | solution.py:31
  14.7 0.7 pad_maximum_fusion.5
  15.4 32.8 %collective-permute-done.10 = f32[2,64,256]{2,1,0:T(8,128)S(1)} collective-permute-done((f32[2,64,256]{2,1,0:T(8,128)S(1)}, f32[2,64,256]{2,1,0:T(8,128)S(1)}, u32[]{:S(2)}, u32[]{:S(2)}) %collective-permute-start.10) | collective-permute-done | bytes 131104 | tf_op jit(solution)/shard_map/ppermute | solution.py:31
  48.2 1.6 %collective-permute-done.11 = f32[2,64,256]{2,1,0:T(8,128)S(1)} collective-permute-done((f32[2,64,256]{2,1,0:T(8,128)S(1)}, f32[2,64,256]{2,1,0:T(8,128)S(1)}, u32[]{:S(2)}, u32[]{:S(2)}) %collective-permute-start.11) | collective-permute-done | bytes 131104 | tf_op jit(solution)/shard_map/ppermute | solution.py:31
  49.9 1.9 %collective-permute-start.24 = (f32[2,64,256]{2,1,0:T(8,128)S(1)}, f32[2,64,256]{2,1,0:T(8,128)S(1)}, u32[]{:S(2)}, u32[]{:S(2)}) collective-permute-start(f32[2,64,256]{2,1,0:T(8,128)S(1)} %get-tuple-element.21), channel_id=1, source_target_pairs={{0,8},{8,16},{16,24},{24,0},{1,9},{9,17},{17,25},{25,1},{2,10},{10... | collective-permute-start | bytes 393224 | tf_op jit(solution)/shard_map/ppermute | solution.py:31
  51.8 0.0 collective-permute-start.22
  51.8 21.7 %collective-permute-start.12 = (f32[2,64,256]{2,1,0:T(8,128)S(1)}, f32[2,64,256]{2,1,0:T(8,128)S(1)}, u32[]{:S(2)}, u32[]{:S(2)}) collective-permute-start(f32[2,64,256]{2,1,0:T(8,128)S(1)} %get-tuple-element.19), channel_id=1, source_target_pairs={{0,6},{2,0},{4,2},{6,4},{1,7},{3,1},{5,3},{7,5},{8,14},{10,8},{12,... | collective-permute-start | bytes 393224 | tf_op jit(solution)/shard_map/ppermute | solution.py:31
  73.5 2.5 %collective-permute-start.20 = (f32[2,64,256]{2,1,0:T(8,128)S(1)}, f32[2,64,256]{2,1,0:T(8,128)S(1)}, u32[]{:S(2)}, u32[]{:S(2)}) collective-permute-start(f32[2,64,256]{2,1,0:T(8,128)S(1)} %get-tuple-element.21), channel_id=1, source_target_pairs={{0,24},{8,0},{16,8},{24,16},{1,25},{9,1},{17,9},{25,17},{2,26},{10... | collective-permute-start | bytes 393224 | tf_op jit(solution)/shard_map/ppermute | solution.py:31
  76.0 0.0 collective-permute-done.24
  76.0 0.0 collective-permute-start.25
  76.1 2.0 %collective-permute-start.23 = (f32[2,64,256]{2,1,0:T(8,128)S(1)}, f32[2,64,256]{2,1,0:T(8,128)S(1)}, u32[]{:S(2)}, u32[]{:S(2)}) collective-permute-start(f32[2,64,256]{2,1,0:T(8,128)S(1)} %get-tuple-element.20), channel_id=1, source_target_pairs={{0,16},{8,24},{16,0},{24,8},{1,17},{9,25},{17,1},{25,9},{2,18},{10... | collective-permute-start | bytes 393224 | tf_op jit(solution)/shard_map/ppermute | solution.py:31
  78.1 0.8 collective-permute-done.20
  78.9 3.3 %collective-permute-start.21 = (f32[2,64,256]{2,1,0:T(8,128)S(1)}, f32[2,64,256]{2,1,0:T(8,128)S(1)}, u32[]{:S(2)}, u32[]{:S(2)}) collective-permute-start(f32[2,64,256]{2,1,0:T(8,128)S(1)} %get-tuple-element.20), channel_id=1, source_target_pairs={{0,24},{8,0},{16,8},{24,16},{1,25},{9,1},{17,9},{25,17},{2,26},{10... | collective-permute-start | bytes 393224 | tf_op jit(solution)/shard_map/ppermute | solution.py:31
  82.2 3.3 %collective-permute-done.25 = f32[2,64,256]{2,1,0:T(8,128)S(1)} collective-permute-done((f32[2,64,256]{2,1,0:T(8,128)S(1)}, f32[2,64,256]{2,1,0:T(8,128)S(1)}, u32[]{:S(2)}, u32[]{:S(2)}) %collective-permute-start.25) | collective-permute-done | bytes 131104 | tf_op jit(solution)/shard_map/ppermute | solution.py:31
  85.5 0.0 collective-permute-start.13
  85.5 2.5 %collective-permute-start.15 = (f32[2,64,256]{2,1,0:T(8,128)S(1)}, f32[2,64,256]{2,1,0:T(8,128)S(1)}, u32[]{:S(2)}, u32[]{:S(2)}) collective-permute-start(f32[2,64,256]{2,1,0:T(8,128)S(1)} %get-tuple-element.18), channel_id=1, source_target_pairs={{0,4},{2,6},{4,0},{6,2},{1,5},{3,7},{5,1},{7,3},{8,12},{10,14},{12... | collective-permute-start | bytes 393224 | tf_op jit(solution)/shard_map/ppermute | solution.py:31
  88.1 1.5 %collective-permute-start.16 = (f32[2,64,256]{2,1,0:T(8,128)S(1)}, f32[2,64,256]{2,1,0:T(8,128)S(1)}, u32[]{:S(2)}, u32[]{:S(2)}) collective-permute-start(f32[2,64,256]{2,1,0:T(8,128)S(1)} %get-tuple-element.19), channel_id=1, source_target_pairs={{0,2},{2,4},{4,6},{6,0},{1,3},{3,5},{5,7},{7,1},{8,10},{10,12},{12... | collective-permute-start | bytes 393224 | tf_op jit(solution)/shard_map/ppermute | solution.py:31
  89.6 0.1 select_select_fusion.5
  89.7 0.1 pad_maximum_fusion.2
  89.8 0.4 fusion.10
  90.2 0.4 fusion.9
  90.6 0.1 collective-permute-start.17
  90.7 0.0 collective-permute-done.14
  90.8 7.2 %collective-permute-done.16 = f32[2,64,256]{2,1,0:T(8,128)S(1)} collective-permute-done((f32[2,64,256]{2,1,0:T(8,128)S(1)}, f32[2,64,256]{2,1,0:T(8,128)S(1)}, u32[]{:S(2)}, u32[]{:S(2)}) %collective-permute-start.16) | collective-permute-done | bytes 131104 | tf_op jit(solution)/shard_map/ppermute | solution.py:31
  98.0 4.6 %collective-permute-done.15 = f32[2,64,256]{2,1,0:T(8,128)S(1)} collective-permute-done((f32[2,64,256]{2,1,0:T(8,128)S(1)}, f32[2,64,256]{2,1,0:T(8,128)S(1)}, u32[]{:S(2)}, u32[]{:S(2)}) %collective-permute-start.15) | collective-permute-done | bytes 131104 | tf_op jit(solution)/shard_map/ppermute | solution.py:31
  102.7 0.1 select_select_fusion.7
  102.8 1.2 %collective-permute-start.19 = (f32[2,256,256]{2,1,0:T(8,128)S(1)}, f32[2,256,256]{2,1,0:T(8,128)S(1)}, u32[]{:S(2)}, u32[]{:S(2)}) collective-permute-start(f32[2,256,256]{2,1,0:T(8,128)S(1)} %pad_maximum_fusion.4), channel_id=1, source_target_pairs={{0,1},{1,0},{2,3},{3,2},{4,5},{5,4},{6,7},{7,6},{8,9},{9,8},{10,11... | collective-permute-start | bytes 1572872 | tf_op jit(solution)/shard_map/ppermute | solution.py:31
  104.1 0.1 collective-permute-start.18
  104.2 0.4 convolution_add_fusion
  104.6 0.4 fusion.4
  105.1 0.2 maximum_bitcast_fusion
  105.2 1.1 %collective-permute-done.18 = f32[2,256,256]{2,1,0:T(8,128)S(1)} collective-permute-done((f32[2,256,256]{2,1,0:T(8,128)S(1)}, f32[2,256,256]{2,1,0:T(8,128)S(1)}, u32[]{:S(2)}, u32[]{:S(2)}) %collective-permute-start.18) | collective-permute-done | bytes 524320 | tf_op jit(solution)/shard_map/ppermute | solution.py:31
  106.5 0.2 fusion.8
  106.7 0.0 copy-start.2
  106.7 0.2 pad_maximum_fusion
  106.9 2.0 %copy-done.2 = f32[2,1024,512]{2,1,0:T(8,128)S(1)} copy-done((f32[2,1024,512]{2,1,0:T(8,128)S(1)}, f32[2,1024,512]{2,1,0:T(8,128)}, u32[]{:S(2)}) %copy-start.2) | copy-done | bytes 4194328
  108.9 5.1 %bitcast_subtract_fusion = f32[2,1024,512]{2,1,0:T(8,128)} fusion(f32[2,1024,512]{2,1,0:T(8,128)S(1)} %copy-done.2, f32[1,2,512,256]{3,2,1,0:T(8,128)S(1)} %get-tuple-element.17, f32[1,2,512,256]{3,2,1,0:T(8,128)S(1)} %get-tuple-element.16, f32[2,1024,256]{2,1,0:T(8,128)S(1)} %bitcast.55), kind=kOutput, calls=%fused_computation | convolution fusion | flops 3222798336 | bytes 12582912 | tf_op jit(solution)/shard_map/dot_general | solution.py:111
  (39 shorter events, 0.5 us)
Async XLA Ops:
  0.6 9.3 %copy-start.1 = (f32[2,128,256]{2,1,0:T(8,128)S(1)}, f32[2,128,256]{2,1,0:T(8,128)}, u32[]{:S(2)}) copy-start(f32[2,128,256]{2,1,0:T(8,128)} %param.4) | copy-start | bytes 786436
  0.6 9.3 %copy-start = (f32[2,256,256]{2,1,0:T(8,128)S(1)}, f32[2,256,256]{2,1,0:T(8,128)}, u32[]{:S(2)}) copy-start(f32[2,256,256]{2,1,0:T(8,128)} %param.5) | copy-start | bytes 1572868
  1.7 4.7 %collective-permute-start = (f32[2,64,256]{2,1,0:T(8,128)S(1)}, f32[2,64,256]{2,1,0:T(8,128)S(1)}, u32[]{:S(2)}, u32[]{:S(2)}) collective-permute-start(f32[2,64,256]{2,1,0:T(8,128)S(1)} %get-tuple-element.26), channel_id=1, source_target_pairs={{0,192},{1,200},{2,208},{3,216},{4,193},{5,201},{6,209},{7,217},{8... | collective-permute-start | bytes 393224 | tf_op jit(solution)/shard_map/ppermute | solution.py:31
  2.4 6.0 %collective-permute-start.2 = (f32[2,64,256]{2,1,0:T(8,128)S(1)}, f32[2,64,256]{2,1,0:T(8,128)S(1)}, u32[]{:S(2)}, u32[]{:S(2)}) collective-permute-start(f32[2,64,256]{2,1,0:T(8,128)S(1)} %get-tuple-element.26), channel_id=1, source_target_pairs={{0,64},{1,72},{2,80},{3,88},{4,65},{5,73},{6,81},{7,89},{8,66},{9,... | collective-permute-start | bytes 393224 | tf_op jit(solution)/shard_map/ppermute | solution.py:31
  3.1 5.4 %collective-permute-start.1 = (f32[2,64,256]{2,1,0:T(8,128)S(1)}, f32[2,64,256]{2,1,0:T(8,128)S(1)}, u32[]{:S(2)}, u32[]{:S(2)}) collective-permute-start(f32[2,64,256]{2,1,0:T(8,128)S(1)} %get-tuple-element.27), channel_id=1, source_target_pairs={{0,192},{1,200},{2,208},{3,216},{4,193},{5,201},{6,209},{7,217},{8... | collective-permute-start | bytes 393224 | tf_op jit(solution)/shard_map/ppermute | solution.py:31
  3.7 4.7 %collective-permute-start.3 = (f32[2,64,256]{2,1,0:T(8,128)S(1)}, f32[2,64,256]{2,1,0:T(8,128)S(1)}, u32[]{:S(2)}, u32[]{:S(2)}) collective-permute-start(f32[2,64,256]{2,1,0:T(8,128)S(1)} %get-tuple-element.27), channel_id=1, source_target_pairs={{0,64},{1,72},{2,80},{3,88},{4,65},{5,73},{6,81},{7,89},{8,66},{9,... | collective-permute-start | bytes 393224 | tf_op jit(solution)/shard_map/ppermute | solution.py:31
  4.4 4.0 %collective-permute-start.4 = (f32[2,64,256]{2,1,0:T(8,128)S(1)}, f32[2,64,256]{2,1,0:T(8,128)S(1)}, u32[]{:S(2)}, u32[]{:S(2)}) collective-permute-start(f32[2,64,256]{2,1,0:T(8,128)S(1)} %get-tuple-element.26), channel_id=1, source_target_pairs={{0,0},{1,8},{2,16},{3,24},{4,1},{5,9},{6,17},{7,25},{8,2},{9,10},{... | collective-permute-start | bytes 393224 | tf_op jit(solution)/shard_map/ppermute | solution.py:31
  6.4 2.0 %collective-permute-start.5 = (f32[2,64,256]{2,1,0:T(8,128)S(1)}, f32[2,64,256]{2,1,0:T(8,128)S(1)}, u32[]{:S(2)}, u32[]{:S(2)}) collective-permute-start(f32[2,64,256]{2,1,0:T(8,128)S(1)} %get-tuple-element.27), channel_id=1, source_target_pairs={{0,0},{1,8},{2,16},{3,24},{4,1},{5,9},{6,17},{7,25},{8,2},{9,10},{... | collective-permute-start | bytes 393224 | tf_op jit(solution)/shard_map/ppermute | solution.py:31
  8.6 3.0 %collective-permute-start.8 = (f32[2,64,256]{2,1,0:T(8,128)S(1)}, f32[2,64,256]{2,1,0:T(8,128)S(1)}, u32[]{:S(2)}, u32[]{:S(2)}) collective-permute-start(f32[2,64,256]{2,1,0:T(8,128)S(1)} %get-tuple-element.25), channel_id=1, source_target_pairs={{64,128},{192,224},{65,129},{193,225},{66,130},{194,226},{67,131},... | collective-permute-start | bytes 393224 | tf_op jit(solution)/shard_map/ppermute | solution.py:31
  9.2 2.4 %collective-permute-start.9 = (f32[2,64,256]{2,1,0:T(8,128)S(1)}, f32[2,64,256]{2,1,0:T(8,128)S(1)}, u32[]{:S(2)}, u32[]{:S(2)}) collective-permute-start(f32[2,64,256]{2,1,0:T(8,128)S(1)} %get-tuple-element.24), channel_id=1, source_target_pairs={{64,128},{192,224},{65,129},{193,225},{66,130},{194,226},{67,131},... | collective-permute-start | bytes 393224 | tf_op jit(solution)/shard_map/ppermute | solution.py:31
  10.3 1.4 %collective-permute-start.6 = (f32[2,64,256]{2,1,0:T(8,128)S(1)}, f32[2,64,256]{2,1,0:T(8,128)S(1)}, u32[]{:S(2)}, u32[]{:S(2)}) collective-permute-start(f32[2,64,256]{2,1,0:T(8,128)S(1)} %get-tuple-element.25), channel_id=1, source_target_pairs={{64,96},{65,97},{66,98},{67,99},{68,100},{69,101},{70,102},{71,103... | collective-permute-start | bytes 393224 | tf_op jit(solution)/shard_map/ppermute | solution.py:31
  10.9 0.7 collective-permute-start.7
  11.8 36.4 %collective-permute-start.10 = (f32[2,64,256]{2,1,0:T(8,128)S(1)}, f32[2,64,256]{2,1,0:T(8,128)S(1)}, u32[]{:S(2)}, u32[]{:S(2)}) collective-permute-start(f32[2,64,256]{2,1,0:T(8,128)S(1)} %get-tuple-element.23), channel_id=1, source_target_pairs={{96,160},{224,32},{97,161},{225,33},{98,162},{226,34},{99,163},{22... | collective-permute-start | bytes 393224 | tf_op jit(solution)/shard_map/ppermute | solution.py:31
  13.4 36.5 %collective-permute-start.11 = (f32[2,64,256]{2,1,0:T(8,128)S(1)}, f32[2,64,256]{2,1,0:T(8,128)S(1)}, u32[]{:S(2)}, u32[]{:S(2)}) collective-permute-start(f32[2,64,256]{2,1,0:T(8,128)S(1)} %get-tuple-element.22), channel_id=1, source_target_pairs={{96,160},{224,32},{97,161},{225,33},{98,162},{226,34},{99,163},{22... | collective-permute-start | bytes 393224 | tf_op jit(solution)/shard_map/ppermute | solution.py:31
  49.9 26.1 %collective-permute-start.24 = (f32[2,64,256]{2,1,0:T(8,128)S(1)}, f32[2,64,256]{2,1,0:T(8,128)S(1)}, u32[]{:S(2)}, u32[]{:S(2)}) collective-permute-start(f32[2,64,256]{2,1,0:T(8,128)S(1)} %get-tuple-element.21), channel_id=1, source_target_pairs={{0,8},{8,16},{16,24},{24,0},{1,9},{9,17},{17,25},{25,1},{2,10},{10... | collective-permute-start | bytes 393224 | tf_op jit(solution)/shard_map/ppermute | solution.py:31
  51.8 24.3 %collective-permute-start.22 = (f32[2,64,256]{2,1,0:T(8,128)S(1)}, f32[2,64,256]{2,1,0:T(8,128)S(1)}, u32[]{:S(2)}, u32[]{:S(2)}) collective-permute-start(f32[2,64,256]{2,1,0:T(8,128)S(1)} %get-tuple-element.21), channel_id=1, source_target_pairs={{0,16},{8,24},{16,0},{24,8},{1,17},{9,25},{17,1},{25,9},{2,18},{10... | collective-permute-start | bytes 393224 | tf_op jit(solution)/shard_map/ppermute | solution.py:31
  51.8 38.8 %collective-permute-start.12 = (f32[2,64,256]{2,1,0:T(8,128)S(1)}, f32[2,64,256]{2,1,0:T(8,128)S(1)}, u32[]{:S(2)}, u32[]{:S(2)}) collective-permute-start(f32[2,64,256]{2,1,0:T(8,128)S(1)} %get-tuple-element.19), channel_id=1, source_target_pairs={{0,6},{2,0},{4,2},{6,4},{1,7},{3,1},{5,3},{7,5},{8,14},{10,8},{12,... | collective-permute-start | bytes 393224 | tf_op jit(solution)/shard_map/ppermute | solution.py:31
  73.5 17.2 %collective-permute-start.14 = (f32[2,64,256]{2,1,0:T(8,128)S(1)}, f32[2,64,256]{2,1,0:T(8,128)S(1)}, u32[]{:S(2)}, u32[]{:S(2)}) collective-permute-start(f32[2,64,256]{2,1,0:T(8,128)S(1)} %get-tuple-element.19), channel_id=1, source_target_pairs={{0,4},{2,6},{4,0},{6,2},{1,5},{3,7},{5,1},{7,3},{8,12},{10,14},{12... | collective-permute-start | bytes 393224 | tf_op jit(solution)/shard_map/ppermute | solution.py:31
  73.5 5.3 %collective-permute-start.20 = (f32[2,64,256]{2,1,0:T(8,128)S(1)}, f32[2,64,256]{2,1,0:T(8,128)S(1)}, u32[]{:S(2)}, u32[]{:S(2)}) collective-permute-start(f32[2,64,256]{2,1,0:T(8,128)S(1)} %get-tuple-element.21), channel_id=1, source_target_pairs={{0,24},{8,0},{16,8},{24,16},{1,25},{9,1},{17,9},{25,17},{2,26},{10... | collective-permute-start | bytes 393224 | tf_op jit(solution)/shard_map/ppermute | solution.py:31
  76.0 9.5 %collective-permute-start.25 = (f32[2,64,256]{2,1,0:T(8,128)S(1)}, f32[2,64,256]{2,1,0:T(8,128)S(1)}, u32[]{:S(2)}, u32[]{:S(2)}) collective-permute-start(f32[2,64,256]{2,1,0:T(8,128)S(1)} %get-tuple-element.20), channel_id=1, source_target_pairs={{0,8},{8,16},{16,24},{24,0},{1,9},{9,17},{17,25},{25,1},{2,10},{10... | collective-permute-start | bytes 393224 | tf_op jit(solution)/shard_map/ppermute | solution.py:31
  76.1 9.5 %collective-permute-start.23 = (f32[2,64,256]{2,1,0:T(8,128)S(1)}, f32[2,64,256]{2,1,0:T(8,128)S(1)}, u32[]{:S(2)}, u32[]{:S(2)}) collective-permute-start(f32[2,64,256]{2,1,0:T(8,128)S(1)} %get-tuple-element.20), channel_id=1, source_target_pairs={{0,16},{8,24},{16,0},{24,8},{1,17},{9,25},{17,1},{25,9},{2,18},{10... | collective-permute-start | bytes 393224 | tf_op jit(solution)/shard_map/ppermute | solution.py:31
  78.9 9.2 %collective-permute-start.21 = (f32[2,64,256]{2,1,0:T(8,128)S(1)}, f32[2,64,256]{2,1,0:T(8,128)S(1)}, u32[]{:S(2)}, u32[]{:S(2)}) collective-permute-start(f32[2,64,256]{2,1,0:T(8,128)S(1)} %get-tuple-element.20), channel_id=1, source_target_pairs={{0,24},{8,0},{16,8},{24,16},{1,25},{9,1},{17,9},{25,17},{2,26},{10... | collective-permute-start | bytes 393224 | tf_op jit(solution)/shard_map/ppermute | solution.py:31
  85.5 12.5 %collective-permute-start.13 = (f32[2,64,256]{2,1,0:T(8,128)S(1)}, f32[2,64,256]{2,1,0:T(8,128)S(1)}, u32[]{:S(2)}, u32[]{:S(2)}) collective-permute-start(f32[2,64,256]{2,1,0:T(8,128)S(1)} %get-tuple-element.18), channel_id=1, source_target_pairs={{0,6},{2,0},{4,2},{6,4},{1,7},{3,1},{5,3},{7,5},{8,14},{10,8},{12,... | collective-permute-start | bytes 393224 | tf_op jit(solution)/shard_map/ppermute | solution.py:31
  85.5 17.1 %collective-permute-start.15 = (f32[2,64,256]{2,1,0:T(8,128)S(1)}, f32[2,64,256]{2,1,0:T(8,128)S(1)}, u32[]{:S(2)}, u32[]{:S(2)}) collective-permute-start(f32[2,64,256]{2,1,0:T(8,128)S(1)} %get-tuple-element.18), channel_id=1, source_target_pairs={{0,4},{2,6},{4,0},{6,2},{1,5},{3,7},{5,1},{7,3},{8,12},{10,14},{12... | collective-permute-start | bytes 393224 | tf_op jit(solution)/shard_map/ppermute | solution.py:31
  88.1 9.9 %collective-permute-start.16 = (f32[2,64,256]{2,1,0:T(8,128)S(1)}, f32[2,64,256]{2,1,0:T(8,128)S(1)}, u32[]{:S(2)}, u32[]{:S(2)}) collective-permute-start(f32[2,64,256]{2,1,0:T(8,128)S(1)} %get-tuple-element.19), channel_id=1, source_target_pairs={{0,2},{2,4},{4,6},{6,0},{1,3},{3,5},{5,7},{7,1},{8,10},{10,12},{12... | collective-permute-start | bytes 393224 | tf_op jit(solution)/shard_map/ppermute | solution.py:31
  90.6 12.0 %collective-permute-start.17 = (f32[2,64,256]{2,1,0:T(8,128)S(1)}, f32[2,64,256]{2,1,0:T(8,128)S(1)}, u32[]{:S(2)}, u32[]{:S(2)}) collective-permute-start(f32[2,64,256]{2,1,0:T(8,128)S(1)} %get-tuple-element.18), channel_id=1, source_target_pairs={{0,2},{2,4},{4,6},{6,0},{1,3},{3,5},{5,7},{7,1},{8,10},{10,12},{12... | collective-permute-start | bytes 393224 | tf_op jit(solution)/shard_map/ppermute | solution.py:31
  102.8 3.6 %collective-permute-start.19 = (f32[2,256,256]{2,1,0:T(8,128)S(1)}, f32[2,256,256]{2,1,0:T(8,128)S(1)}, u32[]{:S(2)}, u32[]{:S(2)}) collective-permute-start(f32[2,256,256]{2,1,0:T(8,128)S(1)} %pad_maximum_fusion.4), channel_id=1, source_target_pairs={{0,1},{1,0},{2,3},{3,2},{4,5},{5,4},{6,7},{7,6},{8,9},{9,8},{10,11... | collective-permute-start | bytes 1572872 | tf_op jit(solution)/shard_map/ppermute | solution.py:31
  104.1 2.2 %collective-permute-start.18 = (f32[2,256,256]{2,1,0:T(8,128)S(1)}, f32[2,256,256]{2,1,0:T(8,128)S(1)}, u32[]{:S(2)}, u32[]{:S(2)}) collective-permute-start(f32[2,256,256]{2,1,0:T(8,128)S(1)} %pad_maximum_fusion.3), channel_id=1, source_target_pairs={{0,1},{1,0},{2,3},{3,2},{4,5},{5,4},{6,7},{7,6},{8,9},{9,8},{10,11... | collective-permute-start | bytes 1572872 | tf_op jit(solution)/shard_map/ppermute | solution.py:31
  106.7 2.2 %copy-start.2 = (f32[2,1024,512]{2,1,0:T(8,128)S(1)}, f32[2,1024,512]{2,1,0:T(8,128)}, u32[]{:S(2)}) copy-start(f32[2,1024,512]{2,1,0:T(8,128)} %param.3) | copy-start | bytes 12582916

commit v12 on v5

--- a/solution.py
+++ b/solution.py
@@ -46,8 +46,8 @@
 
     first = [(0, 0), (1, 0), (ny - 1, 0)]
     relays = [
-        [[((1, 0), (2, 0)), ((ny - 1, 0), (ny - 1, 1))], [((1, 0), (1, 1))]],
-        [[((1, 1), (2, 1)), ((ny - 1, 1), (0, 1))]],
+        [[((1, 0), (2, 0)), ((ny - 1, 0), (ny - 1, 1))]],
+        [[((2, 0), (2, 1)), ((ny - 1, 1), (0, 1)), ((1, 0), (1, 1))]],
     ]
 
     def shifts(n, k):

time: 102 us -> 102 us (level)
  starting transfers between devices: 59.1 us -> 57.9 us
    dot_general x2, matrix products: 0.66 us -> 1.68 us  [complex_product(): jnp.dot(left[0], right[1], precision=hp)]
  transfers between devices with their start and end apart: 13 -> 12, of which waited for: 5 -> 5; matrix products, arithmetic and copies ran while one was open for 4% -> 5% of each run, Pallas kernels for 0% -> 0%
where the time goes in v12:
time: 102 us
  starting transfers between devices  57.9 us (57%)
  waiting for transfers between devices  30.4 us (30%)
  matrix products  8.71 us (9%)
  local copies, waits for them, and re-layouts  1.99 us (2%)
  other arithmetic  1.8 us (2%)
  between operations  1.1 us (1%)
    ppermute x6, starting transfers between devices, gather(): lax.ppermute(piece, axis, shifts(n, k))  42.3 us
    ppermute x6, waiting for transfers between devices, gather(): lax.ppermute(piece, axis, shifts(n, k))  16 us
    ppermute x3, waiting for transfers between devices, local(): got_a = [lax.ppermute(panel, AXES, spread(y1, h1)) for y1, h1 in first]  14.1 us
    ppermute x3, starting transfers between devices, local(): got_a = [lax.ppermute(panel, AXES, spread(y1, h1)) for y1, h1 in first]  13.5 us
    dot_general x1, matrix products, local(): product = lax.dot_general(lhs, rhs, dims, precision=lax.Precision.HIGH)  5.05 us
  transfers between devices with their start and end apart: 12, of which 5 were waited for; matrix products, arithmetic and copies ran while one was open for 5% of the time, Pallas kernels for 0%

profile of v12, /device:TPU:7, one launch (start us, length us, event | category | flops | bytes accessed | tf_op | source)
XLA Modules:
  0.0 101.8 jit_solution(15926751565742392833)
XLA Ops:
  0.6 0.0 copy-start.2
  0.6 0.0 copy-start
  0.7 10.3 %collective-permute-start = (f32[2,128,256]{2,1,0:T(8,128)}, f32[2,128,256]{2,1,0:T(8,128)S(1)}, u32[]{:S(2)}, u32[]{:S(2)}) collective-permute-start(f32[2,128,256]{2,1,0:T(8,128)} %param.4), channel_id=1, source_target_pairs={{0,192},{1,200},{2,208},{3,216},{4,193},{5,201},{6,209},{7,217},{8... | collective-permute-start | bytes 786440 | tf_op jit(solution)/shard_map/ppermute | solution.py:78
  10.9 1.3 %collective-permute-start.1 = (f32[2,128,256]{2,1,0:T(8,128)}, f32[2,128,256]{2,1,0:T(8,128)S(1)}, u32[]{:S(2)}, u32[]{:S(2)}) collective-permute-start(f32[2,128,256]{2,1,0:T(8,128)} %param.4), channel_id=1, source_target_pairs={{0,64},{1,72},{2,80},{3,88},{4,65},{5,73},{6,81},{7,89},{8,66},{9,... | collective-permute-start | bytes 786440 | tf_op jit(solution)/shard_map/ppermute | solution.py:78
  12.2 1.9 %collective-permute-start.2 = (f32[2,128,256]{2,1,0:T(8,128)}, f32[2,128,256]{2,1,0:T(8,128)S(1)}, u32[]{:S(2)}, u32[]{:S(2)}) collective-permute-start(f32[2,128,256]{2,1,0:T(8,128)} %param.4), channel_id=1, source_target_pairs={{0,0},{1,8},{2,16},{3,24},{4,1},{5,9},{6,17},{7,25},{8,2},{9,10},{... | collective-permute-start | bytes 786440 | tf_op jit(solution)/shard_map/ppermute | solution.py:78
  14.2 3.2 %collective-permute-done = f32[2,128,256]{2,1,0:T(8,128)S(1)} collective-permute-done((f32[2,128,256]{2,1,0:T(8,128)}, f32[2,128,256]{2,1,0:T(8,128)S(1)}, u32[]{:S(2)}, u32[]{:S(2)}) %collective-permute-start) | collective-permute-done | bytes 262176 | tf_op jit(solution)/shard_map/ppermute | solution.py:78
  17.4 5.6 %collective-permute-done.1 = f32[2,128,256]{2,1,0:T(8,128)S(1)} collective-permute-done((f32[2,128,256]{2,1,0:T(8,128)}, f32[2,128,256]{2,1,0:T(8,128)S(1)}, u32[]{:S(2)}, u32[]{:S(2)}) %collective-permute-start.1) | collective-permute-done | bytes 262176 | tf_op jit(solution)/shard_map/ppermute | solution.py:78
  23.0 5.3 %collective-permute-done.2 = f32[2,128,256]{2,1,0:T(8,128)S(1)} collective-permute-done((f32[2,128,256]{2,1,0:T(8,128)}, f32[2,128,256]{2,1,0:T(8,128)S(1)}, u32[]{:S(2)}, u32[]{:S(2)}) %collective-permute-start.2) | collective-permute-done | bytes 262176 | tf_op jit(solution)/shard_map/ppermute | solution.py:78
  28.3 0.7 collective-permute-start.3
  29.0 0.0 collective-permute-done.3
  29.1 0.7 collective-permute-start.4
  29.7 1.3 %fusion.11 = f32[128,256]{1,0:T(8,128)S(1)} fusion(f32[2,256,256]{2,1,0:T(8,128)} %param.5, f32[2,128,256]{2,1,0:T(8,128)} %param.4), kind=kOutput, calls=%fused_computation.29 | convolution fusion | flops 100663296 | bytes 524288 | tf_op jit(solution)/shard_map/dot_general | solution.py:14
  31.1 0.0 copy-done.2
  31.1 0.0 copy-done
  31.1 0.3 fusion.17
  31.4 0.0 collective-permute-done.4
  31.4 0.1 collective-permute-start.5
  31.5 36.3 %collective-permute-start.6 = (f32[2,128,256]{2,1,0:T(8,128)S(1)}, f32[2,128,256]{2,1,0:T(8,128)S(1)}, u32[]{:S(2)}, u32[]{:S(2)}) collective-permute-start(f32[2,128,256]{2,1,0:T(8,128)S(1)} %copy-done.2), channel_id=1, source_target_pairs={{0,4},{2,6},{4,0},{6,2},{1,5},{3,7},{5,1},{7,3},{8,12},{10,14},{12... | collective-permute-start | bytes 786440 | tf_op jit(solution)/shard_map/ppermute | solution.py:66
  67.8 1.4 %collective-permute-start.7 = (f32[2,128,256]{2,1,0:T(8,128)S(1)}, f32[2,128,256]{2,1,0:T(8,128)S(1)}, u32[]{:S(2)}, u32[]{:S(2)}) collective-permute-start(f32[2,128,256]{2,1,0:T(8,128)S(1)} %copy-done.2), channel_id=1, source_target_pairs={{0,2},{2,4},{4,6},{6,0},{1,3},{3,5},{5,7},{7,1},{8,10},{10,12},{12... | collective-permute-start | bytes 786440 | tf_op jit(solution)/shard_map/ppermute | solution.py:66
  69.2 0.3 fusion.5
  69.6 0.3 fusion.6
  69.9 0.7 pad_maximum_fusion.3
  70.6 3.1 %collective-permute-start.10 = (f32[2,128,256]{2,1,0:T(8,128)S(1)}, f32[2,128,256]{2,1,0:T(8,128)S(1)}, u32[]{:S(2)}, u32[]{:S(2)}) collective-permute-start(f32[2,128,256]{2,1,0:T(8,128)S(1)} %select_select_fusion), channel_id=1, source_target_pairs={{0,16},{8,24},{16,0},{24,8},{1,17},{9,25},{17,1},{25,9},{2,18},{10... | collective-permute-start | bytes 786440 | tf_op jit(solution)/shard_map/ppermute | solution.py:66
  73.8 0.0 collective-permute-start.11
  73.8 0.0 collective-permute-done.5
  73.8 1.5 %collective-permute-start.9 = (f32[2,128,256]{2,1,0:T(8,128)S(1)}, f32[2,128,256]{2,1,0:T(8,128)S(1)}, u32[]{:S(2)}, u32[]{:S(2)}) collective-permute-start(f32[2,128,256]{2,1,0:T(8,128)S(1)} %select_select_fusion), channel_id=1, source_target_pairs={{0,24},{8,0},{16,8},{24,16},{1,25},{9,1},{17,9},{25,17},{2,26},{10... | collective-permute-start | bytes 786440 | tf_op jit(solution)/shard_map/ppermute | solution.py:66
  75.2 16.0 %collective-permute-done.6 = f32[2,128,256]{2,1,0:T(8,128)S(1)} collective-permute-done((f32[2,128,256]{2,1,0:T(8,128)S(1)}, f32[2,128,256]{2,1,0:T(8,128)S(1)}, u32[]{:S(2)}, u32[]{:S(2)}) %collective-permute-start.6) | collective-permute-done | bytes 262176 | tf_op jit(solution)/shard_map/ppermute | solution.py:66
  91.2 0.0 collective-permute-done.7
  91.2 0.1 select_select_fusion.9
  91.3 0.1 pad_maximum_fusion.1
  91.4 0.7 collective-permute-start.8
  92.1 0.0 collective-permute-done.10
  92.1 0.0 collective-permute-done.11
  92.1 0.0 collective-permute-done.9
  92.1 0.1 select_select_fusion.5
  92.3 0.1 pad_maximum_fusion.2
  92.3 0.4 fusion.8
  92.7 0.4 fusion.4
  93.1 0.4 fusion.7
  93.5 0.4 convolution_add_fusion
  93.9 0.2 maximum_bitcast_fusion
  94.1 0.3 collective-permute-done.8
  94.4 0.2 broadcast_select_fusion.1
  94.6 0.0 copy-start.1
  94.6 0.2 pad_maximum_fusion
  94.8 2.0 %copy-done.1 = f32[2,1024,512]{2,1,0:T(8,128)S(1)} copy-done((f32[2,1024,512]{2,1,0:T(8,128)S(1)}, f32[2,1024,512]{2,1,0:T(8,128)}, u32[]{:S(2)}) %copy-start.1) | copy-done | bytes 4194328
  96.8 5.1 %bitcast_subtract_fusion = f32[2,1024,512]{2,1,0:T(8,128)} fusion(f32[2,1024,512]{2,1,0:T(8,128)S(1)} %copy-done.1, f32[1,2,512,256]{3,2,1,0:T(8,128)S(1)} %get-tuple-element.17, f32[1,2,512,256]{3,2,1,0:T(8,128)S(1)} %get-tuple-element.16, f32[2,1024,256]{2,1,0:T(8,128)S(1)} %bitcast.55), kind=kOutput, calls=%fused_computation | convolution fusion | flops 3222798336 | bytes 12582912 | tf_op jit(solution)/shard_map/dot_general | solution.py:105
  (4 shorter events, 0.2 us)
Async XLA Ops:
  0.6 30.4 %copy-start.2 = (f32[2,128,256]{2,1,0:T(8,128)S(1)}, f32[2,128,256]{2,1,0:T(8,128)}, u32[]{:S(2)}) copy-start(f32[2,128,256]{2,1,0:T(8,128)} %param.4) | copy-start | bytes 786436
  0.6 30.4 %copy-start = (f32[2,256,256]{2,1,0:T(8,128)S(1)}, f32[2,256,256]{2,1,0:T(8,128)}, u32[]{:S(2)}) copy-start(f32[2,256,256]{2,1,0:T(8,128)} %param.5) | copy-start | bytes 1572868
  0.7 16.7 %collective-permute-start = (f32[2,128,256]{2,1,0:T(8,128)}, f32[2,128,256]{2,1,0:T(8,128)S(1)}, u32[]{:S(2)}, u32[]{:S(2)}) collective-permute-start(f32[2,128,256]{2,1,0:T(8,128)} %param.4), channel_id=1, source_target_pairs={{0,192},{1,200},{2,208},{3,216},{4,193},{5,201},{6,209},{7,217},{8... | collective-permute-start | bytes 786440 | tf_op jit(solution)/shard_map/ppermute | solution.py:78
  10.9 12.1 %collective-permute-start.1 = (f32[2,128,256]{2,1,0:T(8,128)}, f32[2,128,256]{2,1,0:T(8,128)S(1)}, u32[]{:S(2)}, u32[]{:S(2)}) collective-permute-start(f32[2,128,256]{2,1,0:T(8,128)} %param.4), channel_id=1, source_target_pairs={{0,64},{1,72},{2,80},{3,88},{4,65},{5,73},{6,81},{7,89},{8,66},{9,... | collective-permute-start | bytes 786440 | tf_op jit(solution)/shard_map/ppermute | solution.py:78
  12.2 16.0 %collective-permute-start.2 = (f32[2,128,256]{2,1,0:T(8,128)}, f32[2,128,256]{2,1,0:T(8,128)S(1)}, u32[]{:S(2)}, u32[]{:S(2)}) collective-permute-start(f32[2,128,256]{2,1,0:T(8,128)} %param.4), channel_id=1, source_target_pairs={{0,0},{1,8},{2,16},{3,24},{4,1},{5,9},{6,17},{7,25},{8,2},{9,10},{... | collective-permute-start | bytes 786440 | tf_op jit(solution)/shard_map/ppermute | solution.py:78
  28.3 0.7 collective-permute-start.3
  29.1 2.3 %collective-permute-start.4 = (f32[2,128,256]{2,1,0:T(8,128)S(1)}, f32[2,128,256]{2,1,0:T(8,128)S(1)}, u32[]{:S(2)}, u32[]{:S(2)}) collective-permute-start(f32[2,128,256]{2,1,0:T(8,128)S(1)} %select_select_fusion.1), channel_id=1, source_target_pairs={{128,160},{224,32},{64,96},{129,161},{225,33},{65,97},{130,162},{2... | collective-permute-start | bytes 786440 | tf_op jit(solution)/shard_map/ppermute | solution.py:86
  31.4 42.3 %collective-permute-start.5 = (f32[2,128,256]{2,1,0:T(8,128)S(1)}, f32[2,128,256]{2,1,0:T(8,128)S(1)}, u32[]{:S(2)}, u32[]{:S(2)}) collective-permute-start(f32[2,128,256]{2,1,0:T(8,128)S(1)} %copy-done.2), channel_id=1, source_target_pairs={{0,6},{2,0},{4,2},{6,4},{1,7},{3,1},{5,3},{7,5},{8,14},{10,8},{12,... | collective-permute-start | bytes 786440 | tf_op jit(solution)/shard_map/ppermute | solution.py:66
  31.5 59.7 %collective-permute-start.6 = (f32[2,128,256]{2,1,0:T(8,128)S(1)}, f32[2,128,256]{2,1,0:T(8,128)S(1)}, u32[]{:S(2)}, u32[]{:S(2)}) collective-permute-start(f32[2,128,256]{2,1,0:T(8,128)S(1)} %copy-done.2), channel_id=1, source_target_pairs={{0,4},{2,6},{4,0},{6,2},{1,5},{3,7},{5,1},{7,3},{8,12},{10,14},{12... | collective-permute-start | bytes 786440 | tf_op jit(solution)/shard_map/ppermute | solution.py:66
  67.8 23.4 %collective-permute-start.7 = (f32[2,128,256]{2,1,0:T(8,128)S(1)}, f32[2,128,256]{2,1,0:T(8,128)S(1)}, u32[]{:S(2)}, u32[]{:S(2)}) collective-permute-start(f32[2,128,256]{2,1,0:T(8,128)S(1)} %copy-done.2), channel_id=1, source_target_pairs={{0,2},{2,4},{4,6},{6,0},{1,3},{3,5},{5,7},{7,1},{8,10},{10,12},{12... | collective-permute-start | bytes 786440 | tf_op jit(solution)/shard_map/ppermute | solution.py:66
  70.6 21.5 %collective-permute-start.10 = (f32[2,128,256]{2,1,0:T(8,128)S(1)}, f32[2,128,256]{2,1,0:T(8,128)S(1)}, u32[]{:S(2)}, u32[]{:S(2)}) collective-permute-start(f32[2,128,256]{2,1,0:T(8,128)S(1)} %select_select_fusion), channel_id=1, source_target_pairs={{0,16},{8,24},{16,0},{24,8},{1,17},{9,25},{17,1},{25,9},{2,18},{10... | collective-permute-start | bytes 786440 | tf_op jit(solution)/shard_map/ppermute | solution.py:66
  73.8 18.4 %collective-permute-start.11 = (f32[2,128,256]{2,1,0:T(8,128)S(1)}, f32[2,128,256]{2,1,0:T(8,128)S(1)}, u32[]{:S(2)}, u32[]{:S(2)}) collective-permute-start(f32[2,128,256]{2,1,0:T(8,128)S(1)} %select_select_fusion), channel_id=1, source_target_pairs={{0,8},{8,16},{16,24},{24,0},{1,9},{9,17},{17,25},{25,1},{2,10},{10... | collective-permute-start | bytes 786440 | tf_op jit(solution)/shard_map/ppermute | solution.py:66
  73.8 18.4 %collective-permute-start.9 = (f32[2,128,256]{2,1,0:T(8,128)S(1)}, f32[2,128,256]{2,1,0:T(8,128)S(1)}, u32[]{:S(2)}, u32[]{:S(2)}) collective-permute-start(f32[2,128,256]{2,1,0:T(8,128)S(1)} %select_select_fusion), channel_id=1, source_target_pairs={{0,24},{8,0},{16,8},{24,16},{1,25},{9,1},{17,9},{25,17},{2,26},{10... | collective-permute-start | bytes 786440 | tf_op jit(solution)/shard_map/ppermute | solution.py:66
  91.4 3.0 %collective-permute-start.8 = (f32[2,512,256]{2,1,0:T(8,128)S(1)}, f32[2,512,256]{2,1,0:T(8,128)S(1)}, u32[]{:S(2)}, u32[]{:S(2)}) collective-permute-start(f32[2,512,256]{2,1,0:T(8,128)S(1)} %pad_maximum_fusion.1), channel_id=1, source_target_pairs={{0,1},{1,0},{2,3},{3,2},{4,5},{5,4},{6,7},{7,6},{8,9},{9,8},{10,11... | collective-permute-start | bytes 3145736 | tf_op jit(solution)/shard_map/ppermute | solution.py:93
  94.6 2.2 %copy-start.1 = (f32[2,1024,512]{2,1,0:T(8,128)S(1)}, f32[2,1024,512]{2,1,0:T(8,128)}, u32[]{:S(2)}) copy-start(f32[2,1024,512]{2,1,0:T(8,128)} %param.3) | copy-start | bytes 12582916

commit v13 on v5

--- a/solution.py
+++ b/solution.py
@@ -88,6 +88,7 @@
                     held = jnp.where((yi == y1) & (hi == h1), got, held)
         panel_late, held = lax.optimization_barrier((panel, held))
         window = gather(held, "x", xi, nx)
+        panel_late, window = lax.optimization_barrier((panel_late, window))
 
         mine = gather(panel_late, "zl", li, nl)
         other = lax.ppermute(mine, "core", shifts(nc, 1))

time: 102 us -> 113 us (1.11)
  the two profiles are of different devices: /device:TPU:7 before, /device:TPU:33 now
where the time goes in v13:
time: 113 us
  waiting for transfers between devices  75.9 us (67%)
  starting transfers between devices  24.6 us (22%)
  matrix products  7.68 us (7%)
  local copies, waits for them, and re-layouts  1.98 us (2%)
  other arithmetic  1.81 us (2%)
    ppermute x3, waiting for transfers between devices, local(): got_a = [lax.ppermute(panel, AXES, spread(y1, h1)) for y1, h1 in first]  42.2 us
    ppermute x6, waiting for transfers between devices, gather(): lax.ppermute(piece, axis, shifts(n, k))  32.8 us
    ppermute x3, starting transfers between devices, local(): got_a = [lax.ppermute(panel, AXES, spread(y1, h1)) for y1, h1 in first]  14.8 us
    ppermute x6, starting transfers between devices, gather(): lax.ppermute(piece, axis, shifts(n, k))  7.14 us
    dot_general x1, matrix products, local(): product = lax.dot_general(lhs, rhs, dims, precision=lax.Precision.HIGH)  5.06 us
  transfers between devices with their start and end apart: 13, of which 10 were waited for; matrix products, arithmetic and copies ran while one was open for 3% of the time, Pallas kernels for 0%

profile of v13, /device:TPU:33, one launch (start us, length us, event | category | flops | bytes accessed | tf_op | source)
XLA Modules:
  0.0 113.0 jit_solution(11022570353853004913)
XLA Ops:
  0.6 0.0 copy-start.2
  0.6 0.0 copy-start
  0.6 7.1 %collective-permute-start = (f32[2,128,256]{2,1,0:T(8,128)}, f32[2,128,256]{2,1,0:T(8,128)S(1)}, u32[]{:S(2)}, u32[]{:S(2)}) collective-permute-start(f32[2,128,256]{2,1,0:T(8,128)} %param.4), channel_id=1, source_target_pairs={{0,192},{1,200},{2,208},{3,216},{4,193},{5,201},{6,209},{7,217},{8... | collective-permute-start | bytes 786440 | tf_op jit(solution)/shard_map/ppermute | solution.py:78
  7.7 1.3 %collective-permute-start.1 = (f32[2,128,256]{2,1,0:T(8,128)}, f32[2,128,256]{2,1,0:T(8,128)S(1)}, u32[]{:S(2)}, u32[]{:S(2)}) collective-permute-start(f32[2,128,256]{2,1,0:T(8,128)} %param.4), channel_id=1, source_target_pairs={{0,64},{1,72},{2,80},{3,88},{4,65},{5,73},{6,81},{7,89},{8,66},{9,... | collective-permute-start | bytes 786440 | tf_op jit(solution)/shard_map/ppermute | solution.py:78
  9.1 6.4 %collective-permute-start.2 = (f32[2,128,256]{2,1,0:T(8,128)}, f32[2,128,256]{2,1,0:T(8,128)S(1)}, u32[]{:S(2)}, u32[]{:S(2)}) collective-permute-start(f32[2,128,256]{2,1,0:T(8,128)} %param.4), channel_id=1, source_target_pairs={{0,0},{1,8},{2,16},{3,24},{4,1},{5,9},{6,17},{7,25},{8,2},{9,10},{... | collective-permute-start | bytes 786440 | tf_op jit(solution)/shard_map/ppermute | solution.py:78
  15.5 31.0 %collective-permute-done = f32[2,128,256]{2,1,0:T(8,128)S(1)} collective-permute-done((f32[2,128,256]{2,1,0:T(8,128)}, f32[2,128,256]{2,1,0:T(8,128)S(1)}, u32[]{:S(2)}, u32[]{:S(2)}) %collective-permute-start) | collective-permute-done | bytes 262176 | tf_op jit(solution)/shard_map/ppermute | solution.py:78
  46.5 5.6 %collective-permute-done.1 = f32[2,128,256]{2,1,0:T(8,128)S(1)} collective-permute-done((f32[2,128,256]{2,1,0:T(8,128)}, f32[2,128,256]{2,1,0:T(8,128)S(1)}, u32[]{:S(2)}, u32[]{:S(2)}) %collective-permute-start.1) | collective-permute-done | bytes 262176 | tf_op jit(solution)/shard_map/ppermute | solution.py:78
  52.1 5.6 %collective-permute-done.2 = f32[2,128,256]{2,1,0:T(8,128)S(1)} collective-permute-done((f32[2,128,256]{2,1,0:T(8,128)}, f32[2,128,256]{2,1,0:T(8,128)S(1)}, u32[]{:S(2)}, u32[]{:S(2)}) %collective-permute-start.2) | collective-permute-done | bytes 262176 | tf_op jit(solution)/shard_map/ppermute | solution.py:78
  57.8 0.7 collective-permute-start.3
  58.5 0.7 collective-permute-start.4
  59.2 0.0 collective-permute-done.3
  59.2 0.0 collective-permute-done.4
  59.2 0.1 fusion.17
  59.3 0.7 collective-permute-start.5
  59.9 0.0 copy-done.2
  59.9 0.0 copy-done
  60.0 0.3 fusion.20
  60.3 0.3 fusion.26
  60.6 0.0 collective-permute-done.5
  60.7 0.1 collective-permute-start.6
  60.8 0.1 collective-permute-start.7
  60.9 1.4 %collective-permute-start.8 = (f32[2,128,256]{2,1,0:T(8,128)S(1)}, f32[2,128,256]{2,1,0:T(8,128)S(1)}, u32[]{:S(2)}, u32[]{:S(2)}) collective-permute-start(f32[2,128,256]{2,1,0:T(8,128)S(1)} %select_select_fusion), channel_id=1, source_target_pairs={{0,8},{8,16},{16,24},{24,0},{1,9},{9,17},{17,25},{25,1},{2,10},{10... | collective-permute-start | bytes 786440 | tf_op jit(solution)/shard_map/ppermute | solution.py:66
  62.2 0.3 fusion.5
  62.5 0.3 fusion.6
  62.8 5.3 %collective-permute-done.6 = f32[2,128,256]{2,1,0:T(8,128)S(1)} collective-permute-done((f32[2,128,256]{2,1,0:T(8,128)S(1)}, f32[2,128,256]{2,1,0:T(8,128)S(1)}, u32[]{:S(2)}, u32[]{:S(2)}) %collective-permute-start.6) | collective-permute-done | bytes 262176 | tf_op jit(solution)/shard_map/ppermute | solution.py:66
  68.2 1.6 %collective-permute-done.7 = f32[2,128,256]{2,1,0:T(8,128)S(1)} collective-permute-done((f32[2,128,256]{2,1,0:T(8,128)S(1)}, f32[2,128,256]{2,1,0:T(8,128)S(1)}, u32[]{:S(2)}, u32[]{:S(2)}) %collective-permute-start.7) | collective-permute-done | bytes 262176 | tf_op jit(solution)/shard_map/ppermute | solution.py:66
  69.8 6.4 %collective-permute-done.8 = f32[2,128,256]{2,1,0:T(8,128)S(1)} collective-permute-done((f32[2,128,256]{2,1,0:T(8,128)S(1)}, f32[2,128,256]{2,1,0:T(8,128)S(1)}, u32[]{:S(2)}, u32[]{:S(2)}) %collective-permute-start.8) | collective-permute-done | bytes 262176 | tf_op jit(solution)/shard_map/ppermute | solution.py:66
  76.2 0.1 select_select_fusion.9
  76.3 0.1 pad_maximum_fusion.1
  76.4 0.2 collective-permute-start.10
  76.6 4.3 %collective-permute-start.11 = (f32[2,128,256]{2,1,0:T(8,128)S(1)}, f32[2,128,256]{2,1,0:T(8,128)S(1)}, u32[]{:S(2)}, u32[]{:S(2)}) collective-permute-start(f32[2,128,256]{2,1,0:T(8,128)S(1)} %copy-done.2), channel_id=1, source_target_pairs={{0,2},{2,4},{4,6},{6,0},{1,3},{3,5},{5,7},{7,1},{8,10},{10,12},{12... | collective-permute-start | bytes 786440 | tf_op jit(solution)/shard_map/ppermute | solution.py:66
  80.9 1.1 collective-permute-start.9
  82.0 0.7 pad_maximum_fusion.3
  82.8 0.4 fusion.11
  83.1 1.7 %collective-permute-done.10 = f32[2,128,256]{2,1,0:T(8,128)S(1)} collective-permute-done((f32[2,128,256]{2,1,0:T(8,128)S(1)}, f32[2,128,256]{2,1,0:T(8,128)S(1)}, u32[]{:S(2)}, u32[]{:S(2)}) %collective-permute-start.10) | collective-permute-done | bytes 262176 | tf_op jit(solution)/shard_map/ppermute | solution.py:66
  84.8 9.1 %collective-permute-done.11 = f32[2,128,256]{2,1,0:T(8,128)S(1)} collective-permute-done((f32[2,128,256]{2,1,0:T(8,128)S(1)}, f32[2,128,256]{2,1,0:T(8,128)S(1)}, u32[]{:S(2)}, u32[]{:S(2)}) %collective-permute-start.11) | collective-permute-done | bytes 262176 | tf_op jit(solution)/shard_map/ppermute | solution.py:66
  93.9 8.6 %collective-permute-done.9 = f32[2,128,256]{2,1,0:T(8,128)S(1)} collective-permute-done((f32[2,128,256]{2,1,0:T(8,128)S(1)}, f32[2,128,256]{2,1,0:T(8,128)S(1)}, u32[]{:S(2)}, u32[]{:S(2)}) %collective-permute-start.9) | collective-permute-done | bytes 262176 | tf_op jit(solution)/shard_map/ppermute | solution.py:66
  102.5 0.1 select_select_fusion.5
  102.7 0.1 pad_maximum_fusion.2
  102.7 0.6 collective-permute-start.12
  103.3 0.4 fusion.4
  103.7 0.4 fusion.9
  104.1 0.4 convolution_add_fusion
  104.5 0.2 maximum_bitcast_fusion
  104.7 0.9 collective-permute-done.12
  105.6 0.2 broadcast_select_fusion.1
  105.8 0.0 copy-start.1
  105.8 0.2 pad_maximum_fusion
  106.0 2.0 %copy-done.1 = f32[2,1024,512]{2,1,0:T(8,128)S(1)} copy-done((f32[2,1024,512]{2,1,0:T(8,128)S(1)}, f32[2,1024,512]{2,1,0:T(8,128)}, u32[]{:S(2)}) %copy-start.1) | copy-done | bytes 4194328
  108.0 5.1 %bitcast_subtract_fusion = f32[2,1024,512]{2,1,0:T(8,128)} fusion(f32[2,1024,512]{2,1,0:T(8,128)S(1)} %copy-done.1, f32[1,2,512,256]{3,2,1,0:T(8,128)S(1)} %get-tuple-element.21, f32[1,2,512,256]{3,2,1,0:T(8,128)S(1)} %get-tuple-element.20, f32[2,1024,256]{2,1,0:T(8,128)S(1)} %bitcast.57), kind=kOutput, calls=%fused_computation | convolution fusion | flops 3222798336 | bytes 12582912 | tf_op jit(solution)/shard_map/dot_general | solution.py:106
  (3 shorter events, 0.1 us)
Async XLA Ops:
  0.6 59.3 %copy-start.2 = (f32[2,128,256]{2,1,0:T(8,128)S(1)}, f32[2,128,256]{2,1,0:T(8,128)}, u32[]{:S(2)}) copy-start(f32[2,128,256]{2,1,0:T(8,128)} %param.4) | copy-start | bytes 786436
  0.6 59.3 %copy-start = (f32[2,256,256]{2,1,0:T(8,128)S(1)}, f32[2,256,256]{2,1,0:T(8,128)}, u32[]{:S(2)}) copy-start(f32[2,256,256]{2,1,0:T(8,128)} %param.5) | copy-start | bytes 1572868
  0.6 45.8 %collective-permute-start = (f32[2,128,256]{2,1,0:T(8,128)}, f32[2,128,256]{2,1,0:T(8,128)S(1)}, u32[]{:S(2)}, u32[]{:S(2)}) collective-permute-start(f32[2,128,256]{2,1,0:T(8,128)} %param.4), channel_id=1, source_target_pairs={{0,192},{1,200},{2,208},{3,216},{4,193},{5,201},{6,209},{7,217},{8... | collective-permute-start | bytes 786440 | tf_op jit(solution)/shard_map/ppermute | solution.py:78
  7.7 44.4 %collective-permute-start.1 = (f32[2,128,256]{2,1,0:T(8,128)}, f32[2,128,256]{2,1,0:T(8,128)S(1)}, u32[]{:S(2)}, u32[]{:S(2)}) collective-permute-start(f32[2,128,256]{2,1,0:T(8,128)} %param.4), channel_id=1, source_target_pairs={{0,64},{1,72},{2,80},{3,88},{4,65},{5,73},{6,81},{7,89},{8,66},{9,... | collective-permute-start | bytes 786440 | tf_op jit(solution)/shard_map/ppermute | solution.py:78
  9.1 48.7 %collective-permute-start.2 = (f32[2,128,256]{2,1,0:T(8,128)}, f32[2,128,256]{2,1,0:T(8,128)S(1)}, u32[]{:S(2)}, u32[]{:S(2)}) collective-permute-start(f32[2,128,256]{2,1,0:T(8,128)} %param.4), channel_id=1, source_target_pairs={{0,0},{1,8},{2,16},{3,24},{4,1},{5,9},{6,17},{7,25},{8,2},{9,10},{... | collective-permute-start | bytes 786440 | tf_op jit(solution)/shard_map/ppermute | solution.py:78
  57.8 1.4 %collective-permute-start.3 = (f32[2,128,256]{2,1,0:T(8,128)S(1)}, f32[2,128,256]{2,1,0:T(8,128)S(1)}, u32[]{:S(2)}, u32[]{:S(2)}) collective-permute-start(f32[2,128,256]{2,1,0:T(8,128)S(1)} %select_select_fusion.10), channel_id=1, source_target_pairs={{64,96},{65,97},{66,98},{67,99},{68,100},{69,101},{70,102},{71,103... | collective-permute-start | bytes 786440 | tf_op jit(solution)/shard_map/ppermute | solution.py:86
  58.5 0.7 collective-permute-start.4
  59.3 1.4 %collective-permute-start.5 = (f32[2,128,256]{2,1,0:T(8,128)S(1)}, f32[2,128,256]{2,1,0:T(8,128)S(1)}, u32[]{:S(2)}, u32[]{:S(2)}) collective-permute-start(f32[2,128,256]{2,1,0:T(8,128)S(1)} %fusion.17), channel_id=1, source_target_pairs={{96,160},{224,32},{97,161},{225,33},{98,162},{226,34},{99,163},{22... | collective-permute-start | bytes 786440 | tf_op jit(solution)/shard_map/ppermute | solution.py:86
  60.7 7.5 %collective-permute-start.6 = (f32[2,128,256]{2,1,0:T(8,128)S(1)}, f32[2,128,256]{2,1,0:T(8,128)S(1)}, u32[]{:S(2)}, u32[]{:S(2)}) collective-permute-start(f32[2,128,256]{2,1,0:T(8,128)S(1)} %select_select_fusion), channel_id=1, source_target_pairs={{0,24},{8,0},{16,8},{24,16},{1,25},{9,1},{17,9},{25,17},{2,26},{10... | collective-permute-start | bytes 786440 | tf_op jit(solution)/shard_map/ppermute | solution.py:66
  60.8 9.0 %collective-permute-start.7 = (f32[2,128,256]{2,1,0:T(8,128)S(1)}, f32[2,128,256]{2,1,0:T(8,128)S(1)}, u32[]{:S(2)}, u32[]{:S(2)}) collective-permute-start(f32[2,128,256]{2,1,0:T(8,128)S(1)} %select_select_fusion), channel_id=1, source_target_pairs={{0,16},{8,24},{16,0},{24,8},{1,17},{9,25},{17,1},{25,9},{2,18},{10... | collective-permute-start | bytes 786440 | tf_op jit(solution)/shard_map/ppermute | solution.py:66
  60.9 15.3 %collective-permute-start.8 = (f32[2,128,256]{2,1,0:T(8,128)S(1)}, f32[2,128,256]{2,1,0:T(8,128)S(1)}, u32[]{:S(2)}, u32[]{:S(2)}) collective-permute-start(f32[2,128,256]{2,1,0:T(8,128)S(1)} %select_select_fusion), channel_id=1, source_target_pairs={{0,8},{8,16},{16,24},{24,0},{1,9},{9,17},{17,25},{25,1},{2,10},{10... | collective-permute-start | bytes 786440 | tf_op jit(solution)/shard_map/ppermute | solution.py:66
  76.4 8.4 %collective-permute-start.10 = (f32[2,128,256]{2,1,0:T(8,128)S(1)}, f32[2,128,256]{2,1,0:T(8,128)S(1)}, u32[]{:S(2)}, u32[]{:S(2)}) collective-permute-start(f32[2,128,256]{2,1,0:T(8,128)S(1)} %copy-done.2), channel_id=1, source_target_pairs={{0,4},{2,6},{4,0},{6,2},{1,5},{3,7},{5,1},{7,3},{8,12},{10,14},{12... | collective-permute-start | bytes 786440 | tf_op jit(solution)/shard_map/ppermute | solution.py:66
  76.6 17.3 %collective-permute-start.11 = (f32[2,128,256]{2,1,0:T(8,128)S(1)}, f32[2,128,256]{2,1,0:T(8,128)S(1)}, u32[]{:S(2)}, u32[]{:S(2)}) collective-permute-start(f32[2,128,256]{2,1,0:T(8,128)S(1)} %copy-done.2), channel_id=1, source_target_pairs={{0,2},{2,4},{4,6},{6,0},{1,3},{3,5},{5,7},{7,1},{8,10},{10,12},{12... | collective-permute-start | bytes 786440 | tf_op jit(solution)/shard_map/ppermute | solution.py:66
  80.9 21.6 %collective-permute-start.9 = (f32[2,128,256]{2,1,0:T(8,128)S(1)}, f32[2,128,256]{2,1,0:T(8,128)S(1)}, u32[]{:S(2)}, u32[]{:S(2)}) collective-permute-start(f32[2,128,256]{2,1,0:T(8,128)S(1)} %copy-done.2), channel_id=1, source_target_pairs={{0,6},{2,0},{4,2},{6,4},{1,7},{3,1},{5,3},{7,5},{8,14},{10,8},{12,... | collective-permute-start | bytes 786440 | tf_op jit(solution)/shard_map/ppermute | solution.py:66
  102.7 2.9 %collective-permute-start.12 = (f32[2,512,256]{2,1,0:T(8,128)S(1)}, f32[2,512,256]{2,1,0:T(8,128)S(1)}, u32[]{:S(2)}, u32[]{:S(2)}) collective-permute-start(f32[2,512,256]{2,1,0:T(8,128)S(1)} %pad_maximum_fusion.2), channel_id=1, source_target_pairs={{0,1},{1,0},{2,3},{3,2},{4,5},{5,4},{6,7},{7,6},{8,9},{9,8},{10,11... | collective-permute-start | bytes 3145736 | tf_op jit(solution)/shard_map/ppermute | solution.py:94
  105.8 2.2 %copy-start.1 = (f32[2,1024,512]{2,1,0:T(8,128)S(1)}, f32[2,1024,512]{2,1,0:T(8,128)}, u32[]{:S(2)}) copy-start(f32[2,1024,512]{2,1,0:T(8,128)} %param.3) | copy-start | bytes 12582916

commit v14 on v5

--- a/solution.py
+++ b/solution.py
@@ -89,8 +89,9 @@
         panel_late, held = lax.optimization_barrier((panel, held))
         window = gather(held, "x", xi, nx)
 
-        mine = gather(panel_late, "zl", li, nl)
-        other = lax.ppermute(mine, "core", shifts(nc, 1))
+        got_z = [panel_late] + [lax.ppermute(panel_late, "zl", shifts(nl, k)) for k in range(1, nl)]
+        mine = reorder(got_z, li, nl)
+        other = reorder([lax.ppermute(g, "core", shifts(nc, 1)) for g in got_z], li, nl)
         lo = jnp.where(ci == 0, mine, other)
         hi_ = jnp.where(ci == 0, other, mine)
         two, rows, width = mine.shape[0], panel.shape[1], mine.shape[2]

time: 102 us -> 107 us (1.049)
  the two profiles are of different devices: /device:TPU:7 before, /device:TPU:209 now
where the time goes in v14:
time: 107 us
  waiting for transfers between devices  64.6 us (60%)
  starting transfers between devices  29.5 us (28%)
  matrix products  7.7 us (7%)
  local copies, waits for them, and re-layouts  2.05 us (2%)
  other arithmetic  1.79 us (2%)
  between operations  1.16 us (1%)
    ppermute x3, waiting for transfers between devices, local(): lax.ppermute(sent, ('y', 'zh'), [(plane(h0, y0), plane(h1, y1)) for (y0,...  43.1 us
    ppermute x3, starting transfers between devices, local(): lax.ppermute(panel_late, 'zl', shifts(nl, k))  21.4 us
    ppermute x3, waiting for transfers between devices, local(): lax.ppermute(panel_late, 'zl', shifts(nl, k))  20.2 us
    dot_general x1, matrix products, local(): product = lax.dot_general(lhs, rhs, dims, precision=lax.Precision.HIGH)  5.06 us
    ppermute x3, starting transfers between devices, local(): lax.ppermute(sent, ('y', 'zh'), [(plane(h0, y0), plane(h1, y1)) for (y0,...  2.65 us
    ppermute x3, starting transfers between devices, local(): got_a = [lax.ppermute(panel, AXES, spread(y1, h1)) for y1, h1 in first]  2.16 us
  transfers between devices with their start and end apart: 16, of which 5 were waited for; matrix products, arithmetic and copies ran while one was open for 4% of the time, Pallas kernels for 0%

profile of v14, /device:TPU:209, one launch (start us, length us, event | category | flops | bytes accessed | tf_op | source)
XLA Modules:
  0.0 106.8 jit_solution(4973422122916539007)
XLA Ops:
  0.6 0.0 copy-start.2
  0.6 0.0 copy-start
  0.6 0.8 collective-permute-start
  1.5 0.7 collective-permute-start.1
  2.2 0.7 collective-permute-start.2
  2.9 0.0 collective-permute-done
  2.9 0.0 collective-permute-done.1
  2.9 0.0 collective-permute-done.2
  2.9 0.1 select_select_fusion.14
  2.9 0.7 collective-permute-start.3
  3.6 0.7 collective-permute-start.4
  4.3 0.0 collective-permute-done.3
  4.3 0.0 collective-permute-done.4
  4.4 0.1 fusion.11
  4.4 1.3 %collective-permute-start.5 = (f32[2,128,256]{2,1,0:T(8,128)S(1)}, f32[2,128,256]{2,1,0:T(8,128)S(1)}, u32[]{:S(2)}, u32[]{:S(2)}) collective-permute-start(f32[2,128,256]{2,1,0:T(8,128)S(1)} %fusion.11), channel_id=1, source_target_pairs={{96,160},{224,32},{97,161},{225,33},{98,162},{226,34},{99,163},{22... | collective-permute-start | bytes 786440 | tf_op jit(solution)/shard_map/ppermute | solution.py:86
  5.7 0.0 copy-done.2
  5.7 0.0 copy-done
  5.7 0.3 fusion.14
  6.0 0.3 fusion.20
  6.3 43.1 %collective-permute-done.5 = f32[2,128,256]{2,1,0:T(8,128)S(1)} collective-permute-done((f32[2,128,256]{2,1,0:T(8,128)S(1)}, f32[2,128,256]{2,1,0:T(8,128)S(1)}, u32[]{:S(2)}, u32[]{:S(2)}) %collective-permute-start.5) | collective-permute-done | bytes 262176 | tf_op jit(solution)/shard_map/ppermute | solution.py:86
  49.5 0.1 collective-permute-start.13
  49.6 0.1 collective-permute-start.14
  49.7 1.4 %collective-permute-start.15 = (f32[2,128,256]{2,1,0:T(8,128)S(1)}, f32[2,128,256]{2,1,0:T(8,128)S(1)}, u32[]{:S(2)}, u32[]{:S(2)}) collective-permute-start(f32[2,128,256]{2,1,0:T(8,128)S(1)} %select_select_fusion), channel_id=1, source_target_pairs={{0,8},{8,16},{16,24},{24,0},{1,9},{9,17},{17,25},{25,1},{2,10},{10... | collective-permute-start | bytes 786440 | tf_op jit(solution)/shard_map/ppermute | solution.py:66
  51.0 0.3 fusion.5
  51.5 0.3 fusion.6
  51.8 0.7 pad_maximum_fusion.4
  52.5 0.0 collective-permute-start.6
  52.5 21.4 %collective-permute-start.7 = (f32[2,128,256]{2,1,0:T(8,128)S(1)}, f32[2,128,256]{2,1,0:T(8,128)S(1)}, u32[]{:S(2)}, u32[]{:S(2)}) collective-permute-start(f32[2,128,256]{2,1,0:T(8,128)S(1)} %copy-done.2), channel_id=1, source_target_pairs={{0,4},{2,6},{4,0},{6,2},{1,5},{3,7},{5,1},{7,3},{8,12},{10,14},{12... | collective-permute-start | bytes 786440 | tf_op jit(solution)/shard_map/ppermute | solution.py:92
  73.9 0.0 collective-permute-done.13
  73.9 0.0 collective-permute-start.8
  73.9 0.0 collective-permute-done.14
  73.9 1.0 collective-permute-start.12
  74.9 0.0 collective-permute-done.15
  74.9 0.1 select_select_fusion.5
  75.0 0.1 pad_maximum_fusion.3
  75.1 0.4 fusion.9
  75.5 0.4 convolution_add_fusion
  75.9 14.5 %collective-permute-done.7 = f32[2,128,256]{2,1,0:T(8,128)S(1)} collective-permute-done((f32[2,128,256]{2,1,0:T(8,128)S(1)}, f32[2,128,256]{2,1,0:T(8,128)S(1)}, u32[]{:S(2)}, u32[]{:S(2)}) %collective-permute-start.7) | collective-permute-done | bytes 262176 | tf_op jit(solution)/shard_map/ppermute | solution.py:92
  90.4 0.0 collective-permute-start.10
  90.5 0.4 fusion.10
  90.8 5.7 %collective-permute-done.8 = f32[2,128,256]{2,1,0:T(8,128)S(1)} collective-permute-done((f32[2,128,256]{2,1,0:T(8,128)S(1)}, f32[2,128,256]{2,1,0:T(8,128)S(1)}, u32[]{:S(2)}, u32[]{:S(2)}) %collective-permute-start.8) | collective-permute-done | bytes 262176 | tf_op jit(solution)/shard_map/ppermute | solution.py:92
  96.5 0.4 collective-permute-start.11
  96.9 0.4 fusion.4
  97.3 0.2 maximum_bitcast_fusion
  97.5 0.0 collective-permute-done.6
  97.5 0.4 collective-permute-start.9
  97.8 0.1 select_select_fusion.13
  98.0 0.0 collective-permute-done.12
  98.0 0.0 collective-permute-done.10
  98.0 0.1 collective-permute-done.11
  98.1 1.2 %collective-permute-done.9 = f32[2,128,256]{2,1,0:T(8,128)S(1)} collective-permute-done((f32[2,128,256]{2,1,0:T(8,128)S(1)}, f32[2,128,256]{2,1,0:T(8,128)S(1)}, u32[]{:S(2)}, u32[]{:S(2)}) %collective-permute-start.9) | collective-permute-done | bytes 262176 | tf_op jit(solution)/shard_map/ppermute | solution.py:94
  99.3 0.1 select_select_fusion.9
  99.4 0.2 fusion.8
  99.6 0.0 copy-start.1
  99.6 0.1 pad_maximum_fusion
  99.7 2.0 %copy-done.1 = f32[2,1024,512]{2,1,0:T(8,128)S(1)} copy-done((f32[2,1024,512]{2,1,0:T(8,128)S(1)}, f32[2,1024,512]{2,1,0:T(8,128)}, u32[]{:S(2)}) %copy-start.1) | copy-done | bytes 4194328
  101.8 5.1 %bitcast_subtract_fusion = f32[2,1024,512]{2,1,0:T(8,128)} fusion(f32[2,1024,512]{2,1,0:T(8,128)S(1)} %copy-done.1, f32[1,2,512,256]{3,2,1,0:T(8,128)S(1)} %get-tuple-element.21, f32[1,2,512,256]{3,2,1,0:T(8,128)S(1)} %get-tuple-element.20, f32[2,1024,256]{2,1,0:T(8,128)S(1)} %bitcast.55), kind=kOutput, calls=%fused_computation | convolution fusion | flops 3222798336 | bytes 12582912 | tf_op jit(solution)/shard_map/dot_general | solution.py:106
  (2 shorter events, 0.1 us)
Async XLA Ops:
  0.6 5.1 %copy-start.2 = (f32[2,128,256]{2,1,0:T(8,128)S(1)}, f32[2,128,256]{2,1,0:T(8,128)}, u32[]{:S(2)}) copy-start(f32[2,128,256]{2,1,0:T(8,128)} %param.4) | copy-start | bytes 786436
  0.6 5.1 %copy-start = (f32[2,256,256]{2,1,0:T(8,128)S(1)}, f32[2,256,256]{2,1,0:T(8,128)}, u32[]{:S(2)}) copy-start(f32[2,256,256]{2,1,0:T(8,128)} %param.5) | copy-start | bytes 1572868
  0.6 2.2 %collective-permute-start = (f32[2,128,256]{2,1,0:T(8,128)}, f32[2,128,256]{2,1,0:T(8,128)S(1)}, u32[]{:S(2)}, u32[]{:S(2)}) collective-permute-start(f32[2,128,256]{2,1,0:T(8,128)} %param.4), channel_id=1, source_target_pairs={{0,192},{1,200},{2,208},{3,216},{4,193},{5,201},{6,209},{7,217},{8... | collective-permute-start | bytes 786440 | tf_op jit(solution)/shard_map/ppermute | solution.py:78
  1.5 1.4 %collective-permute-start.1 = (f32[2,128,256]{2,1,0:T(8,128)}, f32[2,128,256]{2,1,0:T(8,128)S(1)}, u32[]{:S(2)}, u32[]{:S(2)}) collective-permute-start(f32[2,128,256]{2,1,0:T(8,128)} %param.4), channel_id=1, source_target_pairs={{0,64},{1,72},{2,80},{3,88},{4,65},{5,73},{6,81},{7,89},{8,66},{9,... | collective-permute-start | bytes 786440 | tf_op jit(solution)/shard_map/ppermute | solution.py:78
  2.2 0.7 collective-permute-start.2
  2.9 1.4 %collective-permute-start.3 = (f32[2,128,256]{2,1,0:T(8,128)S(1)}, f32[2,128,256]{2,1,0:T(8,128)S(1)}, u32[]{:S(2)}, u32[]{:S(2)}) collective-permute-start(f32[2,128,256]{2,1,0:T(8,128)S(1)} %select_select_fusion.14), channel_id=1, source_target_pairs={{64,96},{65,97},{66,98},{67,99},{68,100},{69,101},{70,102},{71,103... | collective-permute-start | bytes 786440 | tf_op jit(solution)/shard_map/ppermute | solution.py:86
  3.6 0.7 collective-permute-start.4
  4.4 45.0 %collective-permute-start.5 = (f32[2,128,256]{2,1,0:T(8,128)S(1)}, f32[2,128,256]{2,1,0:T(8,128)S(1)}, u32[]{:S(2)}, u32[]{:S(2)}) collective-permute-start(f32[2,128,256]{2,1,0:T(8,128)S(1)} %fusion.11), channel_id=1, source_target_pairs={{96,160},{224,32},{97,161},{225,33},{98,162},{226,34},{99,163},{22... | collective-permute-start | bytes 786440 | tf_op jit(solution)/shard_map/ppermute | solution.py:86
  49.5 24.4 %collective-permute-start.13 = (f32[2,128,256]{2,1,0:T(8,128)S(1)}, f32[2,128,256]{2,1,0:T(8,128)S(1)}, u32[]{:S(2)}, u32[]{:S(2)}) collective-permute-start(f32[2,128,256]{2,1,0:T(8,128)S(1)} %select_select_fusion), channel_id=1, source_target_pairs={{0,24},{8,0},{16,8},{24,16},{1,25},{9,1},{17,9},{25,17},{2,26},{10... | collective-permute-start | bytes 786440 | tf_op jit(solution)/shard_map/ppermute | solution.py:66
  49.6 24.3 %collective-permute-start.14 = (f32[2,128,256]{2,1,0:T(8,128)S(1)}, f32[2,128,256]{2,1,0:T(8,128)S(1)}, u32[]{:S(2)}, u32[]{:S(2)}) collective-permute-start(f32[2,128,256]{2,1,0:T(8,128)S(1)} %select_select_fusion), channel_id=1, source_target_pairs={{0,16},{8,24},{16,0},{24,8},{1,17},{9,25},{17,1},{25,9},{2,18},{10... | collective-permute-start | bytes 786440 | tf_op jit(solution)/shard_map/ppermute | solution.py:66
  49.7 25.2 %collective-permute-start.15 = (f32[2,128,256]{2,1,0:T(8,128)S(1)}, f32[2,128,256]{2,1,0:T(8,128)S(1)}, u32[]{:S(2)}, u32[]{:S(2)}) collective-permute-start(f32[2,128,256]{2,1,0:T(8,128)S(1)} %select_select_fusion), channel_id=1, source_target_pairs={{0,8},{8,16},{16,24},{24,0},{1,9},{9,17},{17,25},{25,1},{2,10},{10... | collective-permute-start | bytes 786440 | tf_op jit(solution)/shard_map/ppermute | solution.py:66
  52.5 45.0 %collective-permute-start.6 = (f32[2,128,256]{2,1,0:T(8,128)S(1)}, f32[2,128,256]{2,1,0:T(8,128)S(1)}, u32[]{:S(2)}, u32[]{:S(2)}) collective-permute-start(f32[2,128,256]{2,1,0:T(8,128)S(1)} %copy-done.2), channel_id=1, source_target_pairs={{0,6},{2,0},{4,2},{6,4},{1,7},{3,1},{5,3},{7,5},{8,14},{10,8},{12,... | collective-permute-start | bytes 786440 | tf_op jit(solution)/shard_map/ppermute | solution.py:92
  52.5 37.9 %collective-permute-start.7 = (f32[2,128,256]{2,1,0:T(8,128)S(1)}, f32[2,128,256]{2,1,0:T(8,128)S(1)}, u32[]{:S(2)}, u32[]{:S(2)}) collective-permute-start(f32[2,128,256]{2,1,0:T(8,128)S(1)} %copy-done.2), channel_id=1, source_target_pairs={{0,4},{2,6},{4,0},{6,2},{1,5},{3,7},{5,1},{7,3},{8,12},{10,14},{12... | collective-permute-start | bytes 786440 | tf_op jit(solution)/shard_map/ppermute | solution.py:92
  73.9 22.6 %collective-permute-start.8 = (f32[2,128,256]{2,1,0:T(8,128)S(1)}, f32[2,128,256]{2,1,0:T(8,128)S(1)}, u32[]{:S(2)}, u32[]{:S(2)}) collective-permute-start(f32[2,128,256]{2,1,0:T(8,128)S(1)} %copy-done.2), channel_id=1, source_target_pairs={{0,2},{2,4},{4,6},{6,0},{1,3},{3,5},{5,7},{7,1},{8,10},{10,12},{12... | collective-permute-start | bytes 786440 | tf_op jit(solution)/shard_map/ppermute | solution.py:92
  73.9 24.0 %collective-permute-start.12 = (f32[2,128,256]{2,1,0:T(8,128)S(1)}, f32[2,128,256]{2,1,0:T(8,128)S(1)}, u32[]{:S(2)}, u32[]{:S(2)}) collective-permute-start(f32[2,128,256]{2,1,0:T(8,128)S(1)} %copy-done.2), channel_id=1, source_target_pairs={{0,1},{1,0},{2,3},{3,2},{4,5},{5,4},{6,7},{7,6},{8,9},{9,8},{10,11... | collective-permute-start | bytes 786440 | tf_op jit(solution)/shard_map/ppermute | solution.py:94
  90.4 7.5 %collective-permute-start.10 = (f32[2,128,256]{2,1,0:T(8,128)S(1)}, f32[2,128,256]{2,1,0:T(8,128)S(1)}, u32[]{:S(2)}, u32[]{:S(2)}) collective-permute-start(f32[2,128,256]{2,1,0:T(8,128)S(1)} %collective-permute-done.7), channel_id=1, source_target_pairs={{0,1},{1,0},{2,3},{3,2},{4,5},{5,4},{6,7},{7,6},{8,9},{9,8},{10,11... | collective-permute-start | bytes 786440 | tf_op jit(solution)/shard_map/ppermute | solution.py:94
  96.5 1.6 %collective-permute-start.11 = (f32[2,128,256]{2,1,0:T(8,128)S(1)}, f32[2,128,256]{2,1,0:T(8,128)S(1)}, u32[]{:S(2)}, u32[]{:S(2)}) collective-permute-start(f32[2,128,256]{2,1,0:T(8,128)S(1)} %collective-permute-done.8), channel_id=1, source_target_pairs={{0,1},{1,0},{2,3},{3,2},{4,5},{5,4},{6,7},{7,6},{8,9},{9,8},{10,11... | collective-permute-start | bytes 786440 | tf_op jit(solution)/shard_map/ppermute | solution.py:94
  97.5 1.8 %collective-permute-start.9 = (f32[2,128,256]{2,1,0:T(8,128)S(1)}, f32[2,128,256]{2,1,0:T(8,128)S(1)}, u32[]{:S(2)}, u32[]{:S(2)}) collective-permute-start(f32[2,128,256]{2,1,0:T(8,128)S(1)} %collective-permute-done.6), channel_id=1, source_target_pairs={{0,1},{1,0},{2,3},{3,2},{4,5},{5,4},{6,7},{7,6},{8,9},{9,8},{10,11... | collective-permute-start | bytes 786440 | tf_op jit(solution)/shard_map/ppermute | solution.py:94
  99.6 2.2 %copy-start.1 = (f32[2,1024,512]{2,1,0:T(8,128)S(1)}, f32[2,1024,512]{2,1,0:T(8,128)}, u32[]{:S(2)}) copy-start(f32[2,1024,512]{2,1,0:T(8,128)} %param.3) | copy-start | bytes 12582916

commit v15 on v12

--- a/solution.py
+++ b/solution.py
@@ -44,10 +44,9 @@
                     pairs.append((lin(0, 0, g, l, c), lin(y1, h1, p % nx, g, p // nx)))
         return pairs
 
-    first = [(0, 0), (1, 0), (ny - 1, 0)]
+    first = [(0, 0), (1, 0), (ny - 1, 0), (0, 1)]
     relays = [
-        [[((1, 0), (2, 0)), ((ny - 1, 0), (ny - 1, 1))]],
-        [[((2, 0), (2, 1)), ((ny - 1, 1), (0, 1)), ((1, 0), (1, 1))]],
+        [[((1, 0), (2, 0)), ((0, 1), (1, 1)), ((ny - 1, 0), (2, 1))], [((0, 1), (ny - 1, 1))]],
     ]
 
     def shifts(n, k):

time: 102 us -> 105 us (1.029)
  starting transfers between devices: 57.9 us -> 59.2 us
    ppermute x3 -> x4, starting transfers between devices: 13.5 us -> 16.3 us  [local(): got_a = [lax.ppermute(panel, AXES, spread(y1, h1)) for y1, h1 in first]]
    ppermute x6, starting transfers between devices: 42.3 us -> 40.7 us  [gather(): lax.ppermute(piece, axis, shifts(n, k))]
    ppermute x3 -> x4, waiting for transfers between devices: 14.1 us -> 15.6 us  [local(): got_a = [lax.ppermute(panel, AXES, spread(y1, h1)) for y1, h1 in first]]
  transfers between devices with their start and end apart: 12 -> 13, of which waited for: 5 -> 3; matrix products, arithmetic and copies ran while one was open for 5% -> 6% of each run, Pallas kernels for 0% -> 0%
where the time goes in v15:
time: 105 us
  starting transfers between devices  59.2 us (56%)
  waiting for transfers between devices  30.9 us (29%)
  matrix products  9.74 us (9%)
  local copies, waits for them, and re-layouts  1.99 us (2%)
  other arithmetic  1.8 us (2%)
  between operations  1.1 us (1%)
    ppermute x6, starting transfers between devices, gather(): lax.ppermute(piece, axis, shifts(n, k))  40.7 us
    ppermute x4, starting transfers between devices, local(): got_a = [lax.ppermute(panel, AXES, spread(y1, h1)) for y1, h1 in first]  16.3 us
    ppermute x4, waiting for transfers between devices, local(): got_a = [lax.ppermute(panel, AXES, spread(y1, h1)) for y1, h1 in first]  15.6 us
    ppermute x6, waiting for transfers between devices, gather(): lax.ppermute(piece, axis, shifts(n, k))  15 us
    dot_general x1, matrix products, local(): product = lax.dot_general(lhs, rhs, dims, precision=lax.Precision.HIGH)  5.06 us
  transfers between devices with their start and end apart: 13, of which 3 were waited for; matrix products, arithmetic and copies ran while one was open for 6% of the time, Pallas kernels for 0%

profile of v15, /device:TPU:7, one launch (start us, length us, event | category | flops | bytes accessed | tf_op | source)
XLA Modules:
  0.0 104.7 jit_solution(16146305188194855037)
XLA Ops:
  0.6 0.0 copy-start.2
  0.6 0.0 copy-start
  0.7 9.0 %collective-permute-start = (f32[2,128,256]{2,1,0:T(8,128)}, f32[2,128,256]{2,1,0:T(8,128)S(1)}, u32[]{:S(2)}, u32[]{:S(2)}) collective-permute-start(f32[2,128,256]{2,1,0:T(8,128)} %param.4), channel_id=1, source_target_pairs={{0,32},{1,40},{2,48},{3,56},{4,33},{5,41},{6,49},{7,57},{8,34},{9,... | collective-permute-start | bytes 786440 | tf_op jit(solution)/shard_map/ppermute | solution.py:77
  9.7 1.9 %collective-permute-start.1 = (f32[2,128,256]{2,1,0:T(8,128)}, f32[2,128,256]{2,1,0:T(8,128)S(1)}, u32[]{:S(2)}, u32[]{:S(2)}) collective-permute-start(f32[2,128,256]{2,1,0:T(8,128)} %param.4), channel_id=1, source_target_pairs={{0,192},{1,200},{2,208},{3,216},{4,193},{5,201},{6,209},{7,217},{8... | collective-permute-start | bytes 786440 | tf_op jit(solution)/shard_map/ppermute | solution.py:77
  11.6 1.3 %collective-permute-start.2 = (f32[2,128,256]{2,1,0:T(8,128)}, f32[2,128,256]{2,1,0:T(8,128)S(1)}, u32[]{:S(2)}, u32[]{:S(2)}) collective-permute-start(f32[2,128,256]{2,1,0:T(8,128)} %param.4), channel_id=1, source_target_pairs={{0,64},{1,72},{2,80},{3,88},{4,65},{5,73},{6,81},{7,89},{8,66},{9,... | collective-permute-start | bytes 786440 | tf_op jit(solution)/shard_map/ppermute | solution.py:77
  12.9 4.0 %collective-permute-start.3 = (f32[2,128,256]{2,1,0:T(8,128)}, f32[2,128,256]{2,1,0:T(8,128)S(1)}, u32[]{:S(2)}, u32[]{:S(2)}) collective-permute-start(f32[2,128,256]{2,1,0:T(8,128)} %param.4), channel_id=1, source_target_pairs={{0,0},{1,8},{2,16},{3,24},{4,1},{5,9},{6,17},{7,25},{8,2},{9,10},{... | collective-permute-start | bytes 786440 | tf_op jit(solution)/shard_map/ppermute | solution.py:77
  17.0 15.6 %collective-permute-done = f32[2,128,256]{2,1,0:T(8,128)S(1)} collective-permute-done((f32[2,128,256]{2,1,0:T(8,128)}, f32[2,128,256]{2,1,0:T(8,128)S(1)}, u32[]{:S(2)}, u32[]{:S(2)}) %collective-permute-start) | collective-permute-done | bytes 262176 | tf_op jit(solution)/shard_map/ppermute | solution.py:77
  32.6 0.0 collective-permute-done.1
  32.6 0.0 collective-permute-done.2
  32.6 0.0 collective-permute-done.3
  32.6 0.1 select_select_fusion.9
  32.7 0.7 collective-permute-start.4
  33.4 0.7 collective-permute-start.5
  34.1 1.3 %fusion.12 = f32[128,256]{1,0:T(8,128)S(1)} fusion(f32[2,256,256]{2,1,0:T(8,128)} %param.5, f32[2,128,256]{2,1,0:T(8,128)} %param.4), kind=kOutput, calls=%fused_computation.29 | convolution fusion | flops 100663296 | bytes 524288 | tf_op jit(solution)/shard_map/dot_general | solution.py:14
  35.4 1.3 %fusion.18 = f32[128,256]{1,0:T(8,128)S(1)} fusion(f32[2,256,256]{2,1,0:T(8,128)} %param.5, f32[2,128,256]{2,1,0:T(8,128)} %param.4), kind=kOutput, calls=%fused_computation.35 | convolution fusion | flops 100663296 | bytes 524288 | tf_op jit(solution)/shard_map/dot_general | solution.py:13
  36.7 0.0 collective-permute-done.4
  36.7 0.0 collective-permute-done.5
  36.7 0.1 fusion.9
  36.8 0.0 copy-done.2
  36.8 0.1 collective-permute-start.6
  36.9 33.8 %collective-permute-start.7 = (f32[2,128,256]{2,1,0:T(8,128)S(1)}, f32[2,128,256]{2,1,0:T(8,128)S(1)}, u32[]{:S(2)}, u32[]{:S(2)}) collective-permute-start(f32[2,128,256]{2,1,0:T(8,128)S(1)} %copy-done.2), channel_id=1, source_target_pairs={{0,4},{2,6},{4,0},{6,2},{1,5},{3,7},{5,1},{7,3},{8,12},{10,14},{12... | collective-permute-start | bytes 786440 | tf_op jit(solution)/shard_map/ppermute | solution.py:65
  70.7 1.4 %collective-permute-start.8 = (f32[2,128,256]{2,1,0:T(8,128)S(1)}, f32[2,128,256]{2,1,0:T(8,128)S(1)}, u32[]{:S(2)}, u32[]{:S(2)}) collective-permute-start(f32[2,128,256]{2,1,0:T(8,128)S(1)} %copy-done.2), channel_id=1, source_target_pairs={{0,2},{2,4},{4,6},{6,0},{1,3},{3,5},{5,7},{7,1},{8,10},{10,12},{12... | collective-permute-start | bytes 786440 | tf_op jit(solution)/shard_map/ppermute | solution.py:65
  72.1 0.0 copy-done
  72.1 0.3 fusion.5
  72.5 0.3 fusion.6
  72.8 0.7 pad_maximum_fusion.3
  73.5 0.0 collective-permute-start.10
  73.5 3.8 %collective-permute-start.11 = (f32[2,128,256]{2,1,0:T(8,128)S(1)}, f32[2,128,256]{2,1,0:T(8,128)S(1)}, u32[]{:S(2)}, u32[]{:S(2)}) collective-permute-start(f32[2,128,256]{2,1,0:T(8,128)S(1)} %fusion.9), channel_id=1, source_target_pairs={{0,16},{8,24},{16,0},{24,8},{1,17},{9,25},{17,1},{25,9},{2,18},{10... | collective-permute-start | bytes 786440 | tf_op jit(solution)/shard_map/ppermute | solution.py:65
  77.4 0.0 collective-permute-done.6
  77.4 1.6 %collective-permute-start.12 = (f32[2,128,256]{2,1,0:T(8,128)S(1)}, f32[2,128,256]{2,1,0:T(8,128)S(1)}, u32[]{:S(2)}, u32[]{:S(2)}) collective-permute-start(f32[2,128,256]{2,1,0:T(8,128)S(1)} %fusion.9), channel_id=1, source_target_pairs={{0,8},{8,16},{16,24},{24,0},{1,9},{9,17},{17,25},{25,1},{2,10},{10... | collective-permute-start | bytes 786440 | tf_op jit(solution)/shard_map/ppermute | solution.py:65
  78.9 15.0 %collective-permute-done.7 = f32[2,128,256]{2,1,0:T(8,128)S(1)} collective-permute-done((f32[2,128,256]{2,1,0:T(8,128)S(1)}, f32[2,128,256]{2,1,0:T(8,128)S(1)}, u32[]{:S(2)}, u32[]{:S(2)}) %collective-permute-start.7) | collective-permute-done | bytes 262176 | tf_op jit(solution)/shard_map/ppermute | solution.py:65
  93.9 0.0 collective-permute-done.8
  93.9 0.1 select_select_fusion.8
  94.0 0.1 pad_maximum_fusion.1
  94.1 0.9 collective-permute-start.9
  95.0 0.0 collective-permute-done.10
  95.0 0.0 collective-permute-done.11
  95.0 0.0 collective-permute-done.12
  95.0 0.1 select_select_fusion.4
  95.2 0.1 pad_maximum_fusion.2
  95.2 0.4 fusion.8
  95.6 0.4 fusion.4
  96.0 0.4 fusion.7
  96.4 0.4 convolution_add_fusion
  96.8 0.2 maximum_bitcast_fusion
  97.0 0.3 collective-permute-done.9
  97.3 0.2 broadcast_select_fusion.1
  97.5 0.0 copy-start.1
  97.5 0.2 pad_maximum_fusion
  97.7 2.0 %copy-done.1 = f32[2,1024,512]{2,1,0:T(8,128)S(1)} copy-done((f32[2,1024,512]{2,1,0:T(8,128)S(1)}, f32[2,1024,512]{2,1,0:T(8,128)}, u32[]{:S(2)}) %copy-start.1) | copy-done | bytes 4194328
  99.7 5.1 %bitcast_subtract_fusion = f32[2,1024,512]{2,1,0:T(8,128)} fusion(f32[2,1024,512]{2,1,0:T(8,128)S(1)} %copy-done.1, f32[1,2,512,256]{3,2,1,0:T(8,128)S(1)} %get-tuple-element.17, f32[1,2,512,256]{3,2,1,0:T(8,128)S(1)} %get-tuple-element.16, f32[2,1024,256]{2,1,0:T(8,128)S(1)} %bitcast.55), kind=kOutput, calls=%fused_computation | convolution fusion | flops 3222798336 | bytes 12582912 | tf_op jit(solution)/shard_map/dot_general | solution.py:104
  (1 shorter events, 0.0 us)
Async XLA Ops:
  0.6 36.2 %copy-start.2 = (f32[2,128,256]{2,1,0:T(8,128)S(1)}, f32[2,128,256]{2,1,0:T(8,128)}, u32[]{:S(2)}) copy-start(f32[2,128,256]{2,1,0:T(8,128)} %param.4) | copy-start | bytes 786436
  0.6 71.4 %copy-start = (f32[2,256,256]{2,1,0:T(8,128)S(1)}, f32[2,256,256]{2,1,0:T(8,128)}, u32[]{:S(2)}) copy-start(f32[2,256,256]{2,1,0:T(8,128)} %param.5) | copy-start | bytes 1572868
  0.7 31.9 %collective-permute-start = (f32[2,128,256]{2,1,0:T(8,128)}, f32[2,128,256]{2,1,0:T(8,128)S(1)}, u32[]{:S(2)}, u32[]{:S(2)}) collective-permute-start(f32[2,128,256]{2,1,0:T(8,128)} %param.4), channel_id=1, source_target_pairs={{0,32},{1,40},{2,48},{3,56},{4,33},{5,41},{6,49},{7,57},{8,34},{9,... | collective-permute-start | bytes 786440 | tf_op jit(solution)/shard_map/ppermute | solution.py:77
  9.7 22.9 %collective-permute-start.1 = (f32[2,128,256]{2,1,0:T(8,128)}, f32[2,128,256]{2,1,0:T(8,128)S(1)}, u32[]{:S(2)}, u32[]{:S(2)}) collective-permute-start(f32[2,128,256]{2,1,0:T(8,128)} %param.4), channel_id=1, source_target_pairs={{0,192},{1,200},{2,208},{3,216},{4,193},{5,201},{6,209},{7,217},{8... | collective-permute-start | bytes 786440 | tf_op jit(solution)/shard_map/ppermute | solution.py:77
  11.6 21.0 %collective-permute-start.2 = (f32[2,128,256]{2,1,0:T(8,128)}, f32[2,128,256]{2,1,0:T(8,128)S(1)}, u32[]{:S(2)}, u32[]{:S(2)}) collective-permute-start(f32[2,128,256]{2,1,0:T(8,128)} %param.4), channel_id=1, source_target_pairs={{0,64},{1,72},{2,80},{3,88},{4,65},{5,73},{6,81},{7,89},{8,66},{9,... | collective-permute-start | bytes 786440 | tf_op jit(solution)/shard_map/ppermute | solution.py:77
  12.9 19.7 %collective-permute-start.3 = (f32[2,128,256]{2,1,0:T(8,128)}, f32[2,128,256]{2,1,0:T(8,128)S(1)}, u32[]{:S(2)}, u32[]{:S(2)}) collective-permute-start(f32[2,128,256]{2,1,0:T(8,128)} %param.4), channel_id=1, source_target_pairs={{0,0},{1,8},{2,16},{3,24},{4,1},{5,9},{6,17},{7,25},{8,2},{9,10},{... | collective-permute-start | bytes 786440 | tf_op jit(solution)/shard_map/ppermute | solution.py:77
  32.7 4.0 %collective-permute-start.4 = (f32[2,128,256]{2,1,0:T(8,128)S(1)}, f32[2,128,256]{2,1,0:T(8,128)S(1)}, u32[]{:S(2)}, u32[]{:S(2)}) collective-permute-start(f32[2,128,256]{2,1,0:T(8,128)S(1)} %select_select_fusion.9), channel_id=1, source_target_pairs={{32,224},{33,225},{34,226},{35,227},{36,228},{37,229},{38,230},{39... | collective-permute-start | bytes 786440 | tf_op jit(solution)/shard_map/ppermute | solution.py:85
  33.4 3.3 %collective-permute-start.5 = (f32[2,128,256]{2,1,0:T(8,128)S(1)}, f32[2,128,256]{2,1,0:T(8,128)S(1)}, u32[]{:S(2)}, u32[]{:S(2)}) collective-permute-start(f32[2,128,256]{2,1,0:T(8,128)S(1)} %select_select_fusion.9), channel_id=1, source_target_pairs={{64,128},{32,96},{192,160},{65,129},{33,97},{193,161},{66,130},{34... | collective-permute-start | bytes 786440 | tf_op jit(solution)/shard_map/ppermute | solution.py:85
  36.8 40.6 %collective-permute-start.6 = (f32[2,128,256]{2,1,0:T(8,128)S(1)}, f32[2,128,256]{2,1,0:T(8,128)S(1)}, u32[]{:S(2)}, u32[]{:S(2)}) collective-permute-start(f32[2,128,256]{2,1,0:T(8,128)S(1)} %copy-done.2), channel_id=1, source_target_pairs={{0,6},{2,0},{4,2},{6,4},{1,7},{3,1},{5,3},{7,5},{8,14},{10,8},{12,... | collective-permute-start | bytes 786440 | tf_op jit(solution)/shard_map/ppermute | solution.py:65
  36.9 57.0 %collective-permute-start.7 = (f32[2,128,256]{2,1,0:T(8,128)S(1)}, f32[2,128,256]{2,1,0:T(8,128)S(1)}, u32[]{:S(2)}, u32[]{:S(2)}) collective-permute-start(f32[2,128,256]{2,1,0:T(8,128)S(1)} %copy-done.2), channel_id=1, source_target_pairs={{0,4},{2,6},{4,0},{6,2},{1,5},{3,7},{5,1},{7,3},{8,12},{10,14},{12... | collective-permute-start | bytes 786440 | tf_op jit(solution)/shard_map/ppermute | solution.py:65
  70.7 23.2 %collective-permute-start.8 = (f32[2,128,256]{2,1,0:T(8,128)S(1)}, f32[2,128,256]{2,1,0:T(8,128)S(1)}, u32[]{:S(2)}, u32[]{:S(2)}) collective-permute-start(f32[2,128,256]{2,1,0:T(8,128)S(1)} %copy-done.2), channel_id=1, source_target_pairs={{0,2},{2,4},{4,6},{6,0},{1,3},{3,5},{5,7},{7,1},{8,10},{10,12},{12... | collective-permute-start | bytes 786440 | tf_op jit(solution)/shard_map/ppermute | solution.py:65
  73.5 21.5 %collective-permute-start.10 = (f32[2,128,256]{2,1,0:T(8,128)S(1)}, f32[2,128,256]{2,1,0:T(8,128)S(1)}, u32[]{:S(2)}, u32[]{:S(2)}) collective-permute-start(f32[2,128,256]{2,1,0:T(8,128)S(1)} %fusion.9), channel_id=1, source_target_pairs={{0,24},{8,0},{16,8},{24,16},{1,25},{9,1},{17,9},{25,17},{2,26},{10... | collective-permute-start | bytes 786440 | tf_op jit(solution)/shard_map/ppermute | solution.py:65
  73.5 21.5 %collective-permute-start.11 = (f32[2,128,256]{2,1,0:T(8,128)S(1)}, f32[2,128,256]{2,1,0:T(8,128)S(1)}, u32[]{:S(2)}, u32[]{:S(2)}) collective-permute-start(f32[2,128,256]{2,1,0:T(8,128)S(1)} %fusion.9), channel_id=1, source_target_pairs={{0,16},{8,24},{16,0},{24,8},{1,17},{9,25},{17,1},{25,9},{2,18},{10... | collective-permute-start | bytes 786440 | tf_op jit(solution)/shard_map/ppermute | solution.py:65
  77.4 17.6 %collective-permute-start.12 = (f32[2,128,256]{2,1,0:T(8,128)S(1)}, f32[2,128,256]{2,1,0:T(8,128)S(1)}, u32[]{:S(2)}, u32[]{:S(2)}) collective-permute-start(f32[2,128,256]{2,1,0:T(8,128)S(1)} %fusion.9), channel_id=1, source_target_pairs={{0,8},{8,16},{16,24},{24,0},{1,9},{9,17},{17,25},{25,1},{2,10},{10... | collective-permute-start | bytes 786440 | tf_op jit(solution)/shard_map/ppermute | solution.py:65
  94.1 3.2 %collective-permute-start.9 = (f32[2,512,256]{2,1,0:T(8,128)S(1)}, f32[2,512,256]{2,1,0:T(8,128)S(1)}, u32[]{:S(2)}, u32[]{:S(2)}) collective-permute-start(f32[2,512,256]{2,1,0:T(8,128)S(1)} %pad_maximum_fusion.1), channel_id=1, source_target_pairs={{0,1},{1,0},{2,3},{3,2},{4,5},{5,4},{6,7},{7,6},{8,9},{9,8},{10,11... | collective-permute-start | bytes 3145736 | tf_op jit(solution)/shard_map/ppermute | solution.py:92
  97.5 2.2 %copy-start.1 = (f32[2,1024,512]{2,1,0:T(8,128)S(1)}, f32[2,1024,512]{2,1,0:T(8,128)}, u32[]{:S(2)}) copy-start(f32[2,1024,512]{2,1,0:T(8,128)} %param.3) | copy-start | bytes 12582916

commit v16 on v5

--- a/solution.py
+++ b/solution.py
@@ -44,7 +44,7 @@
                     pairs.append((lin(0, 0, g, l, c), lin(y1, h1, p % nx, g, p // nx)))
         return pairs
 
-    first = [(0, 0), (1, 0), (ny - 1, 0)]
+    first = [(ny - 1, 0), (1, 0), (0, 0)]
     relays = [
         [[((1, 0), (2, 0)), ((ny - 1, 0), (ny - 1, 1))], [((1, 0), (1, 1))]],
         [[((1, 1), (2, 1)), ((ny - 1, 1), (0, 1))]],
@@ -76,8 +76,8 @@
         ci = lax.axis_index("core")
 
         got_a = [lax.ppermute(panel, AXES, spread(y1, h1)) for y1, h1 in first]
-        held_a = got_a[0]
-        for (y1, h1), got in zip(first[1:], got_a[1:]):
+        held_a = got_a[-1]
+        for (y1, h1), got in zip(first[:-1], got_a[:-1]):
             held_a = jnp.where((yi == y1) & (hi == h1), got, held_a)
         held = held_a
         for stage in relays:

time: 102 us -> 100 us (0.980)
  no operation moved by 1% of the time
where the time goes in v16:
time: 100 us
  starting transfers between devices  58.5 us (58%)
  waiting for transfers between devices  29 us (29%)
  matrix products  7.7 us (8%)
  local copies, waits for them, and re-layouts  1.98 us (2%)
  other arithmetic  1.82 us (2%)
  between operations  1.12 us (1%)
    ppermute x6, starting transfers between devices, gather(): lax.ppermute(piece, axis, shifts(n, k))  42.9 us
    ppermute x6, waiting for transfers between devices, gather(): lax.ppermute(piece, axis, shifts(n, k))  15.4 us
    ppermute x3, waiting for transfers between devices, local(): got_a = [lax.ppermute(panel, AXES, spread(y1, h1)) for y1, h1 in first]  13.3 us
    ppermute x3, starting transfers between devices, local(): got_a = [lax.ppermute(panel, AXES, spread(y1, h1)) for y1, h1 in first]  12.9 us
    dot_general x1, matrix products, local(): product = lax.dot_general(lhs, rhs, dims, precision=lax.Precision.HIGH)  5.06 us
    ppermute x3, starting transfers between devices, local(): lax.ppermute(sent, ('y', 'zh'), [(plane(h0, y0), plane(h1, y1)) for (y0,...  2.03 us
  transfers between devices with their start and end apart: 13, of which 5 were waited for; matrix products, arithmetic and copies ran while one was open for 4% of the time, Pallas kernels for 0%

profile of v16, /device:TPU:7, one launch (start us, length us, event | category | flops | bytes accessed | tf_op | source)
XLA Modules:
  0.0 100.1 jit_solution(464474303619036961)
XLA Ops:
  0.6 0.0 copy-start.2
  0.6 0.0 copy-start
  0.6 8.8 %collective-permute-start = (f32[2,128,256]{2,1,0:T(8,128)}, f32[2,128,256]{2,1,0:T(8,128)S(1)}, u32[]{:S(2)}, u32[]{:S(2)}) collective-permute-start(f32[2,128,256]{2,1,0:T(8,128)} %param.4), channel_id=1, source_target_pairs={{0,64},{1,72},{2,80},{3,88},{4,65},{5,73},{6,81},{7,89},{8,66},{9,... | collective-permute-start | bytes 786440 | tf_op jit(solution)/shard_map/ppermute | solution.py:78
  9.5 2.1 %collective-permute-start.1 = (f32[2,128,256]{2,1,0:T(8,128)}, f32[2,128,256]{2,1,0:T(8,128)S(1)}, u32[]{:S(2)}, u32[]{:S(2)}) collective-permute-start(f32[2,128,256]{2,1,0:T(8,128)} %param.4), channel_id=1, source_target_pairs={{0,192},{1,200},{2,208},{3,216},{4,193},{5,201},{6,209},{7,217},{8... | collective-permute-start | bytes 786440 | tf_op jit(solution)/shard_map/ppermute | solution.py:78
  11.6 1.9 %collective-permute-start.2 = (f32[2,128,256]{2,1,0:T(8,128)}, f32[2,128,256]{2,1,0:T(8,128)S(1)}, u32[]{:S(2)}, u32[]{:S(2)}) collective-permute-start(f32[2,128,256]{2,1,0:T(8,128)} %param.4), channel_id=1, source_target_pairs={{0,0},{1,8},{2,16},{3,24},{4,1},{5,9},{6,17},{7,25},{8,2},{9,10},{... | collective-permute-start | bytes 786440 | tf_op jit(solution)/shard_map/ppermute | solution.py:78
  13.5 2.4 %collective-permute-done = f32[2,128,256]{2,1,0:T(8,128)S(1)} collective-permute-done((f32[2,128,256]{2,1,0:T(8,128)}, f32[2,128,256]{2,1,0:T(8,128)S(1)}, u32[]{:S(2)}, u32[]{:S(2)}) %collective-permute-start) | collective-permute-done | bytes 262176 | tf_op jit(solution)/shard_map/ppermute | solution.py:78
  15.9 5.6 %collective-permute-done.1 = f32[2,128,256]{2,1,0:T(8,128)S(1)} collective-permute-done((f32[2,128,256]{2,1,0:T(8,128)}, f32[2,128,256]{2,1,0:T(8,128)S(1)}, u32[]{:S(2)}, u32[]{:S(2)}) %collective-permute-start.1) | collective-permute-done | bytes 262176 | tf_op jit(solution)/shard_map/ppermute | solution.py:78
  21.5 5.3 %collective-permute-done.2 = f32[2,128,256]{2,1,0:T(8,128)S(1)} collective-permute-done((f32[2,128,256]{2,1,0:T(8,128)}, f32[2,128,256]{2,1,0:T(8,128)S(1)}, u32[]{:S(2)}, u32[]{:S(2)}) %collective-permute-start.2) | collective-permute-done | bytes 262176 | tf_op jit(solution)/shard_map/ppermute | solution.py:78
  26.9 0.7 collective-permute-start.3
  27.5 0.7 collective-permute-start.4
  28.2 0.0 collective-permute-done.3
  28.3 0.0 collective-permute-done.4
  28.3 0.1 fusion.9
  28.3 0.7 collective-permute-start.5
  29.0 0.0 copy-done.2
  29.0 0.0 copy-done
  29.0 0.3 fusion.12
  29.3 0.3 fusion.18
  29.6 0.0 collective-permute-done.5
  29.7 0.1 collective-permute-start.6
  29.8 36.3 %collective-permute-start.7 = (f32[2,128,256]{2,1,0:T(8,128)S(1)}, f32[2,128,256]{2,1,0:T(8,128)S(1)}, u32[]{:S(2)}, u32[]{:S(2)}) collective-permute-start(f32[2,128,256]{2,1,0:T(8,128)S(1)} %copy-done.2), channel_id=1, source_target_pairs={{0,4},{2,6},{4,0},{6,2},{1,5},{3,7},{5,1},{7,3},{8,12},{10,14},{12... | collective-permute-start | bytes 786440 | tf_op jit(solution)/shard_map/ppermute | solution.py:66
  66.1 1.4 %collective-permute-start.8 = (f32[2,128,256]{2,1,0:T(8,128)S(1)}, f32[2,128,256]{2,1,0:T(8,128)S(1)}, u32[]{:S(2)}, u32[]{:S(2)}) collective-permute-start(f32[2,128,256]{2,1,0:T(8,128)S(1)} %copy-done.2), channel_id=1, source_target_pairs={{0,2},{2,4},{4,6},{6,0},{1,3},{3,5},{5,7},{7,1},{8,10},{10,12},{12... | collective-permute-start | bytes 786440 | tf_op jit(solution)/shard_map/ppermute | solution.py:66
  67.4 0.3 fusion.5
  67.9 0.3 fusion.6
  68.2 0.7 pad_maximum_fusion.3
  68.9 0.0 collective-permute-start.10
  68.9 3.6 %collective-permute-start.11 = (f32[2,128,256]{2,1,0:T(8,128)S(1)}, f32[2,128,256]{2,1,0:T(8,128)S(1)}, u32[]{:S(2)}, u32[]{:S(2)}) collective-permute-start(f32[2,128,256]{2,1,0:T(8,128)S(1)} %select_select_fusion), channel_id=1, source_target_pairs={{0,16},{8,24},{16,0},{24,8},{1,17},{9,25},{17,1},{25,9},{2,18},{10... | collective-permute-start | bytes 786440 | tf_op jit(solution)/shard_map/ppermute | solution.py:66
  72.5 0.0 collective-permute-done.6
  72.5 1.5 %collective-permute-start.12 = (f32[2,128,256]{2,1,0:T(8,128)S(1)}, f32[2,128,256]{2,1,0:T(8,128)S(1)}, u32[]{:S(2)}, u32[]{:S(2)}) collective-permute-start(f32[2,128,256]{2,1,0:T(8,128)S(1)} %select_select_fusion), channel_id=1, source_target_pairs={{0,8},{8,16},{16,24},{24,0},{1,9},{9,17},{17,25},{25,1},{2,10},{10... | collective-permute-start | bytes 786440 | tf_op jit(solution)/shard_map/ppermute | solution.py:66
  74.1 15.4 %collective-permute-done.7 = f32[2,128,256]{2,1,0:T(8,128)S(1)} collective-permute-done((f32[2,128,256]{2,1,0:T(8,128)S(1)}, f32[2,128,256]{2,1,0:T(8,128)S(1)}, u32[]{:S(2)}, u32[]{:S(2)}) %collective-permute-start.7) | collective-permute-done | bytes 262176 | tf_op jit(solution)/shard_map/ppermute | solution.py:66
  89.5 0.0 collective-permute-done.8
  89.5 0.1 select_select_fusion.9
  89.6 0.1 pad_maximum_fusion.1
  89.7 0.7 collective-permute-start.9
  90.4 0.0 collective-permute-done.10
  90.4 0.0 collective-permute-done.11
  90.4 0.0 collective-permute-done.12
  90.4 0.1 select_select_fusion.5
  90.5 0.1 pad_maximum_fusion.2
  90.6 0.4 fusion.8
  91.0 0.4 fusion.4
  91.4 0.4 fusion.7
  91.8 0.4 convolution_add_fusion
  92.2 0.2 maximum_bitcast_fusion
  92.4 0.3 collective-permute-done.9
  92.7 0.2 broadcast_select_fusion.1
  92.8 0.0 copy-start.1
  92.8 0.2 pad_maximum_fusion
  93.1 2.0 %copy-done.1 = f32[2,1024,512]{2,1,0:T(8,128)S(1)} copy-done((f32[2,1024,512]{2,1,0:T(8,128)S(1)}, f32[2,1024,512]{2,1,0:T(8,128)}, u32[]{:S(2)}) %copy-start.1) | copy-done | bytes 4194328
  95.0 5.1 %bitcast_subtract_fusion = f32[2,1024,512]{2,1,0:T(8,128)} fusion(f32[2,1024,512]{2,1,0:T(8,128)S(1)} %copy-done.1, f32[1,2,512,256]{3,2,1,0:T(8,128)S(1)} %get-tuple-element.17, f32[1,2,512,256]{3,2,1,0:T(8,128)S(1)} %get-tuple-element.16, f32[2,1024,256]{2,1,0:T(8,128)S(1)} %bitcast.55), kind=kOutput, calls=%fused_computation | convolution fusion | flops 3222798336 | bytes 12582912 | tf_op jit(solution)/shard_map/dot_general | solution.py:105
  (3 shorter events, 0.1 us)
Async XLA Ops:
  0.6 28.4 %copy-start.2 = (f32[2,128,256]{2,1,0:T(8,128)S(1)}, f32[2,128,256]{2,1,0:T(8,128)}, u32[]{:S(2)}) copy-start(f32[2,128,256]{2,1,0:T(8,128)} %param.4) | copy-start | bytes 786436
  0.6 28.4 %copy-start = (f32[2,256,256]{2,1,0:T(8,128)S(1)}, f32[2,256,256]{2,1,0:T(8,128)}, u32[]{:S(2)}) copy-start(f32[2,256,256]{2,1,0:T(8,128)} %param.5) | copy-start | bytes 1572868
  0.6 15.3 %collective-permute-start = (f32[2,128,256]{2,1,0:T(8,128)}, f32[2,128,256]{2,1,0:T(8,128)S(1)}, u32[]{:S(2)}, u32[]{:S(2)}) collective-permute-start(f32[2,128,256]{2,1,0:T(8,128)} %param.4), channel_id=1, source_target_pairs={{0,64},{1,72},{2,80},{3,88},{4,65},{5,73},{6,81},{7,89},{8,66},{9,... | collective-permute-start | bytes 786440 | tf_op jit(solution)/shard_map/ppermute | solution.py:78
  9.5 12.1 %collective-permute-start.1 = (f32[2,128,256]{2,1,0:T(8,128)}, f32[2,128,256]{2,1,0:T(8,128)S(1)}, u32[]{:S(2)}, u32[]{:S(2)}) collective-permute-start(f32[2,128,256]{2,1,0:T(8,128)} %param.4), channel_id=1, source_target_pairs={{0,192},{1,200},{2,208},{3,216},{4,193},{5,201},{6,209},{7,217},{8... | collective-permute-start | bytes 786440 | tf_op jit(solution)/shard_map/ppermute | solution.py:78
  11.6 15.2 %collective-permute-start.2 = (f32[2,128,256]{2,1,0:T(8,128)}, f32[2,128,256]{2,1,0:T(8,128)S(1)}, u32[]{:S(2)}, u32[]{:S(2)}) collective-permute-start(f32[2,128,256]{2,1,0:T(8,128)} %param.4), channel_id=1, source_target_pairs={{0,0},{1,8},{2,16},{3,24},{4,1},{5,9},{6,17},{7,25},{8,2},{9,10},{... | collective-permute-start | bytes 786440 | tf_op jit(solution)/shard_map/ppermute | solution.py:78
  26.9 1.4 %collective-permute-start.3 = (f32[2,128,256]{2,1,0:T(8,128)S(1)}, f32[2,128,256]{2,1,0:T(8,128)S(1)}, u32[]{:S(2)}, u32[]{:S(2)}) collective-permute-start(f32[2,128,256]{2,1,0:T(8,128)S(1)} %select_select_fusion.10), channel_id=1, source_target_pairs={{64,96},{65,97},{66,98},{67,99},{68,100},{69,101},{70,102},{71,103... | collective-permute-start | bytes 786440 | tf_op jit(solution)/shard_map/ppermute | solution.py:86
  27.5 0.7 collective-permute-start.4
  28.3 1.3 %collective-permute-start.5 = (f32[2,128,256]{2,1,0:T(8,128)S(1)}, f32[2,128,256]{2,1,0:T(8,128)S(1)}, u32[]{:S(2)}, u32[]{:S(2)}) collective-permute-start(f32[2,128,256]{2,1,0:T(8,128)S(1)} %fusion.9), channel_id=1, source_target_pairs={{96,160},{224,32},{97,161},{225,33},{98,162},{226,34},{99,163},{22... | collective-permute-start | bytes 786440 | tf_op jit(solution)/shard_map/ppermute | solution.py:86
  29.7 42.9 %collective-permute-start.6 = (f32[2,128,256]{2,1,0:T(8,128)S(1)}, f32[2,128,256]{2,1,0:T(8,128)S(1)}, u32[]{:S(2)}, u32[]{:S(2)}) collective-permute-start(f32[2,128,256]{2,1,0:T(8,128)S(1)} %copy-done.2), channel_id=1, source_target_pairs={{0,6},{2,0},{4,2},{6,4},{1,7},{3,1},{5,3},{7,5},{8,14},{10,8},{12,... | collective-permute-start | bytes 786440 | tf_op jit(solution)/shard_map/ppermute | solution.py:66
  29.8 59.7 %collective-permute-start.7 = (f32[2,128,256]{2,1,0:T(8,128)S(1)}, f32[2,128,256]{2,1,0:T(8,128)S(1)}, u32[]{:S(2)}, u32[]{:S(2)}) collective-permute-start(f32[2,128,256]{2,1,0:T(8,128)S(1)} %copy-done.2), channel_id=1, source_target_pairs={{0,4},{2,6},{4,0},{6,2},{1,5},{3,7},{5,1},{7,3},{8,12},{10,14},{12... | collective-permute-start | bytes 786440 | tf_op jit(solution)/shard_map/ppermute | solution.py:66
  66.1 23.4 %collective-permute-start.8 = (f32[2,128,256]{2,1,0:T(8,128)S(1)}, f32[2,128,256]{2,1,0:T(8,128)S(1)}, u32[]{:S(2)}, u32[]{:S(2)}) collective-permute-start(f32[2,128,256]{2,1,0:T(8,128)S(1)} %copy-done.2), channel_id=1, source_target_pairs={{0,2},{2,4},{4,6},{6,0},{1,3},{3,5},{5,7},{7,1},{8,10},{10,12},{12... | collective-permute-start | bytes 786440 | tf_op jit(solution)/shard_map/ppermute | solution.py:66
  68.9 21.5 %collective-permute-start.10 = (f32[2,128,256]{2,1,0:T(8,128)S(1)}, f32[2,128,256]{2,1,0:T(8,128)S(1)}, u32[]{:S(2)}, u32[]{:S(2)}) collective-permute-start(f32[2,128,256]{2,1,0:T(8,128)S(1)} %select_select_fusion), channel_id=1, source_target_pairs={{0,24},{8,0},{16,8},{24,16},{1,25},{9,1},{17,9},{25,17},{2,26},{10... | collective-permute-start | bytes 786440 | tf_op jit(solution)/shard_map/ppermute | solution.py:66
  68.9 21.5 %collective-permute-start.11 = (f32[2,128,256]{2,1,0:T(8,128)S(1)}, f32[2,128,256]{2,1,0:T(8,128)S(1)}, u32[]{:S(2)}, u32[]{:S(2)}) collective-permute-start(f32[2,128,256]{2,1,0:T(8,128)S(1)} %select_select_fusion), channel_id=1, source_target_pairs={{0,16},{8,24},{16,0},{24,8},{1,17},{9,25},{17,1},{25,9},{2,18},{10... | collective-permute-start | bytes 786440 | tf_op jit(solution)/shard_map/ppermute | solution.py:66
  72.5 17.8 %collective-permute-start.12 = (f32[2,128,256]{2,1,0:T(8,128)S(1)}, f32[2,128,256]{2,1,0:T(8,128)S(1)}, u32[]{:S(2)}, u32[]{:S(2)}) collective-permute-start(f32[2,128,256]{2,1,0:T(8,128)S(1)} %select_select_fusion), channel_id=1, source_target_pairs={{0,8},{8,16},{16,24},{24,0},{1,9},{9,17},{17,25},{25,1},{2,10},{10... | collective-permute-start | bytes 786440 | tf_op jit(solution)/shard_map/ppermute | solution.py:66
  89.7 3.0 %collective-permute-start.9 = (f32[2,512,256]{2,1,0:T(8,128)S(1)}, f32[2,512,256]{2,1,0:T(8,128)S(1)}, u32[]{:S(2)}, u32[]{:S(2)}) collective-permute-start(f32[2,512,256]{2,1,0:T(8,128)S(1)} %pad_maximum_fusion.1), channel_id=1, source_target_pairs={{0,1},{1,0},{2,3},{3,2},{4,5},{5,4},{6,7},{7,6},{8,9},{9,8},{10,11... | collective-permute-start | bytes 3145736 | tf_op jit(solution)/shard_map/ppermute | solution.py:93
  92.8 2.2 %copy-start.1 = (f32[2,1024,512]{2,1,0:T(8,128)S(1)}, f32[2,1024,512]{2,1,0:T(8,128)}, u32[]{:S(2)}) copy-start(f32[2,1024,512]{2,1,0:T(8,128)} %param.3) | copy-start | bytes 12582916
